TPU v7x, 768 devices: a whole 4x8x12 slice. The times are simulated.
768 devices in a mesh: gx: 24 (over x, z_hi, core), gy: 32 (over z_lo, y).
Axes of the slice: x: 4, y: 8, z: 12 (z_hi: 3, z_lo: 4; z = z_hi * 4 + z_lo), core: 2. Of those that a mesh axis runs over, the one named last changes fastest.
Arguments:
- state: float32 [10, 192, 256, 128], P(None, 'gx', 'gy'), may hold values from 0.01 to 3, as said below
- source_in: float32 [10, 192, 256, 128], P(None, 'gx', 'gy'), may hold values from -3 to 3
- counts: int32 [192, 256], P('gx', 'gy'), may hold values from 1 to 8, as said below
- diffusivity: float32 [10], replicated, may hold values from 0.3 to 1
- log_rate: float32 [21], replicated, may hold values from 0.3 to 1
- activation: float32 [21], replicated, may hold values from 0.4 to 0.8
- heat_release: float32 [21], replicated, may hold values from -1 to 2
Outputs:
- next_state: float32 [10, 192, 256, 128], P(None, 'gx', 'gy')
- late_source: float32 [10, 192, 256, 128], P(None, 'gx', 'gy')
Inputs may be any that keep to these rules, and one draw needn't show every extreme that they name: Boxes of 8 x 8 blocks are either flame boxes, about an eighth of them, where every count is 5 or more and one is 8, or others, where counts are 1 or 2. `state`: rows 0 to 8 lie in [0.01, 1]; the last row lies in [1, 3].
All inputs are finite; a program needn't handle non-finite values.
Results may differ from a plain program's by a relative error of at most 0.0003.
Values sent between devices are 32-bit elements; how exact they have to be, the bound alone decides.
No kernel may reach another device: no remote copies, remote signals or barrier semaphores. Data moves between devices by JAX's collectives and lax.ppermute only.
A program may use at most 32 MiB of HBM per device.

v0:
```python
import jax
import jax.numpy as jnp
import numpy as np
from jax import lax
from jax.sharding import PartitionSpec as P

time_step = 0.15
reaction_table = (
    (3, 1, (4, 5)),
    (4, 0, (3, 5)),
    (5, 0, (3, 2)),
    (5, 5, (4, 2)),
    (3, 3, (0,)),
    (3, 5, (2,)),
    (4, 4, (1,)),
    (3, 4, (5,)),
    (3, 1, (6,)),
    (6, 3, (0, 1)),
    (6, 3, (5, 5)),
    (6, 4, (1, 5)),
    (6, 5, (2, 1)),
    (6, 6, (7, 1)),
    (7, 9, (5, 5)),
    (7, 3, (2, 5)),
    (7, 3, (6, 0)),
    (7, 4, (5, 6)),
    (7, 5, (6, 2)),
    (0, 9, (3, 3)),
    (2, 9, (3, 5)),
)


def with_halo(x, sides, width):
    for axis, dim in sides:
        size, length = (lax.axis_size(axis), x.shape[dim])
        up = [(i, (i + 1) % size) for i in range(size)]
        down = [(j, i) for i, j in up]
        last = lax.slice_in_dim(x, length - width, length, axis=dim)
        initial = lax.slice_in_dim(x, 0, width, axis=dim)
        before = lax.ppermute(last, axis, up)
        after = lax.ppermute(initial, axis, down)
        x = jnp.concatenate([before, x, after], axis=dim)
    return x


def tables(heat_release):
    leading = np.zeros((21, 10), np.float32)
    trailing = np.zeros((21, 10), np.float32)
    change = np.zeros((9, 21), np.float32)
    for reaction, entry in enumerate(reaction_table):
        leading[reaction, entry[0]] = 1.0
        trailing[reaction, entry[1]] = 1.0
        change[entry[0], reaction] -= 1.0
        if entry[1] < 9:
            change[entry[1], reaction] -= 1.0
        for product in entry[2]:
            change[product, reaction] += 1.0
    matrix = jnp.concatenate([jnp.asarray(change).astype(jnp.float32), heat_release[None, :]], 0)
    return (
        jnp.asarray(leading).astype(jnp.float32),
        jnp.asarray(trailing).astype(jnp.float32),
        matrix,
    )


def advance(current, coeffs, stride, active, leading, trailing, matrix):
    augmented = jnp.concatenate([current[:9], jnp.ones_like(current[:1])], 0)
    reactant_one = jnp.dot(leading, augmented, precision=lax.Precision.HIGHEST)
    reactant_two = jnp.dot(trailing, augmented, precision=lax.Precision.HIGHEST)
    rate_terms = coeffs * reactant_one * reactant_two
    change_now = jnp.dot(matrix, rate_terms, precision=lax.Precision.HIGHEST)
    return jnp.where(active[None, :], current + stride[None, :] * change_now, current)


def react(blocks, block_counts, log_rate, activation, heat_release):
    field_count = blocks.shape[0]
    block_total = blocks.shape[1]
    length_z = blocks.shape[2]
    members = 32
    groups = block_total // members
    ranking = jnp.argsort(-block_counts, stable=True)
    sorted_counts = jnp.take(block_counts, ranking)
    gathered = jnp.take(blocks, ranking, axis=1).reshape(field_count, groups, members, length_z)
    gathered = jnp.moveaxis(gathered, 1, 0)
    grouped_counts = sorted_counts.reshape(groups, members)
    leading, trailing, matrix = tables(heat_release)

    def integrate_group(carry, group):
        block_fields, counts_group = group
        cell_rows = block_fields.reshape(field_count, members * length_z)
        counts_cells = jnp.repeat(counts_group, length_z)
        coeffs = jnp.exp(log_rate[:, None] - activation[:, None] / cell_rows[9][None, :])
        stride = time_step / counts_cells.astype(jnp.float32)

        def substep(turn_index, current):
            return advance(
                current, coeffs, stride, turn_index < counts_cells, leading, trailing, matrix
            )

        finished = lax.fori_loop(0, jnp.max(counts_group), substep, cell_rows)
        return (carry, ((finished - cell_rows) / time_step).reshape(field_count, members, length_z))

    unused, results = lax.scan(integrate_group, jnp.int32(0), (gathered, grouped_counts))
    results = jnp.moveaxis(results, 0, 1).reshape(field_count, block_total, length_z)
    inverse = jnp.argsort(ranking)
    return jnp.take(results, inverse, axis=1)


def chemistry(fields_in, counts, log_rate, activation, heat_release):
    field_count = fields_in.shape[0]
    length_z = fields_in.shape[3]
    block_total = fields_in.shape[1] * fields_in.shape[2]
    blocks = fields_in.reshape(field_count, block_total, length_z)
    block_counts = counts.reshape(block_total)
    helpers = lax.axis_size("gy")
    rounds = block_total // helpers
    count_rows = jnp.broadcast_to(
        block_counts.astype(jnp.float32)[None, :, None], (1, block_total, length_z)
    )
    tagged = jnp.concatenate([blocks, count_rows], 0).reshape(
        field_count + 1, rounds, helpers, length_z
    )
    arrived = lax.all_to_all(tagged, "gy", split_axis=2, concat_axis=2, tiled=True)
    arrived = arrived.reshape(field_count + 1, block_total, length_z)
    own_counts = arrived[field_count, :, 0].astype(jnp.int32)
    produced = react(arrived[:field_count], own_counts, log_rate, activation, heat_release)
    returned = lax.all_to_all(
        produced.reshape(field_count, rounds, helpers, length_z),
        "gy",
        split_axis=2,
        concat_axis=2,
        tiled=True,
    )
    sources = returned.reshape(field_count, block_total, length_z)
    return sources.reshape(fields_in.shape)


def laplace_local(field):
    padded = with_halo(field, (("gx", 1), ("gy", 2)), 1)
    beside = padded[:, 2:, 1:-1] + padded[:, :-2, 1:-1]
    beside = beside + padded[:, 1:-1, 2:] + padded[:, 1:-1, :-2]
    beside = beside + jnp.roll(field, 1, 3) + jnp.roll(field, -1, 3)
    return beside - 6.0 * field


def local(state, source_in, counts, diffusivity, log_rate, activation, heat_release):
    spread = diffusivity[:, None, None, None]
    first_section = state + time_step * (spread * laplace_local(state) + source_in)
    early = chemistry(state, counts, log_rate, activation, heat_release)
    next_state = 0.5 * state + 0.5 * (
        first_section + time_step * (spread * laplace_local(first_section) + early)
    )
    late_source = chemistry(first_section, counts, log_rate, activation, heat_release)
    return (next_state, late_source)


def solution(mesh):
    in_specs = (
        P(None, "gx", "gy", None),
        P(None, "gx", "gy", None),
        P("gx", "gy"),
        P(),
        P(),
        P(),
        P(),
    )
    out_specs = (P(None, "gx", "gy", None), P(None, "gx", "gy", None))
    return jax.shard_map(local, mesh=mesh, in_specs=in_specs, out_specs=out_specs, check_vma=False)
```

profile of v0, /device:TPU:6, one launch (start us, length us, event | category | flops | bytes accessed | tf_op | source)
XLA Modules:
  0.0 191.1 jit_solution(363837384226115191)
XLA Ops:
  0.6 0.8 fusion.74
  1.4 1.9 collective-permute-start.1
  3.4 14.4 %collective-permute-start = (f32[10,1,8,128]{3,2,1,0:T(8,128)S(1)}, f32[10,1,8,128]{3,2,1,0:T(8,128)S(1)}, u32[]{:S(2)}, u32[]{:S(2)}) collective-permute-start(f32[10,1,8,128]{3,2,1,0:T(8,128)S(1)} %get-tuple-element.554), channel_id=1, source_target_pairs={{32,0},{64,32},{96,64},{128,96},{160,128},{192,160},{224,192},{256... | collective-permute-start | bytes 122888 | tf_op jit(solution)/shard_map/ppermute | solution.py:41
  17.8 1.2 fusion.72
  19.5 8.1 %collective-permute-start.2 = (f32[10,10,1,128]{3,2,1,0:T(1,128)S(1)}, f32[10,10,1,128]{3,2,1,0:T(1,128)S(1)}, u32[]{:S(2)}, u32[]{:S(2)}) collective-permute-start(f32[10,10,1,128]{3,2,1,0:T(1,128)S(1)} %get-tuple-element.542), channel_id=1, source_target_pairs={{1,0},{2,1},{3,2},{4,3},{5,4},{6,5},{7,6},{8,7},{9,8},{10,9},{11,1... | collective-permute-start | bytes 153608 | tf_op jit(solution)/shard_map/ppermute | solution.py:41
  27.6 2.1 %collective-permute-start.3 = (f32[10,10,1,128]{3,2,1,0:T(1,128)S(1)}, f32[10,10,1,128]{3,2,1,0:T(1,128)S(1)}, u32[]{:S(2)}, u32[]{:S(2)}) collective-permute-start(f32[10,10,1,128]{3,2,1,0:T(1,128)S(1)} %get-tuple-element.543), channel_id=1, source_target_pairs={{0,1},{1,2},{2,3},{3,4},{4,5},{5,6},{6,7},{7,8},{8,9},{9,10},{10,1... | collective-permute-start | bytes 153608 | tf_op jit(solution)/shard_map/ppermute | solution.py:40
  30.0 7.7 %collective-permute-done.3 = f32[10,10,1,128]{3,2,1,0:T(1,128)S(1)} collective-permute-done((f32[10,10,1,128]{3,2,1,0:T(1,128)S(1)}, f32[10,10,1,128]{3,2,1,0:T(1,128)S(1)}, u32[]{:S(2)}, u32[]{:S(2)}) %collective-permute-start.3) | collective-permute-done | bytes 51232 | tf_op jit(solution)/shard_map/ppermute | solution.py:40
  37.7 0.7 copy-done.6
  38.8 1.0 copy.65
  39.9 4.0 %all-to-all-start.2 = ((f32[11,2,32,128]{3,1,0,2:T(2,128)}), f32[11,2,32,128]{3,1,0,2:T(2,128)S(1)}, u32[]{:S(2)}, u32[]{:S(2)}) async-start(f32[11,2,32,128]{3,1,0,2:T(2,128)} %copy.65), calls=%async_computation.2 | async-start | bytes 720896 | tf_op jit(solution)/shard_map/all_to_all | solution.py:123
  43.9 0.6 copy-done.7
  44.6 1.0 copy.56
  45.6 10.9 %all-to-all-done.2 = f32[11,2,32,128]{3,1,0,2:T(2,128)S(1)} async-done(((f32[11,2,32,128]{3,1,0,2:T(2,128)}), f32[11,2,32,128]{3,1,0,2:T(2,128)S(1)}, u32[]{:S(2)}, u32[]{:S(2)}) %all-to-all-start.2) | async-done | bytes 360480 | tf_op jit(solution)/shard_map/all_to_all | solution.py:123
  56.5 7.3 %all-to-all-start = ((f32[11,2,32,128]{3,1,0,2:T(2,128)}), f32[11,2,32,128]{3,1,0,2:T(2,128)S(1)}, u32[]{:S(2)}, u32[]{:S(2)}) async-start(f32[11,2,32,128]{3,1,0,2:T(2,128)} %copy.56), calls=%async_computation | async-start | bytes 720896 | tf_op jit(solution)/shard_map/all_to_all | solution.py:123
  64.0 2.0 %sort.64 = (s32[64]{0:T(128)}, s32[64]{0:T(128)S(1)}) sort(s32[64]{0:T(128)S(1)} %neg.7, s32[64]{0:T(128)S(1)} %iota.16), dimensions={0}, to_apply=%region_7.10 | sort | flops 384 | bytes 1024 | tf_op jit(solution)/shard_map/jit(argsort)/sort | solution.py:81
  66.0 2.0 %sort.65 = (s32[64]{0:T(128)}, s32[64]{0:T(128)S(1)}) sort(s32[64]{0:T(128)S(1)} %get-tuple-element.201, s32[64]{0:T(128)S(1)} %iota.17), dimensions={0}, to_apply=%region_13.16 | sort | flops 384 | bytes 1024 | tf_op jit(solution)/shard_map/jit(argsort)/sort | solution.py:105
  68.1 0.8 gather_fusion.4
  68.9 0.6 gather_fusion.3
  70.0 0.7 copy-done
  70.7 27.3 %while.55 = (s32[]{:T(128)}, f32[2,10,32,128]{3,2,0,1:T(8,128)S(1)}, f32[2,10,32,128]{3,2,1,0:T(8,128)S(1)}, s32[2,32]{1,0:T(2,128)S(1)}, f32[21]{0:T(128)S(1)},...) while((s32[]{:T(128)}, ...), condition=%wide.region_12.15_spmd.clone, body=%wide.region_8.14_spmd.sunk.clone.sunk | while | flops 31608864 | bytes 5074514 | solution.py:103
  70.9 0.7 fusion.105
  71.6 19.8 %while.57 = (s32[]{:T(128)}, f32[10,4096]{1,0:T(8,128)S(1)}, s32[]{:T(128)}, f32[10,21]{1,0:T(8,128)S(1)}, s32[32]{0:T(128)S(1)}, /*index=5*/f32[4096]{0:T(1024)...) while((s32[]{:T(128)}, f32[10,4096]{1,0:T(8,128)S(1)}, ...), condition=%wide.region_11.13_spmd.clone.clone.clone, body=%wide.region_10.12_spmd.sunk.clone.clone.clone.sunk | while | flops 31526912 | bytes 2092045 | solution.py:100
  72.2 0.5 convolution_multiply_fusion.10
  74.6 0.5 convolution_multiply_fusion.10
  77.0 0.5 convolution_multiply_fusion.10
  79.4 0.5 convolution_multiply_fusion.10
  81.8 0.5 convolution_multiply_fusion.10
  86.6 0.5 convolution_multiply_fusion.10
  89.0 0.5 convolution_multiply_fusion.10
  91.8 0.7 fusion.105
  92.4 5.4 %while.57 = (s32[]{:T(128)}, f32[10,4096]{1,0:T(8,128)S(1)}, s32[]{:T(128)}, f32[10,21]{1,0:T(8,128)S(1)}, s32[32]{0:T(128)S(1)}, /*index=5*/f32[4096]{0:T(1024)...) while((s32[]{:T(128)}, f32[10,4096]{1,0:T(8,128)S(1)}, ...), condition=%wide.region_11.13_spmd.clone.clone.clone, body=%wide.region_10.12_spmd.sunk.clone.clone.clone.sunk | while | flops 31526912 | bytes 2092045 | solution.py:100
  93.1 0.5 convolution_multiply_fusion.10
  95.5 0.5 convolution_multiply_fusion.10
  98.2 0.6 gather_fusion.5
  99.0 1.0 copy.72
  100.0 10.1 %all-to-all-start.3 = ((f32[10,2,32,128]{3,1,0,2:T(2,128)}), f32[10,2,32,128]{3,1,0,2:T(2,128)S(1)}, u32[]{:S(2)}, u32[]{:S(2)}) async-start(f32[10,2,32,128]{3,1,0,2:T(2,128)} %copy.72), calls=%async_computation.3 | async-start | bytes 655360 | tf_op jit(solution)/shard_map/all_to_all | solution.py:127
  110.3 2.1 %sort.62 = (s32[64]{0:T(128)}, s32[64]{0:T(128)S(1)}) sort(s32[64]{0:T(128)S(1)} %neg.6, s32[64]{0:T(128)S(1)} %iota.14), dimensions={0}, to_apply=%region_0.1 | sort | flops 384 | bytes 1024 | tf_op jit(solution)/shard_map/jit(argsort)/sort | solution.py:81
  112.4 2.1 %sort.63 = (s32[64]{0:T(128)}, s32[64]{0:T(128)S(1)}) sort(s32[64]{0:T(128)S(1)} %get-tuple-element.198, s32[64]{0:T(128)S(1)} %iota.15), dimensions={0}, to_apply=%region_6.9 | sort | flops 384 | bytes 1024 | tf_op jit(solution)/shard_map/jit(argsort)/sort | solution.py:105
  114.5 0.8 gather_fusion.1
  115.4 0.6 gather_fusion
  116.4 27.5 %while.53 = (s32[]{:T(128)}, f32[2,10,32,128]{3,2,0,1:T(8,128)S(1)}, f32[2,10,32,128]{3,2,1,0:T(8,128)S(1)}, s32[2,32]{1,0:T(2,128)S(1)}, f32[21]{0:T(128)S(1)},...) while((s32[]{:T(128)}, ...), condition=%wide.region_5.8_spmd.clone, body=%wide.region_1.7_spmd.sunk.clone.sunk | while | flops 31608864 | bytes 5074474 | solution.py:103
  116.7 0.7 fusion.103
  117.4 19.8 %while.56 = (s32[]{:T(128)}, f32[10,4096]{1,0:T(8,128)S(1)}, s32[]{:T(128)}, f32[10,21]{1,0:T(8,128)S(1)}, s32[32]{0:T(128)S(1)}, /*index=5*/f32[4096]{0:T(1024)...) while((s32[]{:T(128)}, f32[10,4096]{1,0:T(8,128)S(1)}, ...), condition=%wide.region_4.6_spmd.clone.clone.clone, body=%wide.region_3.5_spmd.sunk.clone.clone.clone.sunk | while | flops 31526912 | bytes 2092045 | solution.py:100
  118.0 0.5 convolution_multiply_fusion.12
  120.4 0.5 convolution_multiply_fusion.12
  122.8 0.5 convolution_multiply_fusion.12
  127.6 0.5 convolution_multiply_fusion.12
  130.0 0.5 convolution_multiply_fusion.12
  132.4 0.5 convolution_multiply_fusion.12
  137.6 0.7 fusion.103
  138.3 5.4 %while.56 = (s32[]{:T(128)}, f32[10,4096]{1,0:T(8,128)S(1)}, s32[]{:T(128)}, f32[10,21]{1,0:T(8,128)S(1)}, s32[32]{0:T(128)S(1)}, /*index=5*/f32[4096]{0:T(1024)...) while((s32[]{:T(128)}, f32[10,4096]{1,0:T(8,128)S(1)}, ...), condition=%wide.region_4.6_spmd.clone.clone.clone, body=%wide.region_3.5_spmd.sunk.clone.clone.clone.sunk | while | flops 31526912 | bytes 2092045 | solution.py:100
  139.0 0.5 convolution_multiply_fusion.12
  141.4 0.5 convolution_multiply_fusion.12
  144.1 0.6 gather_fusion.2
  144.9 1.0 copy.63
  145.9 10.1 %all-to-all-start.1 = ((f32[10,2,32,128]{3,1,0,2:T(2,128)}), f32[10,2,32,128]{3,1,0,2:T(2,128)S(1)}, u32[]{:S(2)}, u32[]{:S(2)}) async-start(f32[10,2,32,128]{3,1,0,2:T(2,128)} %copy.63), calls=%async_computation.1 | async-start | bytes 655360 | tf_op jit(solution)/shard_map/all_to_all | solution.py:127
  156.0 5.2 %collective-permute-start.4 = (f32[10,1,8,128]{3,2,1,0:T(8,128)S(1)}, f32[10,1,8,128]{3,2,1,0:T(8,128)S(1)}, u32[]{:S(2)}, u32[]{:S(2)}) collective-permute-start(f32[10,1,8,128]{3,2,1,0:T(8,128)S(1)} %get-tuple-element.549), channel_id=1, source_target_pairs={{32,0},{64,32},{96,64},{128,96},{160,128},{192,160},{224,192},{256... | collective-permute-start | bytes 122888 | tf_op jit(solution)/shard_map/ppermute | solution.py:41
  161.2 1.9 %collective-permute-start.5 = (f32[10,1,8,128]{3,2,1,0:T(8,128)S(1)}, f32[10,1,8,128]{3,2,1,0:T(8,128)S(1)}, u32[]{:S(2)}, u32[]{:S(2)}) collective-permute-start(f32[10,1,8,128]{3,2,1,0:T(8,128)S(1)} %get-tuple-element.548), channel_id=1, source_target_pairs={{0,32},{32,64},{64,96},{96,128},{128,160},{160,192},{192,224},{224... | collective-permute-start | bytes 122888 | tf_op jit(solution)/shard_map/ppermute | solution.py:40
  163.3 8.2 %collective-permute-done.5 = f32[10,1,8,128]{3,2,1,0:T(8,128)S(1)} collective-permute-done((f32[10,1,8,128]{3,2,1,0:T(8,128)S(1)}, f32[10,1,8,128]{3,2,1,0:T(8,128)S(1)}, u32[]{:S(2)}, u32[]{:S(2)}) %collective-permute-start.5) | collective-permute-done | bytes 40992 | tf_op jit(solution)/shard_map/ppermute | solution.py:40
  171.6 8.5 %collective-permute-start.6 = (f32[10,10,1,128]{3,2,1,0:T(1,128)S(1)}, f32[10,10,1,128]{3,2,1,0:T(1,128)S(1)}, u32[]{:S(2)}, u32[]{:S(2)}) collective-permute-start(f32[10,10,1,128]{3,2,1,0:T(1,128)S(1)} %get-tuple-element.540), channel_id=1, source_target_pairs={{1,0},{2,1},{3,2},{4,3},{5,4},{6,5},{7,6},{8,7},{9,8},{10,9},{11,1... | collective-permute-start | bytes 153608 | tf_op jit(solution)/shard_map/ppermute | solution.py:41
  180.1 1.9 %collective-permute-start.7 = (f32[10,10,1,128]{3,2,1,0:T(1,128)S(1)}, f32[10,10,1,128]{3,2,1,0:T(1,128)S(1)}, u32[]{:S(2)}, u32[]{:S(2)}) collective-permute-start(f32[10,10,1,128]{3,2,1,0:T(1,128)S(1)} %get-tuple-element.541), channel_id=1, source_target_pairs={{0,1},{1,2},{2,3},{3,4},{4,5},{5,6},{6,7},{7,8},{8,9},{9,10},{10,1... | collective-permute-start | bytes 153608 | tf_op jit(solution)/shard_map/ppermute | solution.py:40
  182.2 0.8 copy.73
  183.0 7.0 %collective-permute-done.7 = f32[10,10,1,128]{3,2,1,0:T(1,128)S(1)} collective-permute-done((f32[10,10,1,128]{3,2,1,0:T(1,128)S(1)}, f32[10,10,1,128]{3,2,1,0:T(1,128)S(1)}, u32[]{:S(2)}, u32[]{:S(2)}) %collective-permute-start.7) | collective-permute-done | bytes 51232 | tf_op jit(solution)/shard_map/ppermute | solution.py:40
  190.0 1.1 fusion.53
  (194 shorter events, 30.4 us)
Async XLA Ops:
  1.4 17.6 %collective-permute-start.1 = (f32[10,1,8,128]{3,2,1,0:T(8,128)S(1)}, f32[10,1,8,128]{3,2,1,0:T(8,128)S(1)}, u32[]{:S(2)}, u32[]{:S(2)}) collective-permute-start(f32[10,1,8,128]{3,2,1,0:T(8,128)S(1)} %get-tuple-element.555), channel_id=1, source_target_pairs={{0,32},{32,64},{64,96},{96,128},{128,160},{160,192},{192,224},{224... | collective-permute-start | bytes 122888 | tf_op jit(solution)/shard_map/ppermute | solution.py:40
  3.4 15.7 %copy-start.1 = (f32[10,8,8,128]{3,2,1,0:T(8,128)S(1)}, f32[10,8,8,128]{3,2,1,0:T(8,128)}, u32[]{:S(2)}) copy-start(f32[10,8,8,128]{3,2,1,0:T(8,128)} %param.25) | copy-start | bytes 983044
  3.4 16.1 %collective-permute-start = (f32[10,1,8,128]{3,2,1,0:T(8,128)S(1)}, f32[10,1,8,128]{3,2,1,0:T(8,128)S(1)}, u32[]{:S(2)}, u32[]{:S(2)}) collective-permute-start(f32[10,1,8,128]{3,2,1,0:T(8,128)S(1)} %get-tuple-element.554), channel_id=1, source_target_pairs={{32,0},{64,32},{96,64},{128,96},{160,128},{192,160},{224,192},{256... | collective-permute-start | bytes 122888 | tf_op jit(solution)/shard_map/ppermute | solution.py:41
  19.5 10.5 %collective-permute-start.2 = (f32[10,10,1,128]{3,2,1,0:T(1,128)S(1)}, f32[10,10,1,128]{3,2,1,0:T(1,128)S(1)}, u32[]{:S(2)}, u32[]{:S(2)}) collective-permute-start(f32[10,10,1,128]{3,2,1,0:T(1,128)S(1)} %get-tuple-element.542), channel_id=1, source_target_pairs={{1,0},{2,1},{3,2},{4,3},{5,4},{6,5},{7,6},{8,7},{9,8},{10,9},{11,1... | collective-permute-start | bytes 153608 | tf_op jit(solution)/shard_map/ppermute | solution.py:41
  27.6 2.2 %copy-start.5 = (s32[8,8]{1,0:T(8,128)S(1)}, s32[8,8]{1,0:T(8,128)}, u32[]{:S(2)}) copy-start(s32[8,8]{1,0:T(8,128)} %param.27) | copy-start | bytes 772
  27.6 10.1 %copy-start.3 = (f32[10,8,8,128]{3,2,1,0:T(8,128)S(1)}, f32[10,8,8,128]{3,2,1,0:T(8,128)}, u32[]{:S(2)}) copy-start(f32[10,8,8,128]{3,2,1,0:T(8,128)} %param.26) | copy-start | bytes 983044
  27.6 10.0 %collective-permute-start.3 = (f32[10,10,1,128]{3,2,1,0:T(1,128)S(1)}, f32[10,10,1,128]{3,2,1,0:T(1,128)S(1)}, u32[]{:S(2)}, u32[]{:S(2)}) collective-permute-start(f32[10,10,1,128]{3,2,1,0:T(1,128)S(1)} %get-tuple-element.543), channel_id=1, source_target_pairs={{0,1},{1,2},{2,3},{3,4},{4,5},{5,6},{6,7},{7,8},{8,9},{9,10},{10,1... | collective-permute-start | bytes 153608 | tf_op jit(solution)/shard_map/ppermute | solution.py:40
  37.7 0.7 copy-start.6
  39.9 4.0 %copy-start.4 = (f32[9,21]{1,0:T(8,128)S(1)}, f32[9,21]{1,0:T(8,128)}, u32[]{:S(2)}) copy-start(f32[9,21]{1,0:T(8,128)} %constant.83.clone) | copy-start | bytes 2272
  39.9 16.6 %all-to-all-start.2 = ((f32[11,2,32,128]{3,1,0,2:T(2,128)}), f32[11,2,32,128]{3,1,0,2:T(2,128)S(1)}, u32[]{:S(2)}, u32[]{:S(2)}) async-start(f32[11,2,32,128]{3,1,0,2:T(2,128)} %copy.65), calls=%async_computation.2 | async-start | bytes 720896 | tf_op jit(solution)/shard_map/all_to_all | solution.py:123
  43.9 0.7 copy-start.7
  56.5 43.5 %all-to-all-start = ((f32[11,2,32,128]{3,1,0,2:T(2,128)}), f32[11,2,32,128]{3,1,0,2:T(2,128)S(1)}, u32[]{:S(2)}, u32[]{:S(2)}) async-start(f32[11,2,32,128]{3,1,0,2:T(2,128)} %copy.56), calls=%async_computation | async-start | bytes 720896 | tf_op jit(solution)/shard_map/all_to_all | solution.py:123
  69.9 0.7 copy-start
  69.9 0.7 copy-start.2
  69.9 0.7 copy-start.8
  69.9 0.7 copy-start.9
  69.9 0.8 copy-start.10
  100.0 45.9 %all-to-all-start.3 = ((f32[10,2,32,128]{3,1,0,2:T(2,128)}), f32[10,2,32,128]{3,1,0,2:T(2,128)S(1)}, u32[]{:S(2)}, u32[]{:S(2)}) async-start(f32[10,2,32,128]{3,1,0,2:T(2,128)} %copy.72), calls=%async_computation.3 | async-start | bytes 655360 | tf_op jit(solution)/shard_map/all_to_all | solution.py:127
  145.9 37.1 %all-to-all-start.1 = ((f32[10,2,32,128]{3,1,0,2:T(2,128)}), f32[10,2,32,128]{3,1,0,2:T(2,128)S(1)}, u32[]{:S(2)}, u32[]{:S(2)}) async-start(f32[10,2,32,128]{3,1,0,2:T(2,128)} %copy.63), calls=%async_computation.1 | async-start | bytes 655360 | tf_op jit(solution)/shard_map/all_to_all | solution.py:127
  156.0 7.3 %collective-permute-start.4 = (f32[10,1,8,128]{3,2,1,0:T(8,128)S(1)}, f32[10,1,8,128]{3,2,1,0:T(8,128)S(1)}, u32[]{:S(2)}, u32[]{:S(2)}) collective-permute-start(f32[10,1,8,128]{3,2,1,0:T(8,128)S(1)} %get-tuple-element.549), channel_id=1, source_target_pairs={{32,0},{64,32},{96,64},{128,96},{160,128},{192,160},{224,192},{256... | collective-permute-start | bytes 122888 | tf_op jit(solution)/shard_map/ppermute | solution.py:41
  161.2 10.3 %collective-permute-start.5 = (f32[10,1,8,128]{3,2,1,0:T(8,128)S(1)}, f32[10,1,8,128]{3,2,1,0:T(8,128)S(1)}, u32[]{:S(2)}, u32[]{:S(2)}) collective-permute-start(f32[10,1,8,128]{3,2,1,0:T(8,128)S(1)} %get-tuple-element.548), channel_id=1, source_target_pairs={{0,32},{32,64},{64,96},{96,128},{128,160},{160,192},{192,224},{224... | collective-permute-start | bytes 122888 | tf_op jit(solution)/shard_map/ppermute | solution.py:40
  171.6 11.4 %collective-permute-start.6 = (f32[10,10,1,128]{3,2,1,0:T(1,128)S(1)}, f32[10,10,1,128]{3,2,1,0:T(1,128)S(1)}, u32[]{:S(2)}, u32[]{:S(2)}) collective-permute-start(f32[10,10,1,128]{3,2,1,0:T(1,128)S(1)} %get-tuple-element.540), channel_id=1, source_target_pairs={{1,0},{2,1},{3,2},{4,3},{5,4},{6,5},{7,6},{8,7},{9,8},{10,9},{11,1... | collective-permute-start | bytes 153608 | tf_op jit(solution)/shard_map/ppermute | solution.py:41
  180.1 9.9 %collective-permute-start.7 = (f32[10,10,1,128]{3,2,1,0:T(1,128)S(1)}, f32[10,10,1,128]{3,2,1,0:T(1,128)S(1)}, u32[]{:S(2)}, u32[]{:S(2)}) collective-permute-start(f32[10,10,1,128]{3,2,1,0:T(1,128)S(1)} %get-tuple-element.541), channel_id=1, source_target_pairs={{0,1},{1,2},{2,3},{3,4},{4,5},{5,6},{6,7},{7,8},{8,9},{9,10},{10,1... | collective-permute-start | bytes 153608 | tf_op jit(solution)/shard_map/ppermute | solution.py:40
where the time goes:
time: 192 us; the launch traced here: 191 us
  starting transfers between devices  75.6 us (39%)
  waiting for transfers between devices  34.2 us (18%)
  matrix products  31.6 us (16%)
  other arithmetic  16.6 us (9%)
  loops' own time  16.1 us (8%)
  local copies, waits for them, and re-layouts  15.9 us (8%)
    ppermute x4, starting transfers between devices, with_halo(): after = lax.ppermute(initial, axis, down)  36.2 us
    ppermute x4, waiting for transfers between devices, with_halo(): before = lax.ppermute(last, axis, up)  22.9 us
    all_to_all x2, starting transfers between devices, chemistry(): lax.all_to_all(produced.reshape(field_count, rounds, helpers, length_z),...  20.3 us
    another operation x4, loops' own time, integrate_group(): finished = lax.fori_loop(0, jnp.max(counts_group), substep, cell_rows)  15.8 us
    all_to_all x2, starting transfers between devices, chemistry(): lax.all_to_all(tagged, 'gy', split_axis=2, concat_axis=2, tiled=True)  11.3 us
    all_to_all x2, waiting for transfers between devices, chemistry(): lax.all_to_all(tagged, 'gy', split_axis=2, concat_axis=2, tiled=True)  10.9 us
    dot_general x20, matrix products, advance(): reactant_one = jnp.dot(leading, augmented, precision=lax.Precision.HIGHEST)  10.9 us
    dot_general x20, matrix products, advance(): reactant_two = jnp.dot(trailing, augmented, precision=lax.Precision.HIGHEST)  10.6 us
  transfers between devices with their start and end apart: 12, of which 5 were waited for; matrix products, arithmetic and copies ran while one was open for 31% of the time, Pallas kernels for 0%

commit v1 on v0

v1 whole, which is shorter than its diff:
```python
import jax
import jax.numpy as jnp
import numpy as np
from jax import lax
from jax.experimental import pallas as pl
from jax.experimental.pallas import tpu as pltpu
from jax.sharding import PartitionSpec as P

time_step = 0.15
reaction_table = (
    (3, 1, (4, 5)),
    (4, 0, (3, 5)),
    (5, 0, (3, 2)),
    (5, 5, (4, 2)),
    (3, 3, (0,)),
    (3, 5, (2,)),
    (4, 4, (1,)),
    (3, 4, (5,)),
    (3, 1, (6,)),
    (6, 3, (0, 1)),
    (6, 3, (5, 5)),
    (6, 4, (1, 5)),
    (6, 5, (2, 1)),
    (6, 6, (7, 1)),
    (7, 9, (5, 5)),
    (7, 3, (2, 5)),
    (7, 3, (6, 0)),
    (7, 4, (5, 6)),
    (7, 5, (6, 2)),
    (0, 9, (3, 3)),
    (2, 9, (3, 5)),
)
SPECIES = 9
CMAX = 8


def stoichiometry():
    change = np.zeros((SPECIES, len(reaction_table)), np.int64)
    for reaction, entry in enumerate(reaction_table):
        change[entry[0], reaction] -= 1
        if entry[1] < SPECIES:
            change[entry[1], reaction] -= 1
        for product in entry[2]:
            change[product, reaction] += 1
    return change


def chem_kernel(rate_ref, act_ref, heat_ref, u_ref, cnt_ref, o_ref):
    change = stoichiometry()
    reactions = len(reaction_table)
    rows = u_ref.shape[0]

    def per_x(x, carry):
        start = [u_ref[s, x] for s in range(rows)]
        temper = start[rows - 1]
        coeffs = [jnp.exp(rate_ref[r] - act_ref[r] / temper) for r in range(reactions)]
        heat = [heat_ref[r] for r in range(reactions)]
        cnt = cnt_ref[x]
        stride = time_step / cnt.astype(jnp.float32)
        cur = list(start)
        for turn in range(CMAX):
            active = turn < cnt
            rates = []
            for r, entry in enumerate(reaction_table):
                term = coeffs[r] * cur[entry[0]]
                if entry[1] < SPECIES:
                    term = term * cur[entry[1]]
                rates.append(term)
            new = []
            for s in range(SPECIES):
                total = None
                for r in range(reactions):
                    c = int(change[s, r])
                    if c == 0:
                        continue
                    piece = rates[r] if abs(c) == 1 else rates[r] * float(abs(c))
                    if total is None:
                        total = piece if c > 0 else -piece
                    elif c > 0:
                        total = total + piece
                    else:
                        total = total - piece
                if total is None:
                    new.append(cur[s])
                else:
                    new.append(jnp.where(active, cur[s] + stride * total, cur[s]))
            heat_total = heat[0] * rates[0]
            for r in range(1, reactions):
                heat_total = heat_total + heat[r] * rates[r]
            new.append(jnp.where(active, cur[SPECIES] + stride * heat_total, cur[SPECIES]))
            cur = new
        for s in range(rows):
            o_ref[s, x] = (cur[s] - start[s]) / time_step
        return carry

    lax.fori_loop(0, u_ref.shape[1], per_x, 0)


def chemistry(fields, cell_counts, log_rate, activation, heat_release):
    smem = pl.BlockSpec(memory_space=pltpu.SMEM)
    vmem = pl.BlockSpec(memory_space=pltpu.VMEM)
    return pl.pallas_call(
        chem_kernel,
        out_shape=jax.ShapeDtypeStruct(fields.shape, jnp.float32),
        in_specs=[smem, smem, smem, vmem, vmem],
        out_specs=vmem,
    )(log_rate, activation, heat_release, fields, cell_counts)


def shift_pairs(size, step):
    return [(i, (i + step) % size) for i in range(size)]


def diag_pairs(nx, ny, sx, sy):
    return [
        (i * ny + j, ((i + sx) % nx) * ny + (j + sy) % ny)
        for i in range(nx)
        for j in range(ny)
    ]


def laplace_parts(s, lo, hi):
    c = s[:, lo:hi, lo:hi]
    beside = s[:, lo - 1:hi - 1, lo:hi] + s[:, lo + 1:hi + 1, lo:hi]
    beside = beside + s[:, lo:hi, lo - 1:hi - 1] + s[:, lo:hi, lo + 1:hi + 1]
    beside = beside + jnp.roll(c, 1, 3) + jnp.roll(c, -1, 3)
    return beside - 6.0 * c


def local(state, source_in, counts, diffusivity, log_rate, activation, heat_release):
    nx = lax.axis_size("gx")
    ny = lax.axis_size("gy")
    rows, cx, cy, cz = state.shape
    spread = diffusivity[:, None, None, None]
    cell_counts = jnp.broadcast_to(counts[:, :, None], (cx, cy, cz))

    to_xp = jnp.concatenate([state[:, cx - 2:], source_in[:, cx - 1:]], 1)
    to_xm = jnp.concatenate([state[:, :2], source_in[:, :1]], 1)
    to_yp = jnp.concatenate([state[:, :, cy - 2:], source_in[:, :, cy - 1:]], 2)
    to_ym = jnp.concatenate([state[:, :, :2], source_in[:, :, :1]], 2)
    from_xm = lax.ppermute(to_xp, "gx", shift_pairs(nx, 1))
    from_xp = lax.ppermute(to_xm, "gx", shift_pairs(nx, -1))
    from_ym = lax.ppermute(to_yp, "gy", shift_pairs(ny, 1))
    from_yp = lax.ppermute(to_ym, "gy", shift_pairs(ny, -1))
    both = ("gx", "gy")
    c_mm = lax.ppermute(state[:, cx - 1:, cy - 1:], both, diag_pairs(nx, ny, 1, 1))
    c_mp = lax.ppermute(state[:, cx - 1:, :1], both, diag_pairs(nx, ny, 1, -1))
    c_pm = lax.ppermute(state[:, :1, cy - 1:], both, diag_pairs(nx, ny, -1, 1))
    c_pp = lax.ppermute(state[:, :1, :1], both, diag_pairs(nx, ny, -1, -1))

    early = chemistry(state, cell_counts, log_rate, activation, heat_release)

    def zeros(a, b):
        return jnp.zeros((rows, a, b, cz), jnp.float32)

    s_xm, q_xm = from_xm[:, :2], from_xm[:, 2:]
    s_xp, q_xp = from_xp[:, :2], from_xp[:, 2:]
    s_ym, q_ym = from_ym[:, :, :2], from_ym[:, :, 2:]
    s_yp, q_yp = from_yp[:, :, :2], from_yp[:, :, 2:]
    ext = jnp.concatenate(
        [
            jnp.concatenate([zeros(1, 2), s_xm[:, :1], zeros(1, 2)], 2),
            jnp.concatenate([zeros(1, 1), c_mm, s_xm[:, 1:], c_mp, zeros(1, 1)], 2),
            jnp.concatenate([s_ym, state, s_yp], 2),
            jnp.concatenate([zeros(1, 1), c_pm, s_xp[:, :1], c_pp, zeros(1, 1)], 2),
            jnp.concatenate([zeros(1, 2), s_xp[:, 1:], zeros(1, 2)], 2),
        ],
        1,
    )
    src = jnp.concatenate(
        [
            jnp.concatenate([zeros(1, 1), q_xm, zeros(1, 1)], 2),
            jnp.concatenate([q_ym, source_in, q_yp], 2),
            jnp.concatenate([zeros(1, 1), q_xp, zeros(1, 1)], 2),
        ],
        1,
    )
    first_ext = ext[:, 1:-1, 1:-1] + time_step * (
        spread * laplace_parts(ext, 1, cx + 3) + src
    )
    first_section = first_ext[:, 1:-1, 1:-1]
    next_state = 0.5 * state + 0.5 * (
        first_section + time_step * (spread * laplace_parts(first_ext, 1, cx + 1) + early)
    )
    late_source = chemistry(first_section, cell_counts, log_rate, activation, heat_release)
    return (next_state, late_source)


def solution(mesh):
    in_specs = (
        P(None, "gx", "gy", None),
        P(None, "gx", "gy", None),
        P("gx", "gy"),
        P(),
        P(),
        P(),
        P(),
    )
    out_specs = (P(None, "gx", "gy", None), P(None, "gx", "gy", None))
    return jax.shard_map(local, mesh=mesh, in_specs=in_specs, out_specs=out_specs, check_vma=False)
```

time: 192 us -> 68.4 us (0.36)
  the two profiles are of different devices: /device:TPU:6 before, /device:TPU:1 now
where the time goes in v1:
time: 68.4 us; the launch traced here: 67.8 us
  starting transfers between devices  45.3 us (66%)
  Pallas kernels  7.22 us (11%)
  local copies, waits for them, and re-layouts  6.06 us (9%)
  waiting for transfers between devices  5.47 us (8%)
  other arithmetic  2.87 us (4%)
  between operations  0.96 us (1%)
    ppermute x1, starting transfers between devices, local(): c_mp = lax.ppermute(state[:, cx - 1:, :1], both, diag_pairs(nx, ny, 1, -1))  12.3 us
    ppermute x1, starting transfers between devices, local(): from_xm = lax.ppermute(to_xp, 'gx', shift_pairs(nx, 1))  12.2 us
    ppermute x1, starting transfers between devices, local(): c_pp = lax.ppermute(state[:, :1, :1], both, diag_pairs(nx, ny, -1, -1))  7.88 us
    pallas_call x2, Pallas kernels, chemistry(): pl.pallas_call(chem_kernel, out_shape=jax.ShapeDtypeStruct(fields.shape,...  7.22 us
    ppermute x1, starting transfers between devices, local(): from_yp = lax.ppermute(to_ym, 'gy', shift_pairs(ny, -1))  3.86 us
    ppermute x1, starting transfers between devices, local(): lax.ppermute(state[:, cx - 1:, cy - 1:], both, diag_pairs(nx, ny, 1, 1))  2.93 us
    ppermute x1, waiting for transfers between devices, local(): from_yp = lax.ppermute(to_ym, 'gy', shift_pairs(ny, -1))  2.75 us
    ppermute x1, starting transfers between devices, local(): from_ym = lax.ppermute(to_yp, 'gy', shift_pairs(ny, 1))  2.3 us
  transfers between devices with their start and end apart: 8, of which 3 were waited for; matrix products, arithmetic and copies ran while one was open for 2% of the time, Pallas kernels for 5%

profile of v1, /device:TPU:1, one launch (start us, length us, event | category | flops | bytes accessed | tf_op | source)
XLA Modules:
  0.0 67.8 jit_solution(922733580376212878)
XLA Ops:
  0.6 0.0 copy-start
  0.6 1.0 %fusion.25 = (f32[10,2,8,128]{3,2,1,0:T(8,128)S(1)}, f32[10,2,8,128]{3,2,1,0:T(8,128)S(1)}) fusion(f32[10,8,8,128]{3,2,1,0:T(8,128)} %u_ref.1), kind=kLoop, calls=%fused_computation.45 | loop fusion | bytes 327680 | tf_op jit(solution)/shard_map/slice | solution.py:137
  1.6 0.8 %fusion.26 = (f32[10,1,8,128]{3,2,1,0:T(8,128)S(1)}, f32[10,1,8,128]{3,2,1,0:T(8,128)S(1)}) fusion(f32[10,8,8,128]{3,2,1,0:T(8,128)} %param.8), kind=kLoop, calls=%fused_computation.46 | loop fusion | bytes 163840 | tf_op jit(solution)/shard_map/slice | solution.py:137
  2.5 0.0 copy-start.3
  2.5 12.2 %collective-permute-start.1 = (f32[10,3,8,128]{3,2,1,0:T(8,128)S(1)}, f32[10,3,8,128]{3,2,1,0:T(8,128)S(1)}, u32[]{:S(2)}, u32[]{:S(2)}) collective-permute-start(f32[10,3,8,128]{3,2,1,0:T(8,128)S(1)} %pad_maximum_fusion.13), channel_id=1, source_target_pairs={{0,32},{32,64},{64,96},{96,128},{128,160},{160,192},{192,224},{224... | collective-permute-start | bytes 368648 | tf_op jit(solution)/shard_map/ppermute | solution.py:141
  14.6 0.0 copy-done
  14.7 2.9 %collective-permute-start = (f32[10,1,1,128]{3,2,1,0:T(1,128)S(1)}, f32[10,1,1,128]{3,2,1,0:T(1,128)S(1)}, u32[]{:S(2)}, u32[]{:S(2)}) collective-permute-start(f32[10,1,1,128]{3,2,1,0:T(1,128)S(1)} %get-tuple-element.15), channel_id=1, source_target_pairs={{0,33},{1,34},{2,35},{3,36},{4,37},{5,38},{6,39},{7,40},{8,41},{9,... | collective-permute-start | bytes 15368 | tf_op jit(solution)/shard_map/ppermute | solution.py:146
  17.6 12.3 %collective-permute-start.2 = (f32[10,1,1,128]{3,2,1,0:T(1,128)S(1)}, f32[10,1,1,128]{3,2,1,0:T(1,128)S(1)}, u32[]{:S(2)}, u32[]{:S(2)}) collective-permute-start(f32[10,1,1,128]{3,2,1,0:T(1,128)S(1)} %get-tuple-element.12), channel_id=1, source_target_pairs={{0,63},{1,32},{2,33},{3,34},{4,35},{5,36},{6,37},{7,38},{8,39},{9,... | collective-permute-start | bytes 15368 | tf_op jit(solution)/shard_map/ppermute | solution.py:147
  29.9 1.9 %collective-permute-start.6 = (f32[10,3,8,128]{3,2,1,0:T(8,128)S(1)}, f32[10,3,8,128]{3,2,1,0:T(8,128)S(1)}, u32[]{:S(2)}, u32[]{:S(2)}) collective-permute-start(f32[10,3,8,128]{3,2,1,0:T(8,128)S(1)} %pad_maximum_fusion.14), channel_id=1, source_target_pairs={{0,736},{32,0},{64,32},{96,64},{128,96},{160,128},{192,160},{224,1... | collective-permute-start | bytes 368648 | tf_op jit(solution)/shard_map/ppermute | solution.py:142
  31.9 1.9 %collective-permute-start.5 = (f32[10,1,1,128]{3,2,1,0:T(1,128)S(1)}, f32[10,1,1,128]{3,2,1,0:T(1,128)S(1)}, u32[]{:S(2)}, u32[]{:S(2)}) collective-permute-start(f32[10,1,1,128]{3,2,1,0:T(1,128)S(1)} %get-tuple-element.14), channel_id=1, source_target_pairs={{0,737},{1,738},{2,739},{3,740},{4,741},{5,742},{6,743},{7,744},{8... | collective-permute-start | bytes 15368 | tf_op jit(solution)/shard_map/ppermute | solution.py:148
  33.8 0.1 fusion.27
  33.8 0.0 copy-done.3
  33.8 0.1 fusion.28
  33.9 0.0 copy-start.4
  33.9 0.1 pad_maximum_fusion.11
  34.0 0.6 copy-done.4
  34.6 0.7 broadcast_in_dim.2.cnt_ref
  35.3 3.6 %shard_map.86 = f32[10,8,8,128]{3,2,1,0:T(8,128)} custom-call(f32[21]{0:T(128)} %rate_ref.3, f32[21]{0:T(128)} %act_ref.3, f32[21]{0:T(128)} %heat_ref.3, f32[10,8,8,128]{3,2,1,0:T(8,128)} %u_ref.1, s32[8,8,128]{2,1,0:T(8,128)} %broadcast_in_dim.2.cnt_ref), custom_call_target="tpu_custom_call" | custom-call | tf_op jit(solution)/shard_map/pallas_call | solution.py:102
  38.9 0.1 pad_maximum_fusion.12
  39.0 0.0 collective-permute-done.1
  39.0 2.3 %collective-permute-start.3 = (f32[10,8,3,128]{3,2,1,0:T(4,128)S(1)}, f32[10,8,3,128]{3,2,1,0:T(4,128)S(1)}, u32[]{:S(2)}, u32[]{:S(2)}) collective-permute-start(f32[10,8,3,128]{3,2,1,0:T(4,128)S(1)} %pad_maximum_fusion.11), channel_id=1, source_target_pairs={{0,1},{1,2},{2,3},{3,4},{4,5},{5,6},{6,7},{7,8},{8,9},{9,10},{10,1... | collective-permute-start | bytes 368648 | tf_op jit(solution)/shard_map/ppermute | solution.py:143
  41.3 0.7 %collective-permute-done.6 = f32[10,3,8,128]{3,2,1,0:T(8,128)S(1)} collective-permute-done((f32[10,3,8,128]{3,2,1,0:T(8,128)S(1)}, f32[10,3,8,128]{3,2,1,0:T(8,128)S(1)}, u32[]{:S(2)}, u32[]{:S(2)}) %collective-permute-start.6) | collective-permute-done | bytes 122912 | tf_op jit(solution)/shard_map/ppermute | solution.py:142
  42.0 7.9 %collective-permute-start.7 = (f32[10,1,1,128]{3,2,1,0:T(1,128)S(1)}, f32[10,1,1,128]{3,2,1,0:T(1,128)S(1)}, u32[]{:S(2)}, u32[]{:S(2)}) collective-permute-start(f32[10,1,1,128]{3,2,1,0:T(1,128)S(1)} %get-tuple-element.13), channel_id=1, source_target_pairs={{0,767},{1,736},{2,737},{3,738},{4,739},{5,740},{6,741},{7,742},{8... | collective-permute-start | bytes 15368 | tf_op jit(solution)/shard_map/ppermute | solution.py:149
  49.9 2.0 %collective-permute-done.3 = f32[10,8,3,128]{3,2,1,0:T(4,128)S(1)} collective-permute-done((f32[10,8,3,128]{3,2,1,0:T(4,128)S(1)}, f32[10,8,3,128]{3,2,1,0:T(4,128)S(1)}, u32[]{:S(2)}, u32[]{:S(2)}) %collective-permute-start.3) | collective-permute-done | bytes 122912 | tf_op jit(solution)/shard_map/ppermute | solution.py:143
  51.9 3.9 %collective-permute-start.4 = (f32[10,8,3,128]{3,2,1,0:T(4,128)S(1)}, f32[10,8,3,128]{3,2,1,0:T(4,128)S(1)}, u32[]{:S(2)}, u32[]{:S(2)}) collective-permute-start(f32[10,8,3,128]{3,2,1,0:T(4,128)S(1)} %pad_maximum_fusion.12), channel_id=1, source_target_pairs={{0,31},{1,0},{2,1},{3,2},{4,3},{5,4},{6,5},{7,6},{8,7},{9,8},{10,9... | collective-permute-start | bytes 368648 | tf_op jit(solution)/shard_map/ppermute | solution.py:144
  55.8 0.0 copy-start.1
  55.8 2.7 %collective-permute-done.4 = f32[10,8,3,128]{3,2,1,0:T(4,128)S(1)} collective-permute-done((f32[10,8,3,128]{3,2,1,0:T(4,128)S(1)}, f32[10,8,3,128]{3,2,1,0:T(4,128)S(1)}, u32[]{:S(2)}, u32[]{:S(2)}) %collective-permute-start.4) | collective-permute-done | bytes 122912 | tf_op jit(solution)/shard_map/ppermute | solution.py:144
  58.6 0.0 collective-permute-done
  58.6 0.0 collective-permute-done.2
  58.7 0.2 concatenate.68
  58.8 0.0 collective-permute-done.5
  58.8 0.0 collective-permute-done.7
  58.8 0.2 concatenate.73
  59.0 0.0 copy-done.1
  59.0 0.1 pad_maximum_fusion.10
  59.2 0.3 fusion.23
  59.5 0.3 fusion.22
  59.9 0.0 copy-start.5
  59.9 0.6 copy-done.5
  60.5 1.4 %fusion.6 = f32[10,10,10,128]{3,2,1,0:T(8,128)S(1)} fusion(f32[10,10,12,128]{3,2,1,0:T(8,128)S(1)} %pad_maximum_fusion.10, f32[10,1,2,128]{3,2,1,0:T(2,128)S(1)} %broadcast.12, f32[10,1,12,128]{3,2,1,0:T(8,128)S(1)} %concatenate.73, f32[10,1,8,128]{3,2,1,0:T(8,128)S(1)} %get-tuple-element.28, f32[10,8,2,128]{3,2,1,0:T(2,128)S(1)} %slice.191, ...), kind=kLoop, calls=%fused_computation.7 | loop fusion | flops 4224000 | bytes 4275240 | tf_op jit(solution)/shard_map/add | solution.py:178
  61.9 0.2 fusion.20
  62.1 0.0 copy-start.2
  62.1 0.2 fusion.21
  62.2 0.8 %copy-done.2 = f32[10,8,8,128]{3,2,1,0:T(8,128)S(1)} copy-done((f32[10,8,8,128]{3,2,1,0:T(8,128)S(1)}, f32[10,8,8,128]{3,2,1,0:T(8,128)}, u32[]{:S(2)}) %copy-start.2) | copy-done | bytes 327704
  63.0 1.2 %fusion.19 = (f32[10,8,8,128]{3,2,1,0:T(8,128)}, f32[10,8,8,128]{3,2,1,0:T(8,128)}) fusion(f32[10,10,10,128]{3,2,1,0:T(8,128)S(1)} %fusion.6, f32[10,8,8,128]{3,2,1,0:T(8,128)S(1)} %copy-done.1, f32[10,8,8,128]{3,2,1,0:T(8,128)S(1)} %copy-done.2, f32[10,8,8,1]{3,2,1,0:T(8,128)S(1)} %get-tuple-element.6, f32[10,8,8,127]{3,2,1,0:T(8,128)S(1)} %get-tuple-element.4, ...), kind=kLoop, calls=%fused_computation.39 | loop fusion | flops 1228800 | bytes 3604520 | tf_op jit(solution)/shard_map/slice | solution.py:181
  64.2 3.6 %shard_map.87 = f32[10,8,8,128]{3,2,1,0:T(8,128)} custom-call(f32[21]{0:T(128)} %rate_ref.3, f32[21]{0:T(128)} %act_ref.3, f32[21]{0:T(128)} %heat_ref.3, f32[10,8,8,128]{3,2,1,0:T(8,128)} %get-tuple-element.2.u_ref, s32[8,8,128]{2,1,0:T(8,128)} %broadcast_in_dim.2.cnt_ref), custom_call_target="tpu_custom_call" | custom-call | tf_op jit(solution)/shard_map/pallas_call | solution.py:102
  (11 shorter events, 0.2 us)
Async XLA Ops:
  0.6 14.0 %copy-start = (f32[10,8,8,128]{3,2,1,0:T(8,128)S(1)}, f32[10,8,8,128]{3,2,1,0:T(8,128)}, u32[]{:S(2)}) copy-start(f32[10,8,8,128]{3,2,1,0:T(8,128)} %u_ref.1) | copy-start | bytes 983044
  2.5 31.4 %copy-start.3 = (f32[10,8,8,128]{3,2,1,0:T(8,128)S(1)}, f32[10,8,8,128]{3,2,1,0:T(8,128)}, u32[]{:S(2)}) copy-start(f32[10,8,8,128]{3,2,1,0:T(8,128)} %param.8) | copy-start | bytes 983044
  2.5 36.5 %collective-permute-start.1 = (f32[10,3,8,128]{3,2,1,0:T(8,128)S(1)}, f32[10,3,8,128]{3,2,1,0:T(8,128)S(1)}, u32[]{:S(2)}, u32[]{:S(2)}) collective-permute-start(f32[10,3,8,128]{3,2,1,0:T(8,128)S(1)} %pad_maximum_fusion.13), channel_id=1, source_target_pairs={{0,32},{32,64},{64,96},{96,128},{128,160},{160,192},{192,224},{224... | collective-permute-start | bytes 368648 | tf_op jit(solution)/shard_map/ppermute | solution.py:141
  14.7 44.0 %collective-permute-start = (f32[10,1,1,128]{3,2,1,0:T(1,128)S(1)}, f32[10,1,1,128]{3,2,1,0:T(1,128)S(1)}, u32[]{:S(2)}, u32[]{:S(2)}) collective-permute-start(f32[10,1,1,128]{3,2,1,0:T(1,128)S(1)} %get-tuple-element.15), channel_id=1, source_target_pairs={{0,33},{1,34},{2,35},{3,36},{4,37},{5,38},{6,39},{7,40},{8,41},{9,... | collective-permute-start | bytes 15368 | tf_op jit(solution)/shard_map/ppermute | solution.py:146
  17.6 41.0 %collective-permute-start.2 = (f32[10,1,1,128]{3,2,1,0:T(1,128)S(1)}, f32[10,1,1,128]{3,2,1,0:T(1,128)S(1)}, u32[]{:S(2)}, u32[]{:S(2)}) collective-permute-start(f32[10,1,1,128]{3,2,1,0:T(1,128)S(1)} %get-tuple-element.12), channel_id=1, source_target_pairs={{0,63},{1,32},{2,33},{3,34},{4,35},{5,36},{6,37},{7,38},{8,39},{9,... | collective-permute-start | bytes 15368 | tf_op jit(solution)/shard_map/ppermute | solution.py:147
  29.9 12.1 %collective-permute-start.6 = (f32[10,3,8,128]{3,2,1,0:T(8,128)S(1)}, f32[10,3,8,128]{3,2,1,0:T(8,128)S(1)}, u32[]{:S(2)}, u32[]{:S(2)}) collective-permute-start(f32[10,3,8,128]{3,2,1,0:T(8,128)S(1)} %pad_maximum_fusion.14), channel_id=1, source_target_pairs={{0,736},{32,0},{64,32},{96,64},{128,96},{160,128},{192,160},{224,1... | collective-permute-start | bytes 368648 | tf_op jit(solution)/shard_map/ppermute | solution.py:142
  31.9 27.0 %collective-permute-start.5 = (f32[10,1,1,128]{3,2,1,0:T(1,128)S(1)}, f32[10,1,1,128]{3,2,1,0:T(1,128)S(1)}, u32[]{:S(2)}, u32[]{:S(2)}) collective-permute-start(f32[10,1,1,128]{3,2,1,0:T(1,128)S(1)} %get-tuple-element.14), channel_id=1, source_target_pairs={{0,737},{1,738},{2,739},{3,740},{4,741},{5,742},{6,743},{7,744},{8... | collective-permute-start | bytes 15368 | tf_op jit(solution)/shard_map/ppermute | solution.py:148
  33.9 0.7 %copy-start.4 = (s32[8,8]{1,0:T(8,128)S(1)}, s32[8,8]{1,0:T(8,128)}, u32[]{:S(2)}) copy-start(s32[8,8]{1,0:T(8,128)} %param.9) | copy-start | bytes 772
  39.0 12.9 %collective-permute-start.3 = (f32[10,8,3,128]{3,2,1,0:T(4,128)S(1)}, f32[10,8,3,128]{3,2,1,0:T(4,128)S(1)}, u32[]{:S(2)}, u32[]{:S(2)}) collective-permute-start(f32[10,8,3,128]{3,2,1,0:T(4,128)S(1)} %pad_maximum_fusion.11), channel_id=1, source_target_pairs={{0,1},{1,2},{2,3},{3,4},{4,5},{5,6},{6,7},{7,8},{8,9},{9,10},{10,1... | collective-permute-start | bytes 368648 | tf_op jit(solution)/shard_map/ppermute | solution.py:143
  42.0 16.8 %collective-permute-start.7 = (f32[10,1,1,128]{3,2,1,0:T(1,128)S(1)}, f32[10,1,1,128]{3,2,1,0:T(1,128)S(1)}, u32[]{:S(2)}, u32[]{:S(2)}) collective-permute-start(f32[10,1,1,128]{3,2,1,0:T(1,128)S(1)} %get-tuple-element.13), channel_id=1, source_target_pairs={{0,767},{1,736},{2,737},{3,738},{4,739},{5,740},{6,741},{7,742},{8... | collective-permute-start | bytes 15368 | tf_op jit(solution)/shard_map/ppermute | solution.py:149
  51.9 6.7 %collective-permute-start.4 = (f32[10,8,3,128]{3,2,1,0:T(4,128)S(1)}, f32[10,8,3,128]{3,2,1,0:T(4,128)S(1)}, u32[]{:S(2)}, u32[]{:S(2)}) collective-permute-start(f32[10,8,3,128]{3,2,1,0:T(4,128)S(1)} %pad_maximum_fusion.12), channel_id=1, source_target_pairs={{0,31},{1,0},{2,1},{3,2},{4,3},{5,4},{6,5},{7,6},{8,7},{9,8},{10,9... | collective-permute-start | bytes 368648 | tf_op jit(solution)/shard_map/ppermute | solution.py:144
  55.8 3.2 %copy-start.1 = (f32[10,8,8,128]{3,2,1,0:T(8,128)S(1)}, f32[10,8,8,128]{3,2,1,0:T(8,128)}, u32[]{:S(2)}) copy-start(f32[10,8,8,128]{3,2,1,0:T(8,128)} %u_ref.1) | copy-start | bytes 983044
  59.9 0.7 copy-start.5
  62.1 1.0 %copy-start.2 = (f32[10,8,8,128]{3,2,1,0:T(8,128)S(1)}, f32[10,8,8,128]{3,2,1,0:T(8,128)}, u32[]{:S(2)}) copy-start(f32[10,8,8,128]{3,2,1,0:T(8,128)} %shard_map.86) | copy-start | bytes 983044

commit v2 on v1

--- a/solution.py
+++ b/solution.py
@@ -111,14 +111,6 @@
     return [(i, (i + step) % size) for i in range(size)]
 
 
-def diag_pairs(nx, ny, sx, sy):
-    return [
-        (i * ny + j, ((i + sx) % nx) * ny + (j + sy) % ny)
-        for i in range(nx)
-        for j in range(ny)
-    ]
-
-
 def laplace_parts(s, lo, hi):
     c = s[:, lo:hi, lo:hi]
     beside = s[:, lo - 1:hi - 1, lo:hi] + s[:, lo + 1:hi + 1, lo:hi]
@@ -134,47 +126,26 @@
     spread = diffusivity[:, None, None, None]
     cell_counts = jnp.broadcast_to(counts[:, :, None], (cx, cy, cz))
 
-    to_xp = jnp.concatenate([state[:, cx - 2:], source_in[:, cx - 1:]], 1)
-    to_xm = jnp.concatenate([state[:, :2], source_in[:, :1]], 1)
     to_yp = jnp.concatenate([state[:, :, cy - 2:], source_in[:, :, cy - 1:]], 2)
     to_ym = jnp.concatenate([state[:, :, :2], source_in[:, :, :1]], 2)
-    from_xm = lax.ppermute(to_xp, "gx", shift_pairs(nx, 1))
-    from_xp = lax.ppermute(to_xm, "gx", shift_pairs(nx, -1))
     from_ym = lax.ppermute(to_yp, "gy", shift_pairs(ny, 1))
     from_yp = lax.ppermute(to_ym, "gy", shift_pairs(ny, -1))
-    both = ("gx", "gy")
-    c_mm = lax.ppermute(state[:, cx - 1:, cy - 1:], both, diag_pairs(nx, ny, 1, 1))
-    c_mp = lax.ppermute(state[:, cx - 1:, :1], both, diag_pairs(nx, ny, 1, -1))
-    c_pm = lax.ppermute(state[:, :1, cy - 1:], both, diag_pairs(nx, ny, -1, 1))
-    c_pp = lax.ppermute(state[:, :1, :1], both, diag_pairs(nx, ny, -1, -1))
 
     early = chemistry(state, cell_counts, log_rate, activation, heat_release)
 
     def zeros(a, b):
         return jnp.zeros((rows, a, b, cz), jnp.float32)
 
-    s_xm, q_xm = from_xm[:, :2], from_xm[:, 2:]
-    s_xp, q_xp = from_xp[:, :2], from_xp[:, 2:]
-    s_ym, q_ym = from_ym[:, :, :2], from_ym[:, :, 2:]
-    s_yp, q_yp = from_yp[:, :, :2], from_yp[:, :, 2:]
-    ext = jnp.concatenate(
-        [
-            jnp.concatenate([zeros(1, 2), s_xm[:, :1], zeros(1, 2)], 2),
-            jnp.concatenate([zeros(1, 1), c_mm, s_xm[:, 1:], c_mp, zeros(1, 1)], 2),
-            jnp.concatenate([s_ym, state, s_yp], 2),
-            jnp.concatenate([zeros(1, 1), c_pm, s_xp[:, :1], c_pp, zeros(1, 1)], 2),
-            jnp.concatenate([zeros(1, 2), s_xp[:, 1:], zeros(1, 2)], 2),
-        ],
-        1,
+    wide = jnp.concatenate([from_ym[:, :, :2], state, from_yp[:, :, :2]], 2)
+    wide_src = jnp.concatenate(
+        [zeros(cx, 1), from_ym[:, :, 2:], source_in, from_yp[:, :, 2:], zeros(cx, 1)], 2
     )
-    src = jnp.concatenate(
-        [
-            jnp.concatenate([zeros(1, 1), q_xm, zeros(1, 1)], 2),
-            jnp.concatenate([q_ym, source_in, q_yp], 2),
-            jnp.concatenate([zeros(1, 1), q_xp, zeros(1, 1)], 2),
-        ],
-        1,
-    )
+    to_xp = jnp.concatenate([wide[:, cx - 2:], wide_src[:, cx - 1:]], 1)
+    to_xm = jnp.concatenate([wide[:, :2], wide_src[:, :1]], 1)
+    from_xm = lax.ppermute(to_xp, "gx", shift_pairs(nx, 1))
+    from_xp = lax.ppermute(to_xm, "gx", shift_pairs(nx, -1))
+    ext = jnp.concatenate([from_xm[:, :2], wide, from_xp[:, :2]], 1)
+    src = jnp.concatenate([from_xm[:, 2:], wide_src, from_xp[:, 2:]], 1)[:, :, 1:-1]
     first_ext = ext[:, 1:-1, 1:-1] + time_step * (
         spread * laplace_parts(ext, 1, cx + 3) + src
     )

time: 68.4 us -> 58 us (0.85)
  starting transfers between devices: 45.3 us -> 27.6 us
  waiting for transfers between devices: 5.47 us -> 12 us
  local copies, waits for them, and re-layouts: 6.06 us -> 7.24 us
    ppermute x4 -> x0, starting transfers between devices: 25 us -> none  [the longest x1 12.3 us: local(): c_mp = lax.ppermute(state[:, cx - 1:, :1], both, diag_pairs(nx, ny, 1, -1))]
    ppermute x1, waiting for transfers between devices: 0.72 us -> 9.78 us  [local(): from_xp = lax.ppermute(to_xm, 'gx', shift_pairs(nx, -1))]
    ppermute x1, starting transfers between devices: 3.86 us -> 9.24 us  [local(): from_yp = lax.ppermute(to_ym, 'gy', shift_pairs(ny, -1))]
    ppermute x1, starting transfers between devices: 2.3 us -> 4.03 us  [local(): from_ym = lax.ppermute(to_yp, 'gy', shift_pairs(ny, 1))]
    concatenate x2 -> x1, local copies, waits for them, and re-layouts: 0.33 us -> 1.66 us  [local(): jnp.concatenate([zeros(cx, 1), from_ym[:, :, 2:], source_in, from_yp[:, :...]
    ppermute x1, waiting for transfers between devices: 1.99 us -> 0.68 us  [local(): from_ym = lax.ppermute(to_yp, 'gy', shift_pairs(ny, 1))]
    ppermute x1, waiting for transfers between devices: 2.75 us -> 1.51 us  [local(): from_yp = lax.ppermute(to_ym, 'gy', shift_pairs(ny, -1))]
    slice x2, local copies, waits for them, and re-layouts: 0.1 us -> 1.23 us  [local(): to_yp = jnp.concatenate([state[:, :, cy - 2:], source_in[:, :, cy - 1:]], 2)]
  transfers between devices with their start and end apart: 8 -> 4, of which waited for: 3 -> 3; matrix products, arithmetic and copies ran while one was open for 2% -> 1% of each run, Pallas kernels for 5% -> 6%
where the time goes in v2:
time: 58 us; the launch traced here: 57.6 us
  starting transfers between devices  27.6 us (48%)
  waiting for transfers between devices  12 us (21%)
  local copies, waits for them, and re-layouts  7.24 us (12%)
  Pallas kernels  7.22 us (12%)
  other arithmetic  2.74 us (5%)
  between operations  0.88 us (2%)
    ppermute x1, starting transfers between devices, local(): from_xm = lax.ppermute(to_xp, 'gx', shift_pairs(nx, 1))  12.4 us
    ppermute x1, waiting for transfers between devices, local(): from_xp = lax.ppermute(to_xm, 'gx', shift_pairs(nx, -1))  9.78 us
    ppermute x1, starting transfers between devices, local(): from_yp = lax.ppermute(to_ym, 'gy', shift_pairs(ny, -1))  9.24 us
    pallas_call x2, Pallas kernels, chemistry(): pl.pallas_call(chem_kernel, out_shape=jax.ShapeDtypeStruct(fields.shape,...  7.22 us
    ppermute x1, starting transfers between devices, local(): from_ym = lax.ppermute(to_yp, 'gy', shift_pairs(ny, 1))  4.03 us
    ppermute x1, starting transfers between devices, local(): from_xp = lax.ppermute(to_xm, 'gx', shift_pairs(nx, -1))  1.92 us
    unnamed x14, local copies, waits for them, and re-layouts  1.7 us
    concatenate x1, local copies, waits for them, and re-layouts, local(): jnp.concatenate([zeros(cx, 1), from_ym[:, :, 2:], source_in, from_yp[:, :...  1.66 us
  transfers between devices with their start and end apart: 4, of which 3 were waited for; matrix products, arithmetic and copies ran while one was open for 1% of the time, Pallas kernels for 6%

profile of v2, /device:TPU:1, one launch (start us, length us, event | category | flops | bytes accessed | tf_op | source)
XLA Modules:
  0.0 57.6 jit_solution(7536978711090132851)
XLA Ops:
  0.6 0.0 copy-start.3
  0.6 1.2 %fusion.25 = (f32[10,8,2,128]{3,2,1,0:T(2,128)S(1)}, f32[10,8,2,128]{3,2,1,0:T(2,128)S(1)}) fusion(f32[10,8,8,128]{3,2,1,0:T(8,128)} %u_ref.1), kind=kLoop, calls=%fused_computation.46 | loop fusion | bytes 327680 | tf_op jit(solution)/shard_map/slice | solution.py:129
  1.8 0.0 copy-done.3
  1.8 0.1 fusion.26
  1.9 0.1 pad_maximum_fusion.11
  2.0 4.0 %collective-permute-start = (f32[10,8,3,128]{3,2,1,0:T(4,128)S(1)}, f32[10,8,3,128]{3,2,1,0:T(4,128)S(1)}, u32[]{:S(2)}, u32[]{:S(2)}) collective-permute-start(f32[10,8,3,128]{3,2,1,0:T(4,128)S(1)} %pad_maximum_fusion.11), channel_id=1, source_target_pairs={{0,1},{1,2},{2,3},{3,4},{4,5},{5,6},{6,7},{7,8},{8,9},{9,10},{10,1... | collective-permute-start | bytes 368648 | tf_op jit(solution)/shard_map/ppermute | solution.py:131
  6.0 0.1 pad_maximum_fusion.12
  6.1 9.2 %collective-permute-start.1 = (f32[10,8,3,128]{3,2,1,0:T(4,128)S(1)}, f32[10,8,3,128]{3,2,1,0:T(4,128)S(1)}, u32[]{:S(2)}, u32[]{:S(2)}) collective-permute-start(f32[10,8,3,128]{3,2,1,0:T(4,128)S(1)} %pad_maximum_fusion.12), channel_id=1, source_target_pairs={{0,31},{1,0},{2,1},{3,2},{4,3},{5,4},{6,5},{7,6},{8,7},{9,8},{10,9... | collective-permute-start | bytes 368648 | tf_op jit(solution)/shard_map/ppermute | solution.py:132
  15.4 0.7 %collective-permute-done = f32[10,8,3,128]{3,2,1,0:T(4,128)S(1)} collective-permute-done((f32[10,8,3,128]{3,2,1,0:T(4,128)S(1)}, f32[10,8,3,128]{3,2,1,0:T(4,128)S(1)}, u32[]{:S(2)}, u32[]{:S(2)}) %collective-permute-start) | collective-permute-done | bytes 122912 | tf_op jit(solution)/shard_map/ppermute | solution.py:131
  16.1 1.5 %collective-permute-done.1 = f32[10,8,3,128]{3,2,1,0:T(4,128)S(1)} collective-permute-done((f32[10,8,3,128]{3,2,1,0:T(4,128)S(1)}, f32[10,8,3,128]{3,2,1,0:T(4,128)S(1)}, u32[]{:S(2)}, u32[]{:S(2)}) %collective-permute-start.1) | collective-permute-done | bytes 122912 | tf_op jit(solution)/shard_map/ppermute | solution.py:132
  17.7 1.7 %concatenate.49 = f32[10,8,12,128]{3,2,1,0:T(8,128)S(1)} concatenate(f32[10,8,1,128]{3,2,1,0:T(1,128)S(1)} %broadcast.8, f32[10,8,1,128]{3,2,1,0:T(1,128)S(1)} %slice.162, f32[10,8,8,128]{3,2,1,0:T(8,128)S(1)} %copy-done.3, f32[10,8,1,128]{3,2,1,0:T(1,128)S(1)} %slice.163, f32[10,8,1,128]{3,2,1,0:T(1,128)S(1)} %broadcast.8), dimensions={2} | concatenate | bytes 983040 | tf_op jit(solution)/shard_map/concatenate | solution.py:140
  19.3 0.0 copy-start
  19.4 0.9 %copy-done = f32[10,8,8,128]{3,2,1,0:T(8,128)S(1)} copy-done((f32[10,8,8,128]{3,2,1,0:T(8,128)S(1)}, f32[10,8,8,128]{3,2,1,0:T(8,128)}, u32[]{:S(2)}) %copy-start) | copy-done | bytes 327704
  20.3 0.0 copy-start.5
  20.3 0.1 fusion.18
  20.4 12.4 %collective-permute-start.2 = (f32[10,3,12,128]{3,2,1,0:T(8,128)S(1)}, f32[10,3,12,128]{3,2,1,0:T(8,128)S(1)}, u32[]{:S(2)}, u32[]{:S(2)}) collective-permute-start(f32[10,3,12,128]{3,2,1,0:T(8,128)S(1)} %get-tuple-element.14), channel_id=1, source_target_pairs={{0,32},{32,64},{64,96},{96,128},{128,160},{160,192},{192,224},{224... | collective-permute-start | bytes 552968 | tf_op jit(solution)/shard_map/ppermute | solution.py:145
  32.8 1.9 %collective-permute-start.3 = (f32[10,3,12,128]{3,2,1,0:T(8,128)S(1)}, f32[10,3,12,128]{3,2,1,0:T(8,128)S(1)}, u32[]{:S(2)}, u32[]{:S(2)}) collective-permute-start(f32[10,3,12,128]{3,2,1,0:T(8,128)S(1)} %get-tuple-element.15), channel_id=1, source_target_pairs={{0,736},{32,0},{64,32},{96,64},{128,96},{160,128},{192,160},{224,1... | collective-permute-start | bytes 552968 | tf_op jit(solution)/shard_map/ppermute | solution.py:146
  34.7 0.0 copy-done.5
  34.7 0.7 %broadcast_in_dim.2.cnt_ref = s32[8,8,128]{2,1,0:T(8,128)} broadcast(s32[8,8]{1,0:T(8,128)S(1)} %copy-done.5), dimensions={0,1} | broadcast | bytes 33024 | tf_op jit(solution)/shard_map/broadcast_in_dim | solution.py:127
  35.4 3.6 %shard_map.86 = f32[10,8,8,128]{3,2,1,0:T(8,128)} custom-call(f32[21]{0:T(128)} %rate_ref.3, f32[21]{0:T(128)} %act_ref.3, f32[21]{0:T(128)} %heat_ref.3, f32[10,8,8,128]{3,2,1,0:T(8,128)} %u_ref.1, s32[8,8,128]{2,1,0:T(8,128)} %broadcast_in_dim.2.cnt_ref), custom_call_target="tpu_custom_call" | custom-call | tf_op jit(solution)/shard_map/pallas_call | solution.py:102
  39.0 0.0 copy-start.1
  39.0 0.0 collective-permute-done.2
  39.0 0.0 copy-start.4
  39.0 9.8 %collective-permute-done.3 = f32[10,3,12,128]{3,2,1,0:T(8,128)S(1)} collective-permute-done((f32[10,3,12,128]{3,2,1,0:T(8,128)S(1)}, f32[10,3,12,128]{3,2,1,0:T(8,128)S(1)}, u32[]{:S(2)}, u32[]{:S(2)}) %collective-permute-start.3) | collective-permute-done | bytes 184352 | tf_op jit(solution)/shard_map/ppermute | solution.py:146
  48.8 0.0 copy-done.1
  48.8 0.2 pad_maximum_fusion
  49.0 0.3 fusion.19
  49.3 0.3 fusion.20
  49.6 0.0 copy-done.4
  49.6 0.0 slice-start
  49.7 0.0 copy-start.6
  49.7 0.9 %slice-done = f32[10,1,12,128]{3,2,1,0:T(8,128)S(1)} async-done(((f32[10,3,12,128]{3,2,1,0:T(8,128)}), f32[10,1,12,128]{3,2,1,0:T(8,128)S(1)}, s32[]{:S(2)}) %slice-start) | async-done | bytes 61464 | tf_op jit(solution)/shard_map/slice | solution.py:148
  50.5 0.0 copy-done.6
  50.5 1.1 %fusion.2 = f32[10,10,10,128]{3,2,1,0:T(8,128)S(1)} fusion(f32[10,1,12,128]{3,2,1,0:T(8,128)S(1)} %slice.176, f32[10,8,12,128]{3,2,1,0:T(8,128)S(1)} %concatenate.49, f32[10,1,12,128]{3,2,1,0:T(8,128)S(1)} %slice-done, f32[10,12,12,128]{3,2,1,0:T(8,128)S(1)} %pad_maximum_fusion, f32[10,2,12,128]{3,2,1,0:T(8,128)S(1)} %slice.167, ...), kind=kLoop, calls=%fused_computation.4 | loop fusion | flops 2688000 | bytes 4423720 | tf_op jit(solution)/shard_map/add | solution.py:149
  51.6 0.2 fusion.23
  51.8 0.0 copy-start.2
  51.8 0.2 fusion.22
  52.0 0.8 %copy-done.2 = f32[10,8,8,128]{3,2,1,0:T(8,128)S(1)} copy-done((f32[10,8,8,128]{3,2,1,0:T(8,128)S(1)}, f32[10,8,8,128]{3,2,1,0:T(8,128)}, u32[]{:S(2)}) %copy-start.2) | copy-done | bytes 327704
  52.8 1.2 %fusion.21 = (f32[10,8,8,128]{3,2,1,0:T(8,128)}, f32[10,8,8,128]{3,2,1,0:T(8,128)}) fusion(f32[10,10,10,128]{3,2,1,0:T(8,128)S(1)} %fusion.2, f32[10,8,8,128]{3,2,1,0:T(8,128)S(1)} %copy-done.1, f32[10,8,8,128]{3,2,1,0:T(8,128)S(1)} %copy-done.2, f32[10,8,8,1]{3,2,1,0:T(8,128)S(1)} %get-tuple-element.10, f32[10,8,8,127]{3,2,1,0:T(8,128)S(1)} %get-tuple-element.8, ...), kind=kLoop, calls=%fused_computation.42 | loop fusion | flops 1228800 | bytes 3604520 | tf_op jit(solution)/shard_map/slice | solution.py:152
  54.0 3.6 %shard_map.87 = f32[10,8,8,128]{3,2,1,0:T(8,128)} custom-call(f32[21]{0:T(128)} %rate_ref.3, f32[21]{0:T(128)} %act_ref.3, f32[21]{0:T(128)} %heat_ref.3, f32[10,8,8,128]{3,2,1,0:T(8,128)} %get-tuple-element.6.u_ref, s32[8,8,128]{2,1,0:T(8,128)} %broadcast_in_dim.2.cnt_ref), custom_call_target="tpu_custom_call" | custom-call | tf_op jit(solution)/shard_map/pallas_call | solution.py:102
  (9 shorter events, 0.2 us)
Async XLA Ops:
  0.6 1.2 %copy-start.3 = (f32[10,8,8,128]{3,2,1,0:T(8,128)S(1)}, f32[10,8,8,128]{3,2,1,0:T(8,128)}, u32[]{:S(2)}) copy-start(f32[10,8,8,128]{3,2,1,0:T(8,128)} %param.8) | copy-start | bytes 983044
  2.0 14.1 %collective-permute-start = (f32[10,8,3,128]{3,2,1,0:T(4,128)S(1)}, f32[10,8,3,128]{3,2,1,0:T(4,128)S(1)}, u32[]{:S(2)}, u32[]{:S(2)}) collective-permute-start(f32[10,8,3,128]{3,2,1,0:T(4,128)S(1)} %pad_maximum_fusion.11), channel_id=1, source_target_pairs={{0,1},{1,2},{2,3},{3,4},{4,5},{5,6},{6,7},{7,8},{8,9},{9,10},{10,1... | collective-permute-start | bytes 368648 | tf_op jit(solution)/shard_map/ppermute | solution.py:131
  6.1 11.5 %collective-permute-start.1 = (f32[10,8,3,128]{3,2,1,0:T(4,128)S(1)}, f32[10,8,3,128]{3,2,1,0:T(4,128)S(1)}, u32[]{:S(2)}, u32[]{:S(2)}) collective-permute-start(f32[10,8,3,128]{3,2,1,0:T(4,128)S(1)} %pad_maximum_fusion.12), channel_id=1, source_target_pairs={{0,31},{1,0},{2,1},{3,2},{4,3},{5,4},{6,5},{7,6},{8,7},{9,8},{10,9... | collective-permute-start | bytes 368648 | tf_op jit(solution)/shard_map/ppermute | solution.py:132
  19.3 1.0 %copy-start = (f32[10,8,8,128]{3,2,1,0:T(8,128)S(1)}, f32[10,8,8,128]{3,2,1,0:T(8,128)}, u32[]{:S(2)}) copy-start(f32[10,8,8,128]{3,2,1,0:T(8,128)} %u_ref.1) | copy-start | bytes 983044
  20.3 14.4 %copy-start.5 = (s32[8,8]{1,0:T(8,128)S(1)}, s32[8,8]{1,0:T(8,128)}, u32[]{:S(2)}) copy-start(s32[8,8]{1,0:T(8,128)} %param.9) | copy-start | bytes 772
  20.4 18.6 %collective-permute-start.2 = (f32[10,3,12,128]{3,2,1,0:T(8,128)S(1)}, f32[10,3,12,128]{3,2,1,0:T(8,128)S(1)}, u32[]{:S(2)}, u32[]{:S(2)}) collective-permute-start(f32[10,3,12,128]{3,2,1,0:T(8,128)S(1)} %get-tuple-element.14), channel_id=1, source_target_pairs={{0,32},{32,64},{64,96},{96,128},{128,160},{160,192},{192,224},{224... | collective-permute-start | bytes 552968 | tf_op jit(solution)/shard_map/ppermute | solution.py:145
  32.8 16.0 %collective-permute-start.3 = (f32[10,3,12,128]{3,2,1,0:T(8,128)S(1)}, f32[10,3,12,128]{3,2,1,0:T(8,128)S(1)}, u32[]{:S(2)}, u32[]{:S(2)}) collective-permute-start(f32[10,3,12,128]{3,2,1,0:T(8,128)S(1)} %get-tuple-element.15), channel_id=1, source_target_pairs={{0,736},{32,0},{64,32},{96,64},{128,96},{160,128},{192,160},{224,1... | collective-permute-start | bytes 552968 | tf_op jit(solution)/shard_map/ppermute | solution.py:146
  39.0 9.8 %copy-start.1 = (f32[10,8,8,128]{3,2,1,0:T(8,128)S(1)}, f32[10,8,8,128]{3,2,1,0:T(8,128)}, u32[]{:S(2)}) copy-start(f32[10,8,8,128]{3,2,1,0:T(8,128)} %u_ref.1) | copy-start | bytes 983044
  39.0 10.6 %copy-start.4 = (f32[10,3,12,128]{3,2,1,0:T(8,128)}, f32[10,3,12,128]{3,2,1,0:T(8,128)S(1)}, u32[]{:S(2)}) copy-start(f32[10,3,12,128]{3,2,1,0:T(8,128)S(1)} %collective-permute-done.2) | copy-start | bytes 552964
  49.6 0.9 %slice-start = ((f32[10,3,12,128]{3,2,1,0:T(8,128)}), f32[10,1,12,128]{3,2,1,0:T(8,128)S(1)}, s32[]{:S(2)}) async-start(f32[10,3,12,128]{3,2,1,0:T(8,128)} %copy-done.4), calls=%async_computation | async-start | bytes 163840 | tf_op jit(solution)/shard_map/slice | solution.py:148
  49.7 0.9 %copy-start.6 = (f32[10]{0:T(128)S(1)}, f32[10]{0:T(128)}, u32[]{:S(2)}) copy-start(f32[10]{0:T(128)} %param.10) | copy-start | bytes 124
  51.8 1.0 %copy-start.2 = (f32[10,8,8,128]{3,2,1,0:T(8,128)S(1)}, f32[10,8,8,128]{3,2,1,0:T(8,128)}, u32[]{:S(2)}) copy-start(f32[10,8,8,128]{3,2,1,0:T(8,128)} %shard_map.86) | copy-start | bytes 983044

commit v3 on v2

--- a/solution.py
+++ b/solution.py
@@ -111,6 +111,19 @@
     return [(i, (i + step) % size) for i in range(size)]
 
 
+def exchange(to_lo, to_hi, axis, size):
+    if size % 2:
+        from_lo = lax.ppermute(to_hi, axis, shift_pairs(size, 1))
+        from_hi = lax.ppermute(to_lo, axis, shift_pairs(size, -1))
+        return from_lo, from_hi
+    even = lax.axis_index(axis) % 2 == 0
+    inner = [(i, i + 1 if i % 2 == 0 else i - 1) for i in range(size)]
+    outer = [(i, (i - 1) % size if i % 2 == 0 else (i + 1) % size) for i in range(size)]
+    first = lax.ppermute(jnp.where(even, to_hi, to_lo), axis, inner)
+    second = lax.ppermute(jnp.where(even, to_lo, to_hi), axis, outer)
+    return jnp.where(even, second, first), jnp.where(even, first, second)
+
+
 def laplace_parts(s, lo, hi):
     c = s[:, lo:hi, lo:hi]
     beside = s[:, lo - 1:hi - 1, lo:hi] + s[:, lo + 1:hi + 1, lo:hi]
@@ -128,8 +141,7 @@
 
     to_yp = jnp.concatenate([state[:, :, cy - 2:], source_in[:, :, cy - 1:]], 2)
     to_ym = jnp.concatenate([state[:, :, :2], source_in[:, :, :1]], 2)
-    from_ym = lax.ppermute(to_yp, "gy", shift_pairs(ny, 1))
-    from_yp = lax.ppermute(to_ym, "gy", shift_pairs(ny, -1))
+    from_ym, from_yp = exchange(to_ym, to_yp, "gy", ny)
 
     early = chemistry(state, cell_counts, log_rate, activation, heat_release)
 
@@ -142,8 +154,7 @@
     )
     to_xp = jnp.concatenate([wide[:, cx - 2:], wide_src[:, cx - 1:]], 1)
     to_xm = jnp.concatenate([wide[:, :2], wide_src[:, :1]], 1)
-    from_xm = lax.ppermute(to_xp, "gx", shift_pairs(nx, 1))
-    from_xp = lax.ppermute(to_xm, "gx", shift_pairs(nx, -1))
+    from_xm, from_xp = exchange(to_xm, to_xp, "gx", nx)
     ext = jnp.concatenate([from_xm[:, :2], wide, from_xp[:, :2]], 1)
     src = jnp.concatenate([from_xm[:, 2:], wide_src, from_xp[:, 2:]], 1)[:, :, 1:-1]
     first_ext = ext[:, 1:-1, 1:-1] + time_step * (

time: 58 us -> 54.1 us (0.933)
  the two profiles are of different devices: /device:TPU:1 before, /device:TPU:16 now
where the time goes in v3:
time: 54.1 us; the launch traced here: 53.7 us
  starting transfers between devices  25.4 us (47%)
  waiting for transfers between devices  9.27 us (17%)
  local copies, waits for them, and re-layouts  8.03 us (15%)
  Pallas kernels  7.22 us (13%)
  other arithmetic  2.83 us (5%)
  between operations  0.92 us (2%)
    ppermute x2, starting transfers between devices, exchange(): second = lax.ppermute(jnp.where(even, to_lo, to_hi), axis, outer)  17.7 us
    ppermute x2, starting transfers between devices, exchange(): first = lax.ppermute(jnp.where(even, to_hi, to_lo), axis, inner)  7.74 us
    pallas_call x2, Pallas kernels, chemistry(): pl.pallas_call(chem_kernel, out_shape=jax.ShapeDtypeStruct(fields.shape,...  7.22 us
    ppermute x2, waiting for transfers between devices, exchange(): second = lax.ppermute(jnp.where(even, to_lo, to_hi), axis, outer)  5.4 us
    ppermute x2, waiting for transfers between devices, exchange(): first = lax.ppermute(jnp.where(even, to_hi, to_lo), axis, inner)  3.88 us
    unnamed x12, local copies, waits for them, and re-layouts  3.34 us
    concatenate x1, local copies, waits for them, and re-layouts, local(): jnp.concatenate([zeros(cx, 1), from_ym[:, :, 2:], source_in, from_yp[:, :...  1.66 us
    slice x2, local copies, waits for them, and re-layouts, local(): to_ym = jnp.concatenate([state[:, :, :2], source_in[:, :, :1]], 2)  1.23 us
  transfers between devices with their start and end apart: 4, of which 2 were waited for; matrix products, arithmetic and copies ran while one was open for 1% of the time, Pallas kernels for 7%

profile of v3, /device:TPU:16, one launch (start us, length us, event | category | flops | bytes accessed | tf_op | source)
XLA Modules:
  0.0 53.7 jit_solution(5688584023641523248)
XLA Ops:
  0.6 0.0 copy-start.3
  0.7 1.2 %fusion.27 = (f32[10,8,2,128]{3,2,1,0:T(2,128)S(1)}, f32[10,8,2,128]{3,2,1,0:T(2,128)S(1)}) fusion(f32[10,8,8,128]{3,2,1,0:T(8,128)} %u_ref.1), kind=kLoop, calls=%fused_computation.54 | loop fusion | bytes 327680 | tf_op jit(solution)/shard_map/slice | solution.py:143
  1.8 0.0 copy-done.3
  1.8 0.1 fusion.28
  1.9 0.2 fusion.19
  2.1 2.4 %collective-permute-start = (f32[10,8,3,128]{3,2,1,0:T(4,128)S(1)}, f32[10,8,3,128]{3,2,1,0:T(4,128)S(1)}, u32[]{:S(2)}, u32[]{:S(2)}) collective-permute-start(f32[10,8,3,128]{3,2,1,0:T(4,128)S(1)} %get-tuple-element.25), channel_id=1, source_target_pairs={{0,31},{1,2},{2,1},{3,4},{4,3},{5,6},{6,5},{7,8},{8,7},{9,10},{10,... | collective-permute-start | bytes 368648 | tf_op jit(solution)/shard_map/ppermute | solution.py:123
  4.4 5.8 %collective-permute-start.1 = (f32[10,8,3,128]{3,2,1,0:T(4,128)S(1)}, f32[10,8,3,128]{3,2,1,0:T(4,128)S(1)}, u32[]{:S(2)}, u32[]{:S(2)}) collective-permute-start(f32[10,8,3,128]{3,2,1,0:T(4,128)S(1)} %get-tuple-element.24), channel_id=1, source_target_pairs={{0,1},{1,0},{2,3},{3,2},{4,5},{5,4},{6,7},{7,6},{8,9},{9,8},{10,11... | collective-permute-start | bytes 368648 | tf_op jit(solution)/shard_map/ppermute | solution.py:122
  10.3 0.0 collective-permute-done
  10.3 3.9 %collective-permute-done.1 = f32[10,8,3,128]{3,2,1,0:T(4,128)S(1)} collective-permute-done((f32[10,8,3,128]{3,2,1,0:T(4,128)S(1)}, f32[10,8,3,128]{3,2,1,0:T(4,128)S(1)}, u32[]{:S(2)}, u32[]{:S(2)}) %collective-permute-start.1) | collective-permute-done | bytes 122912 | tf_op jit(solution)/shard_map/ppermute | solution.py:122
  14.2 0.1 broadcast_select_fusion.4
  14.4 1.7 %concatenate.49 = f32[10,8,12,128]{3,2,1,0:T(8,128)S(1)} concatenate(f32[10,8,1,128]{3,2,1,0:T(1,128)S(1)} %broadcast.10, f32[10,8,1,128]{3,2,1,0:T(1,128)S(1)} %slice.162, f32[10,8,8,128]{3,2,1,0:T(8,128)S(1)} %copy-done.3, f32[10,8,1,128]{3,2,1,0:T(1,128)S(1)} %slice.163, f32[10,8,1,128]{3,2,1,0:T(1,128)S(1)} %broadcast.10), dimensions={2} | concatenate | bytes 983040 | tf_op jit(solution)/shard_map/concatenate | solution.py:152
  16.1 0.0 copy-start
  16.1 0.9 %copy-done = f32[10,8,8,128]{3,2,1,0:T(8,128)S(1)} copy-done((f32[10,8,8,128]{3,2,1,0:T(8,128)S(1)}, f32[10,8,8,128]{3,2,1,0:T(8,128)}, u32[]{:S(2)}) %copy-start) | copy-done | bytes 327704
  17.1 0.0 copy-start.4
  17.1 0.1 broadcast_select_fusion.3
  17.2 15.3 %collective-permute-start.2 = (f32[10,3,12,128]{3,2,1,0:T(8,128)S(1)}, f32[10,3,12,128]{3,2,1,0:T(8,128)S(1)}, u32[]{:S(2)}, u32[]{:S(2)}) collective-permute-start(f32[10,3,12,128]{3,2,1,0:T(8,128)S(1)} %get-tuple-element.12), channel_id=1, source_target_pairs={{0,736},{32,64},{64,32},{96,128},{128,96},{160,192},{192,160},{224... | collective-permute-start | bytes 552968 | tf_op jit(solution)/shard_map/ppermute | solution.py:123
  32.5 1.9 %collective-permute-start.3 = (f32[10,3,12,128]{3,2,1,0:T(8,128)S(1)}, f32[10,3,12,128]{3,2,1,0:T(8,128)S(1)}, u32[]{:S(2)}, u32[]{:S(2)}) collective-permute-start(f32[10,3,12,128]{3,2,1,0:T(8,128)S(1)} %get-tuple-element.13), channel_id=1, source_target_pairs={{0,32},{32,0},{64,96},{96,64},{128,160},{160,128},{192,224},{224,1... | collective-permute-start | bytes 552968 | tf_op jit(solution)/shard_map/ppermute | solution.py:122
  34.4 0.0 copy-done.4
  34.4 0.7 %broadcast_in_dim.2.cnt_ref = s32[8,8,128]{2,1,0:T(8,128)} broadcast(s32[8,8]{1,0:T(8,128)S(1)} %copy-done.4), dimensions={0,1} | broadcast | bytes 33024 | tf_op jit(solution)/shard_map/broadcast_in_dim | solution.py:140
  35.1 3.6 %shard_map.86 = f32[10,8,8,128]{3,2,1,0:T(8,128)} custom-call(f32[21]{0:T(128)} %rate_ref.3, f32[21]{0:T(128)} %act_ref.3, f32[21]{0:T(128)} %heat_ref.3, f32[10,8,8,128]{3,2,1,0:T(8,128)} %u_ref.1, s32[8,8,128]{2,1,0:T(8,128)} %broadcast_in_dim.2.cnt_ref), custom_call_target="tpu_custom_call" | custom-call | tf_op jit(solution)/shard_map/pallas_call | solution.py:102
  38.7 5.4 %collective-permute-done.2 = f32[10,3,12,128]{3,2,1,0:T(8,128)S(1)} collective-permute-done((f32[10,3,12,128]{3,2,1,0:T(8,128)S(1)}, f32[10,3,12,128]{3,2,1,0:T(8,128)S(1)}, u32[]{:S(2)}, u32[]{:S(2)}) %collective-permute-start.2) | collective-permute-done | bytes 184352 | tf_op jit(solution)/shard_map/ppermute | solution.py:123
  44.1 0.0 collective-permute-done.3
  44.2 0.0 copy-start.1
  44.2 0.9 %copy-done.1 = f32[10,8,8,128]{3,2,1,0:T(8,128)S(1)} copy-done((f32[10,8,8,128]{3,2,1,0:T(8,128)S(1)}, f32[10,8,8,128]{3,2,1,0:T(8,128)}, u32[]{:S(2)}) %copy-start.1) | copy-done | bytes 327704
  45.1 0.1 pad_maximum_fusion
  45.3 0.3 fusion.21
  45.6 0.3 fusion.22
  45.9 0.0 copy-start.5
  45.9 0.6 %copy-done.5 = f32[10]{0:T(128)S(1)} copy-done((f32[10]{0:T(128)S(1)}, f32[10]{0:T(128)}, u32[]{:S(2)}) %copy-start.5) | copy-done | bytes 64
  46.6 1.1 %fusion.2 = f32[10,10,10,128]{3,2,1,0:T(8,128)S(1)} fusion(f32[10,1,12,128]{3,2,1,0:T(8,128)S(1)} %slice.176, f32[10,8,12,128]{3,2,1,0:T(8,128)S(1)} %concatenate.49, f32[10,1,12,128]{3,2,1,0:T(8,128)S(1)} %slice.175, f32[10,12,12,128]{3,2,1,0:T(8,128)S(1)} %pad_maximum_fusion, f32[10,2,12,128]{3,2,1,0:T(8,128)S(1)} %slice.167, ...), kind=kLoop, calls=%fused_computation.4 | loop fusion | flops 2688000 | bytes 4423720 | tf_op jit(solution)/shard_map/add | solution.py:160
  47.7 0.2 fusion.25
  47.9 0.0 copy-start.2
  47.9 0.2 fusion.24
  48.1 0.8 %copy-done.2 = f32[10,8,8,128]{3,2,1,0:T(8,128)S(1)} copy-done((f32[10,8,8,128]{3,2,1,0:T(8,128)S(1)}, f32[10,8,8,128]{3,2,1,0:T(8,128)}, u32[]{:S(2)}) %copy-start.2) | copy-done | bytes 327704
  48.9 1.2 %fusion.23 = (f32[10,8,8,128]{3,2,1,0:T(8,128)}, f32[10,8,8,128]{3,2,1,0:T(8,128)}) fusion(f32[10,10,10,128]{3,2,1,0:T(8,128)S(1)} %fusion.2, f32[10,8,8,128]{3,2,1,0:T(8,128)S(1)} %copy-done.1, f32[10,8,8,128]{3,2,1,0:T(8,128)S(1)} %copy-done.2, f32[10,8,8,1]{3,2,1,0:T(8,128)S(1)} %get-tuple-element.10, f32[10,8,8,127]{3,2,1,0:T(8,128)S(1)} %get-tuple-element.8, ...), kind=kLoop, calls=%fused_computation.50 | loop fusion | flops 1228800 | bytes 3604520 | tf_op jit(solution)/shard_map/slice | solution.py:163
  50.1 3.6 %shard_map.87 = f32[10,8,8,128]{3,2,1,0:T(8,128)} custom-call(f32[21]{0:T(128)} %rate_ref.3, f32[21]{0:T(128)} %act_ref.3, f32[21]{0:T(128)} %heat_ref.3, f32[10,8,8,128]{3,2,1,0:T(8,128)} %get-tuple-element.6.u_ref, s32[8,8,128]{2,1,0:T(8,128)} %broadcast_in_dim.2.cnt_ref), custom_call_target="tpu_custom_call" | custom-call | tf_op jit(solution)/shard_map/pallas_call | solution.py:102
  (11 shorter events, 0.3 us)
Async XLA Ops:
  0.6 1.2 %copy-start.3 = (f32[10,8,8,128]{3,2,1,0:T(8,128)S(1)}, f32[10,8,8,128]{3,2,1,0:T(8,128)}, u32[]{:S(2)}) copy-start(f32[10,8,8,128]{3,2,1,0:T(8,128)} %param.8) | copy-start | bytes 983044
  2.1 8.2 %collective-permute-start = (f32[10,8,3,128]{3,2,1,0:T(4,128)S(1)}, f32[10,8,3,128]{3,2,1,0:T(4,128)S(1)}, u32[]{:S(2)}, u32[]{:S(2)}) collective-permute-start(f32[10,8,3,128]{3,2,1,0:T(4,128)S(1)} %get-tuple-element.25), channel_id=1, source_target_pairs={{0,31},{1,2},{2,1},{3,4},{4,3},{5,6},{6,5},{7,8},{8,7},{9,10},{10,... | collective-permute-start | bytes 368648 | tf_op jit(solution)/shard_map/ppermute | solution.py:123
  4.4 9.7 %collective-permute-start.1 = (f32[10,8,3,128]{3,2,1,0:T(4,128)S(1)}, f32[10,8,3,128]{3,2,1,0:T(4,128)S(1)}, u32[]{:S(2)}, u32[]{:S(2)}) collective-permute-start(f32[10,8,3,128]{3,2,1,0:T(4,128)S(1)} %get-tuple-element.24), channel_id=1, source_target_pairs={{0,1},{1,0},{2,3},{3,2},{4,5},{5,4},{6,7},{7,6},{8,9},{9,8},{10,11... | collective-permute-start | bytes 368648 | tf_op jit(solution)/shard_map/ppermute | solution.py:122
  16.1 1.0 %copy-start = (f32[10,8,8,128]{3,2,1,0:T(8,128)S(1)}, f32[10,8,8,128]{3,2,1,0:T(8,128)}, u32[]{:S(2)}) copy-start(f32[10,8,8,128]{3,2,1,0:T(8,128)} %u_ref.1) | copy-start | bytes 983044
  17.1 17.3 %copy-start.4 = (s32[8,8]{1,0:T(8,128)S(1)}, s32[8,8]{1,0:T(8,128)}, u32[]{:S(2)}) copy-start(s32[8,8]{1,0:T(8,128)} %param.9) | copy-start | bytes 772
  17.2 27.0 %collective-permute-start.2 = (f32[10,3,12,128]{3,2,1,0:T(8,128)S(1)}, f32[10,3,12,128]{3,2,1,0:T(8,128)S(1)}, u32[]{:S(2)}, u32[]{:S(2)}) collective-permute-start(f32[10,3,12,128]{3,2,1,0:T(8,128)S(1)} %get-tuple-element.12), channel_id=1, source_target_pairs={{0,736},{32,64},{64,32},{96,128},{128,96},{160,192},{192,160},{224... | collective-permute-start | bytes 552968 | tf_op jit(solution)/shard_map/ppermute | solution.py:123
  32.5 11.6 %collective-permute-start.3 = (f32[10,3,12,128]{3,2,1,0:T(8,128)S(1)}, f32[10,3,12,128]{3,2,1,0:T(8,128)S(1)}, u32[]{:S(2)}, u32[]{:S(2)}) collective-permute-start(f32[10,3,12,128]{3,2,1,0:T(8,128)S(1)} %get-tuple-element.13), channel_id=1, source_target_pairs={{0,32},{32,0},{64,96},{96,64},{128,160},{160,128},{192,224},{224,1... | collective-permute-start | bytes 552968 | tf_op jit(solution)/shard_map/ppermute | solution.py:122
  44.2 1.0 %copy-start.1 = (f32[10,8,8,128]{3,2,1,0:T(8,128)S(1)}, f32[10,8,8,128]{3,2,1,0:T(8,128)}, u32[]{:S(2)}) copy-start(f32[10,8,8,128]{3,2,1,0:T(8,128)} %u_ref.1) | copy-start | bytes 983044
  45.9 0.7 %copy-start.5 = (f32[10]{0:T(128)S(1)}, f32[10]{0:T(128)}, u32[]{:S(2)}) copy-start(f32[10]{0:T(128)} %param.10) | copy-start | bytes 124
  47.9 1.0 %copy-start.2 = (f32[10,8,8,128]{3,2,1,0:T(8,128)S(1)}, f32[10,8,8,128]{3,2,1,0:T(8,128)}, u32[]{:S(2)}) copy-start(f32[10,8,8,128]{3,2,1,0:T(8,128)} %shard_map.86) | copy-start | bytes 983044

commit v4 on v3

--- a/solution.py
+++ b/solution.py
@@ -139,24 +139,29 @@
     spread = diffusivity[:, None, None, None]
     cell_counts = jnp.broadcast_to(counts[:, :, None], (cx, cy, cz))
 
-    to_yp = jnp.concatenate([state[:, :, cy - 2:], source_in[:, :, cy - 1:]], 2)
-    to_ym = jnp.concatenate([state[:, :, :2], source_in[:, :, :1]], 2)
-    from_ym, from_yp = exchange(to_ym, to_yp, "gy", ny)
+    to_xm = jnp.concatenate([state[:, :2], source_in[:, :1]], 1)
+    to_xp = jnp.concatenate([state[:, cx - 2:], source_in[:, cx - 1:]], 1)
+    from_xm, from_xp = exchange(to_xm, to_xp, "gx", nx)
 
     early = chemistry(state, cell_counts, log_rate, activation, heat_release)
 
     def zeros(a, b):
         return jnp.zeros((rows, a, b, cz), jnp.float32)
 
-    wide = jnp.concatenate([from_ym[:, :, :2], state, from_yp[:, :, :2]], 2)
-    wide_src = jnp.concatenate(
-        [zeros(cx, 1), from_ym[:, :, 2:], source_in, from_yp[:, :, 2:], zeros(cx, 1)], 2
+    wide = jnp.concatenate([from_xm[:, :2], state, from_xp[:, :2]], 1)
+    wide_src = jnp.concatenate([from_xm[:, 2:], source_in, from_xp[:, 2:]], 1)
+    to_ym = jnp.concatenate([wide[:, 1:-1, :2], wide_src[:, :, :1]], 2)
+    to_yp = jnp.concatenate([wide[:, 1:-1, cy - 2:], wide_src[:, :, cy - 1:]], 2)
+    from_ym, from_yp = exchange(to_ym, to_yp, "gy", ny)
+    ext = jnp.concatenate(
+        [
+            jnp.concatenate([zeros(1, 2), wide[:, :1], zeros(1, 2)], 2),
+            jnp.concatenate([from_ym[:, :, :2], wide[:, 1:-1], from_yp[:, :, :2]], 2),
+            jnp.concatenate([zeros(1, 2), wide[:, -1:], zeros(1, 2)], 2),
+        ],
+        1,
     )
-    to_xp = jnp.concatenate([wide[:, cx - 2:], wide_src[:, cx - 1:]], 1)
-    to_xm = jnp.concatenate([wide[:, :2], wide_src[:, :1]], 1)
-    from_xm, from_xp = exchange(to_xm, to_xp, "gx", nx)
-    ext = jnp.concatenate([from_xm[:, :2], wide, from_xp[:, :2]], 1)
-    src = jnp.concatenate([from_xm[:, 2:], wide_src, from_xp[:, 2:]], 1)[:, :, 1:-1]
+    src = jnp.concatenate([from_ym[:, :, 2:], wide_src, from_yp[:, :, 2:]], 2)
     first_ext = ext[:, 1:-1, 1:-1] + time_step * (
         spread * laplace_parts(ext, 1, cx + 3) + src
     )

time: 54.1 us -> 48.9 us (0.904)
  the two profiles are of different devices: /device:TPU:16 before, /device:TPU:6 now
where the time goes in v4:
time: 48.9 us; the launch traced here: 48.6 us
  starting transfers between devices  27.6 us (56%)
  Pallas kernels  7.29 us (15%)
  local copies, waits for them, and re-layouts  5.2 us (11%)
  waiting for transfers between devices  4.47 us (9%)
  other arithmetic  3.09 us (6%)
  between operations  0.9 us (2%)
    ppermute x2, starting transfers between devices, exchange(): second = lax.ppermute(jnp.where(even, to_lo, to_hi), axis, outer)  22.2 us
    pallas_call x2, Pallas kernels, chemistry(): pl.pallas_call(chem_kernel, out_shape=jax.ShapeDtypeStruct(fields.shape,...  7.29 us
    ppermute x2, starting transfers between devices, exchange(): first = lax.ppermute(jnp.where(even, to_hi, to_lo), axis, inner)  5.41 us
    ppermute x2, waiting for transfers between devices, exchange(): second = lax.ppermute(jnp.where(even, to_lo, to_hi), axis, outer)  4.47 us
    unnamed x12, local copies, waits for them, and re-layouts  2.41 us
    add x1, other arithmetic, local(): ext[:, 1:-1, 1:-1]  1.38 us
    slice x1, other arithmetic, local(): first_section = first_ext[:, 1:-1, 1:-1]  1.2 us
    slice x2, local copies, waits for them, and re-layouts, local(): to_xm = jnp.concatenate([state[:, :2], source_in[:, :1]], 1)  0.99 us
  transfers between devices with their start and end apart: 4, of which 1 were waited for; matrix products, arithmetic and copies ran while one was open for 1% of the time, Pallas kernels for 8%

profile of v4, /device:TPU:6, one launch (start us, length us, event | category | flops | bytes accessed | tf_op | source)
XLA Modules:
  0.0 48.6 jit_solution(15708675154978296911)
XLA Ops:
  0.6 0.0 copy-start.2
  0.7 1.0 %fusion.32 = (f32[10,2,8,128]{3,2,1,0:T(8,128)S(1)}, f32[10,2,8,128]{3,2,1,0:T(8,128)S(1)}) fusion(f32[10,8,8,128]{3,2,1,0:T(8,128)} %u_ref.1), kind=kLoop, calls=%fused_computation.62 | loop fusion | bytes 327680 | tf_op jit(solution)/shard_map/slice | solution.py:142
  1.6 0.0 copy-done.2
  1.7 14.3 %collective-permute-start = (f32[10,3,8,128]{3,2,1,0:T(8,128)S(1)}, f32[10,3,8,128]{3,2,1,0:T(8,128)S(1)}, u32[]{:S(2)}, u32[]{:S(2)}) collective-permute-start(f32[10,3,8,128]{3,2,1,0:T(8,128)S(1)} %get-tuple-element.23), channel_id=1, source_target_pairs={{0,736},{32,64},{64,32},{96,128},{128,96},{160,192},{192,160},{224... | collective-permute-start | bytes 368648 | tf_op jit(solution)/shard_map/ppermute | solution.py:123
  16.0 1.9 %collective-permute-start.1 = (f32[10,3,8,128]{3,2,1,0:T(8,128)S(1)}, f32[10,3,8,128]{3,2,1,0:T(8,128)S(1)}, u32[]{:S(2)}, u32[]{:S(2)}) collective-permute-start(f32[10,3,8,128]{3,2,1,0:T(8,128)S(1)} %get-tuple-element.24), channel_id=1, source_target_pairs={{0,32},{32,0},{64,96},{96,64},{128,160},{160,128},{192,224},{224,1... | collective-permute-start | bytes 368648 | tf_op jit(solution)/shard_map/ppermute | solution.py:122
  17.9 4.5 %collective-permute-done = f32[10,3,8,128]{3,2,1,0:T(8,128)S(1)} collective-permute-done((f32[10,3,8,128]{3,2,1,0:T(8,128)S(1)}, f32[10,3,8,128]{3,2,1,0:T(8,128)S(1)}, u32[]{:S(2)}, u32[]{:S(2)}) %collective-permute-start) | collective-permute-done | bytes 122912 | tf_op jit(solution)/shard_map/ppermute | solution.py:123
  22.4 0.0 collective-permute-done.1
  22.4 0.0 copy-start
  22.5 0.9 %copy-done = f32[10,8,8,128]{3,2,1,0:T(8,128)S(1)} copy-done((f32[10,8,8,128]{3,2,1,0:T(8,128)S(1)}, f32[10,8,8,128]{3,2,1,0:T(8,128)}, u32[]{:S(2)}) %copy-start) | copy-done | bytes 327704
  23.4 0.2 broadcast_select_fusion.3
  23.6 0.0 copy-start.4
  23.6 0.1 broadcast_select_fusion.2
  23.6 3.5 %collective-permute-start.3 = (f32[10,10,3,128]{3,2,1,0:T(4,128)S(1)}, f32[10,10,3,128]{3,2,1,0:T(4,128)S(1)}, u32[]{:S(2)}, u32[]{:S(2)}) collective-permute-start(f32[10,10,3,128]{3,2,1,0:T(4,128)S(1)} %broadcast_select_fusion.2), channel_id=1, source_target_pairs={{0,1},{1,0},{2,3},{3,2},{4,5},{5,4},{6,7},{7,6},{8,9},{9,8},{10,11... | collective-permute-start | bytes 460808 | tf_op jit(solution)/shard_map/ppermute | solution.py:122
  27.1 7.9 %collective-permute-start.2 = (f32[10,10,3,128]{3,2,1,0:T(4,128)S(1)}, f32[10,10,3,128]{3,2,1,0:T(4,128)S(1)}, u32[]{:S(2)}, u32[]{:S(2)}) collective-permute-start(f32[10,10,3,128]{3,2,1,0:T(4,128)S(1)} %get-tuple-element.2), channel_id=1, source_target_pairs={{0,31},{1,2},{2,1},{3,4},{4,3},{5,6},{6,5},{7,8},{8,7},{9,10},{10,... | collective-permute-start | bytes 460808 | tf_op jit(solution)/shard_map/ppermute | solution.py:123
  35.1 0.0 copy-done.4
  35.1 0.7 %broadcast_in_dim.2.cnt_ref = s32[8,8,128]{2,1,0:T(8,128)} broadcast(s32[8,8]{1,0:T(8,128)S(1)} %copy-done.4), dimensions={0,1} | broadcast | bytes 33024 | tf_op jit(solution)/shard_map/broadcast_in_dim | solution.py:140
  35.8 0.0 copy-start.1
  35.8 3.7 %shard_map.86 = f32[10,8,8,128]{3,2,1,0:T(8,128)} custom-call(f32[21]{0:T(128)} %rate_ref.3, f32[21]{0:T(128)} %act_ref.3, f32[21]{0:T(128)} %heat_ref.3, f32[10,8,8,128]{3,2,1,0:T(8,128)} %u_ref.1, s32[8,8,128]{2,1,0:T(8,128)} %broadcast_in_dim.2.cnt_ref), custom_call_target="tpu_custom_call" | custom-call | tf_op jit(solution)/shard_map/pallas_call | solution.py:102
  39.4 0.0 copy-done.1
  39.5 0.0 collective-permute-done.3
  39.5 0.0 collective-permute-done.2
  39.5 0.1 broadcast_select_fusion.1
  39.7 0.2 pad_maximum_fusion.8
  39.8 0.3 fusion.30
  40.1 0.3 fusion.31
  40.4 0.1 slice.179
  40.5 0.1 slice.180
  40.6 0.0 copy-start.5
  40.6 0.6 %copy-done.5 = f32[10]{0:T(128)S(1)} copy-done((f32[10]{0:T(128)S(1)}, f32[10]{0:T(128)}, u32[]{:S(2)}) %copy-start.5) | copy-done | bytes 64
  41.2 1.4 %fusion.10 = f32[10,10,10,128]{3,2,1,0:T(8,128)S(1)} fusion(f32[10,1,2,128]{3,2,1,0:T(2,128)S(1)} %broadcast.10, f32[10,10,2,128]{3,2,1,0:T(2,128)S(1)} %slice.171, f32[10,1,8,128]{3,2,1,0:T(8,128)S(1)} %get-tuple-element.30, f32[10,10,8,128]{3,2,1,0:T(8,128)S(1)} %pad_maximum_fusion.9, f32[10,10,2,128]{3,2,1,0:T(2,128)S(1)} %slice.170, ...), kind=kLoop, calls=%fused_computation.11 | loop fusion | flops 3712000 | bytes 3266600 | tf_op jit(solution)/shard_map/add | solution.py:165
  42.6 0.2 fusion.29
  42.8 0.0 copy-start.3
  42.8 0.2 fusion.28
  42.9 0.8 %copy-done.3 = f32[10,8,8,128]{3,2,1,0:T(8,128)S(1)} copy-done((f32[10,8,8,128]{3,2,1,0:T(8,128)S(1)}, f32[10,8,8,128]{3,2,1,0:T(8,128)}, u32[]{:S(2)}) %copy-start.3) | copy-done | bytes 327704
  43.7 1.2 %fusion.27 = (f32[10,8,8,128]{3,2,1,0:T(8,128)}, f32[10,8,8,128]{3,2,1,0:T(8,128)}) fusion(f32[10,10,10,128]{3,2,1,0:T(8,128)S(1)} %fusion.10, f32[10,8,8,128]{3,2,1,0:T(8,128)S(1)} %copy-done.1, f32[10,8,8,128]{3,2,1,0:T(8,128)S(1)} %copy-done.3, f32[10,8,8,1]{3,2,1,0:T(8,128)S(1)} %get-tuple-element.9, f32[10,8,8,127]{3,2,1,0:T(8,128)S(1)} %get-tuple-element.7, ...), kind=kLoop, calls=%fused_computation.57 | loop fusion | flops 1228800 | bytes 3604520 | tf_op jit(solution)/shard_map/slice | solution.py:168
  44.9 3.6 %shard_map.87 = f32[10,8,8,128]{3,2,1,0:T(8,128)} custom-call(f32[21]{0:T(128)} %rate_ref.3, f32[21]{0:T(128)} %act_ref.3, f32[21]{0:T(128)} %heat_ref.3, f32[10,8,8,128]{3,2,1,0:T(8,128)} %get-tuple-element.5.u_ref, s32[8,8,128]{2,1,0:T(8,128)} %broadcast_in_dim.2.cnt_ref), custom_call_target="tpu_custom_call" | custom-call | tf_op jit(solution)/shard_map/pallas_call | solution.py:102
  (10 shorter events, 0.2 us)
Async XLA Ops:
  0.6 1.1 %copy-start.2 = (f32[10,8,8,128]{3,2,1,0:T(8,128)S(1)}, f32[10,8,8,128]{3,2,1,0:T(8,128)}, u32[]{:S(2)}) copy-start(f32[10,8,8,128]{3,2,1,0:T(8,128)} %param.8) | copy-start | bytes 983044
  1.7 20.7 %collective-permute-start = (f32[10,3,8,128]{3,2,1,0:T(8,128)S(1)}, f32[10,3,8,128]{3,2,1,0:T(8,128)S(1)}, u32[]{:S(2)}, u32[]{:S(2)}) collective-permute-start(f32[10,3,8,128]{3,2,1,0:T(8,128)S(1)} %get-tuple-element.23), channel_id=1, source_target_pairs={{0,736},{32,64},{64,32},{96,128},{128,96},{160,192},{192,160},{224... | collective-permute-start | bytes 368648 | tf_op jit(solution)/shard_map/ppermute | solution.py:123
  16.0 6.4 %collective-permute-start.1 = (f32[10,3,8,128]{3,2,1,0:T(8,128)S(1)}, f32[10,3,8,128]{3,2,1,0:T(8,128)S(1)}, u32[]{:S(2)}, u32[]{:S(2)}) collective-permute-start(f32[10,3,8,128]{3,2,1,0:T(8,128)S(1)} %get-tuple-element.24), channel_id=1, source_target_pairs={{0,32},{32,0},{64,96},{96,64},{128,160},{160,128},{192,224},{224,1... | collective-permute-start | bytes 368648 | tf_op jit(solution)/shard_map/ppermute | solution.py:122
  22.4 1.0 %copy-start = (f32[10,8,8,128]{3,2,1,0:T(8,128)S(1)}, f32[10,8,8,128]{3,2,1,0:T(8,128)}, u32[]{:S(2)}) copy-start(f32[10,8,8,128]{3,2,1,0:T(8,128)} %u_ref.1) | copy-start | bytes 983044
  23.6 11.5 %copy-start.4 = (s32[8,8]{1,0:T(8,128)S(1)}, s32[8,8]{1,0:T(8,128)}, u32[]{:S(2)}) copy-start(s32[8,8]{1,0:T(8,128)} %param.9) | copy-start | bytes 772
  23.6 15.9 %collective-permute-start.3 = (f32[10,10,3,128]{3,2,1,0:T(4,128)S(1)}, f32[10,10,3,128]{3,2,1,0:T(4,128)S(1)}, u32[]{:S(2)}, u32[]{:S(2)}) collective-permute-start(f32[10,10,3,128]{3,2,1,0:T(4,128)S(1)} %broadcast_select_fusion.2), channel_id=1, source_target_pairs={{0,1},{1,0},{2,3},{3,2},{4,5},{5,4},{6,7},{7,6},{8,9},{9,8},{10,11... | collective-permute-start | bytes 460808 | tf_op jit(solution)/shard_map/ppermute | solution.py:122
  27.1 12.4 %collective-permute-start.2 = (f32[10,10,3,128]{3,2,1,0:T(4,128)S(1)}, f32[10,10,3,128]{3,2,1,0:T(4,128)S(1)}, u32[]{:S(2)}, u32[]{:S(2)}) collective-permute-start(f32[10,10,3,128]{3,2,1,0:T(4,128)S(1)} %get-tuple-element.2), channel_id=1, source_target_pairs={{0,31},{1,2},{2,1},{3,4},{4,3},{5,6},{6,5},{7,8},{8,7},{9,10},{10,... | collective-permute-start | bytes 460808 | tf_op jit(solution)/shard_map/ppermute | solution.py:123
  35.8 3.7 %copy-start.1 = (f32[10,8,8,128]{3,2,1,0:T(8,128)S(1)}, f32[10,8,8,128]{3,2,1,0:T(8,128)}, u32[]{:S(2)}) copy-start(f32[10,8,8,128]{3,2,1,0:T(8,128)} %u_ref.1) | copy-start | bytes 983044
  40.6 0.7 %copy-start.5 = (f32[10]{0:T(128)S(1)}, f32[10]{0:T(128)}, u32[]{:S(2)}) copy-start(f32[10]{0:T(128)} %param.10) | copy-start | bytes 124
  42.8 1.0 %copy-start.3 = (f32[10,8,8,128]{3,2,1,0:T(8,128)S(1)}, f32[10,8,8,128]{3,2,1,0:T(8,128)}, u32[]{:S(2)}) copy-start(f32[10,8,8,128]{3,2,1,0:T(8,128)} %shard_map.86) | copy-start | bytes 983044

commit v5 on v4

--- a/solution.py
+++ b/solution.py
@@ -45,55 +45,129 @@
     return change
 
 
-def chem_kernel(rate_ref, act_ref, heat_ref, u_ref, cnt_ref, o_ref):
+def react(start, cnt, rate_ref, act_ref, heat_ref):
     change = stoichiometry()
     reactions = len(reaction_table)
+    temper = start[SPECIES]
+    coeffs = [jnp.exp(rate_ref[r] - act_ref[r] / temper) for r in range(reactions)]
+    heat = [heat_ref[r] for r in range(reactions)]
+    stride = time_step / cnt.astype(jnp.float32)
+    cur = list(start)
+    for turn in range(CMAX):
+        active = turn < cnt
+        rates = []
+        for r, entry in enumerate(reaction_table):
+            term = coeffs[r] * cur[entry[0]]
+            if entry[1] < SPECIES:
+                term = term * cur[entry[1]]
+            rates.append(term)
+        new = []
+        for s in range(SPECIES):
+            total = None
+            for r in range(reactions):
+                c = int(change[s, r])
+                if c == 0:
+                    continue
+                piece = rates[r] if abs(c) == 1 else rates[r] * float(abs(c))
+                if total is None:
+                    total = piece if c > 0 else -piece
+                elif c > 0:
+                    total = total + piece
+                else:
+                    total = total - piece
+            if total is None:
+                new.append(cur[s])
+            else:
+                new.append(jnp.where(active, cur[s] + stride * total, cur[s]))
+        heat_total = heat[0] * rates[0]
+        for r in range(1, reactions):
+            heat_total = heat_total + heat[r] * rates[r]
+        new.append(jnp.where(active, cur[SPECIES] + stride * heat_total, cur[SPECIES]))
+        cur = new
+    return [(cur[s] - start[s]) / time_step for s in range(len(start))]
+
+
+def chem_kernel(rate_ref, act_ref, heat_ref, u_ref, cnt_ref, o_ref):
     rows = u_ref.shape[0]
 
     def per_x(x, carry):
         start = [u_ref[s, x] for s in range(rows)]
-        temper = start[rows - 1]
-        coeffs = [jnp.exp(rate_ref[r] - act_ref[r] / temper) for r in range(reactions)]
-        heat = [heat_ref[r] for r in range(reactions)]
-        cnt = cnt_ref[x]
-        stride = time_step / cnt.astype(jnp.float32)
-        cur = list(start)
-        for turn in range(CMAX):
-            active = turn < cnt
-            rates = []
-            for r, entry in enumerate(reaction_table):
-                term = coeffs[r] * cur[entry[0]]
-                if entry[1] < SPECIES:
-                    term = term * cur[entry[1]]
-                rates.append(term)
-            new = []
-            for s in range(SPECIES):
-                total = None
-                for r in range(reactions):
-                    c = int(change[s, r])
-                    if c == 0:
-                        continue
-                    piece = rates[r] if abs(c) == 1 else rates[r] * float(abs(c))
-                    if total is None:
-                        total = piece if c > 0 else -piece
-                    elif c > 0:
-                        total = total + piece
-                    else:
-                        total = total - piece
-                if total is None:
-                    new.append(cur[s])
-                else:
-                    new.append(jnp.where(active, cur[s] + stride * total, cur[s]))
-            heat_total = heat[0] * rates[0]
-            for r in range(1, reactions):
-                heat_total = heat_total + heat[r] * rates[r]
-            new.append(jnp.where(active, cur[SPECIES] + stride * heat_total, cur[SPECIES]))
-            cur = new
+        out = react(start, cnt_ref[x], rate_ref, act_ref, heat_ref)
         for s in range(rows):
-            o_ref[s, x] = (cur[s] - start[s]) / time_step
+            o_ref[s, x] = out[s]
         return carry
 
     lax.fori_loop(0, u_ref.shape[1], per_x, 0)
+
+
+def finish_kernel(
+    diff_ref, rate_ref, act_ref, heat_ref, ext_ref, src_ref, early_ref, cnt_ref,
+    next_ref, late_ref, first_ref,
+):
+    rows, cx, cy, _ = early_ref.shape
+    lanes = ext_ref.shape[3]
+
+    def laplace(centre, xm, xp, ym, yp):
+        beside = xm + xp
+        beside = beside + ym + yp
+        beside = beside + pltpu.roll(centre, 1, 1) + pltpu.roll(centre, lanes - 1, 1)
+        return beside - 6.0 * centre
+
+    def first_row(i, carry):
+        e = i + 1
+        for r in range(rows):
+            for lo in (0, 2):
+                centre = ext_ref[r, e, pl.ds(lo + 1, cy)]
+                lap = laplace(
+                    centre,
+                    ext_ref[r, e - 1, pl.ds(lo + 1, cy)],
+                    ext_ref[r, e + 1, pl.ds(lo + 1, cy)],
+                    ext_ref[r, e, pl.ds(lo, cy)],
+                    ext_ref[r, e, pl.ds(lo + 2, cy)],
+                )
+                first_ref[r, i, pl.ds(lo, cy)] = centre + time_step * (
+                    diff_ref[r] * lap + src_ref[r, i, pl.ds(lo, cy)]
+                )
+        return carry
+
+    lax.fori_loop(0, cx + 2, first_row, 0)
+
+    def box_row(x, carry):
+        start = []
+        for r in range(rows):
+            centre = first_ref[r, x + 1, pl.ds(1, cy)]
+            lap = laplace(
+                centre,
+                first_ref[r, x, pl.ds(1, cy)],
+                first_ref[r, x + 2, pl.ds(1, cy)],
+                first_ref[r, x + 1, pl.ds(0, cy)],
+                first_ref[r, x + 1, pl.ds(2, cy)],
+            )
+            state = ext_ref[r, x + 2, pl.ds(2, cy)]
+            next_ref[r, x] = 0.5 * state + 0.5 * (
+                centre + time_step * (diff_ref[r] * lap + early_ref[r, x])
+            )
+            start.append(centre)
+        out = react(start, cnt_ref[x], rate_ref, act_ref, heat_ref)
+        for r in range(rows):
+            late_ref[r, x] = out[r]
+        return carry
+
+    lax.fori_loop(0, cx, box_row, 0)
+
+
+def finish(ext, src, early, cell_counts, diffusivity, log_rate, activation, heat_release):
+    rows, cx, cy, cz = early.shape
+    smem = pl.BlockSpec(memory_space=pltpu.SMEM)
+    vmem = pl.BlockSpec(memory_space=pltpu.VMEM)
+    box = jax.ShapeDtypeStruct(early.shape, jnp.float32)
+    return pl.pallas_call(
+        finish_kernel,
+        out_shape=(box, box),
+        in_specs=[smem, smem, smem, smem, vmem, vmem, vmem, vmem],
+        out_specs=(vmem, vmem),
+        scratch_shapes=[pltpu.VMEM((rows, cx + 2, 2 * cy, cz), jnp.float32)],
+    )(diffusivity, log_rate, activation, heat_release, ext, src, early, cell_counts)
 
 
 def chemistry(fields, cell_counts, log_rate, activation, heat_release):
@@ -124,19 +198,10 @@
     return jnp.where(even, second, first), jnp.where(even, first, second)
 
 
-def laplace_parts(s, lo, hi):
-    c = s[:, lo:hi, lo:hi]
-    beside = s[:, lo - 1:hi - 1, lo:hi] + s[:, lo + 1:hi + 1, lo:hi]
-    beside = beside + s[:, lo:hi, lo - 1:hi - 1] + s[:, lo:hi, lo + 1:hi + 1]
-    beside = beside + jnp.roll(c, 1, 3) + jnp.roll(c, -1, 3)
-    return beside - 6.0 * c
-
-
 def local(state, source_in, counts, diffusivity, log_rate, activation, heat_release):
     nx = lax.axis_size("gx")
     ny = lax.axis_size("gy")
     rows, cx, cy, cz = state.shape
-    spread = diffusivity[:, None, None, None]
     cell_counts = jnp.broadcast_to(counts[:, :, None], (cx, cy, cz))
 
     to_xm = jnp.concatenate([state[:, :2], source_in[:, :1]], 1)
@@ -162,14 +227,9 @@
         1,
     )
     src = jnp.concatenate([from_ym[:, :, 2:], wide_src, from_yp[:, :, 2:]], 2)
-    first_ext = ext[:, 1:-1, 1:-1] + time_step * (
-        spread * laplace_parts(ext, 1, cx + 3) + src
+    next_state, late_source = finish(
+        ext, src, early, cell_counts, diffusivity, log_rate, activation, heat_release
     )
-    first_section = first_ext[:, 1:-1, 1:-1]
-    next_state = 0.5 * state + 0.5 * (
-        first_section + time_step * (spread * laplace_parts(first_ext, 1, cx + 1) + early)
-    )
-    late_source = chemistry(first_section, cell_counts, log_rate, activation, heat_release)
     return (next_state, late_source)
 
 

time: 48.9 us -> 48.8 us (level)
  Pallas kernels: 7.29 us -> 9.21 us
  local copies, waits for them, and re-layouts: 5.2 us -> 3.67 us
  other arithmetic: 3.09 us -> 2.59 us
    pallas_call x0 -> x1, Pallas kernels: none -> 5.56 us  [finish(): pl.pallas_call(finish_kernel, out_shape=(box, box), in_specs=[smem, smem,...]
    pallas_call x2 -> x1, Pallas kernels: 7.29 us -> 3.65 us  [chemistry(): pl.pallas_call(chem_kernel, out_shape=jax.ShapeDtypeStruct(fields.shape,...]
    concatenate x2, other arithmetic: 0.18 us -> 2.25 us  [the longest x1 1.14 us: local(): jnp.concatenate([jnp.concatenate([zeros(1, 2), wide[:, :1], zeros(1, 2)],...]
    unnamed x12 -> x8, local copies, waits for them, and re-layouts: 2.41 us -> 1.02 us
    add x1 -> x0, other arithmetic: 1.38 us -> none  [local(): ext[:, 1:-1, 1:-1]]
    slice x1 -> x0, other arithmetic: 1.2 us -> none  [local(): first_section = first_ext[:, 1:-1, 1:-1]]
    slice x4 -> x0, local copies, waits for them, and re-layouts: 0.9 us -> none  [laplace_parts(): beside = beside + jnp.roll(c, 1, 3) + jnp.roll(c, -1, 3)]
    slice x2, local copies, waits for them, and re-layouts: 0.99 us -> 1.75 us  [local(): to_xm = jnp.concatenate([state[:, :2], source_in[:, :1]], 1)]
where the time goes in v5:
time: 48.8 us; the launch traced here: 48.4 us
  starting transfers between devices  27.6 us (57%)
  Pallas kernels  9.21 us (19%)
  waiting for transfers between devices  4.47 us (9%)
  local copies, waits for them, and re-layouts  3.67 us (8%)
  other arithmetic  2.59 us (5%)
  between operations  0.83 us (2%)
    ppermute x2, starting transfers between devices, exchange(): second = lax.ppermute(jnp.where(even, to_lo, to_hi), axis, outer)  22.2 us
    pallas_call x1, Pallas kernels, finish(): pl.pallas_call(finish_kernel, out_shape=(box, box), in_specs=[smem, smem,...  5.56 us
    ppermute x2, starting transfers between devices, exchange(): first = lax.ppermute(jnp.where(even, to_hi, to_lo), axis, inner)  5.41 us
    ppermute x2, waiting for transfers between devices, exchange(): second = lax.ppermute(jnp.where(even, to_lo, to_hi), axis, outer)  4.47 us
    pallas_call x1, Pallas kernels, chemistry(): pl.pallas_call(chem_kernel, out_shape=jax.ShapeDtypeStruct(fields.shape,...  3.65 us
    slice x2, local copies, waits for them, and re-layouts, local(): to_xm = jnp.concatenate([state[:, :2], source_in[:, :1]], 1)  1.75 us
    concatenate x1, other arithmetic, local(): jnp.concatenate([jnp.concatenate([zeros(1, 2), wide[:, :1], zeros(1, 2)],...  1.14 us
    concatenate x1, other arithmetic, local(): src = jnp.concatenate([from_ym[:, :, 2:], wide_src, from_yp[:, :, 2:]], 2)  1.11 us
  transfers between devices with their start and end apart: 4, of which 1 were waited for; matrix products, arithmetic and copies ran while one was open for 1% of the time, Pallas kernels for 8%

profile of v5, /device:TPU:6, one launch (start us, length us, event | category | flops | bytes accessed | tf_op | source)
XLA Modules:
  0.0 48.4 jit_solution(14594237085571173903)
XLA Ops:
  0.6 0.8 %fusion.14 = (f32[10,1,8,128]{3,2,1,0:T(8,128)S(1)}, f32[10,1,8,128]{3,2,1,0:T(8,128)S(1)}) fusion(f32[10,8,8,128]{3,2,1,0:T(8,128)} %param.8), kind=kLoop, calls=%fused_computation.37 | loop fusion | bytes 163840 | tf_op jit(solution)/shard_map/slice | solution.py:207
  1.5 0.9 %fusion.13 = (f32[10,2,8,128]{3,2,1,0:T(8,128)S(1)}, f32[10,2,8,128]{3,2,1,0:T(8,128)S(1)}) fusion(f32[10,8,8,128]{3,2,1,0:T(8,128)} %u_ref.1), kind=kLoop, calls=%fused_computation.36 | loop fusion | bytes 327680 | tf_op jit(solution)/shard_map/slice | solution.py:207
  2.4 14.3 %collective-permute-start = (f32[10,3,8,128]{3,2,1,0:T(8,128)S(1)}, f32[10,3,8,128]{3,2,1,0:T(8,128)S(1)}, u32[]{:S(2)}, u32[]{:S(2)}) collective-permute-start(f32[10,3,8,128]{3,2,1,0:T(8,128)S(1)} %get-tuple-element.13), channel_id=1, source_target_pairs={{0,736},{32,64},{64,32},{96,128},{128,96},{160,192},{192,160},{224... | collective-permute-start | bytes 368648 | tf_op jit(solution)/shard_map/ppermute | solution.py:197
  16.7 1.9 %collective-permute-start.1 = (f32[10,3,8,128]{3,2,1,0:T(8,128)S(1)}, f32[10,3,8,128]{3,2,1,0:T(8,128)S(1)}, u32[]{:S(2)}, u32[]{:S(2)}) collective-permute-start(f32[10,3,8,128]{3,2,1,0:T(8,128)S(1)} %get-tuple-element.14), channel_id=1, source_target_pairs={{0,32},{32,0},{64,96},{96,64},{128,160},{160,128},{192,224},{224,1... | collective-permute-start | bytes 368648 | tf_op jit(solution)/shard_map/ppermute | solution.py:196
  18.6 4.5 %collective-permute-done = f32[10,3,8,128]{3,2,1,0:T(8,128)S(1)} collective-permute-done((f32[10,3,8,128]{3,2,1,0:T(8,128)S(1)}, f32[10,3,8,128]{3,2,1,0:T(8,128)S(1)}, u32[]{:S(2)}, u32[]{:S(2)}) %collective-permute-start) | collective-permute-done | bytes 122912 | tf_op jit(solution)/shard_map/ppermute | solution.py:197
  23.1 0.0 collective-permute-done.1
  23.1 0.0 copy-start
  23.1 0.0 copy-start.2
  23.2 0.9 %copy-done = f32[10,8,8,128]{3,2,1,0:T(8,128)S(1)} copy-done((f32[10,8,8,128]{3,2,1,0:T(8,128)S(1)}, f32[10,8,8,128]{3,2,1,0:T(8,128)}, u32[]{:S(2)}) %copy-start) | copy-done | bytes 327704
  24.1 0.1 copy-done.2
  24.2 0.2 broadcast_select_fusion.3
  24.4 0.0 copy-start.3
  24.4 0.1 broadcast_select_fusion.2
  24.4 3.5 %collective-permute-start.3 = (f32[10,10,3,128]{3,2,1,0:T(4,128)S(1)}, f32[10,10,3,128]{3,2,1,0:T(4,128)S(1)}, u32[]{:S(2)}, u32[]{:S(2)}) collective-permute-start(f32[10,10,3,128]{3,2,1,0:T(4,128)S(1)} %broadcast_select_fusion.2), channel_id=1, source_target_pairs={{0,1},{1,0},{2,3},{3,2},{4,5},{5,4},{6,7},{7,6},{8,9},{9,8},{10,11... | collective-permute-start | bytes 460808 | tf_op jit(solution)/shard_map/ppermute | solution.py:196
  27.9 7.9 %collective-permute-start.2 = (f32[10,10,3,128]{3,2,1,0:T(4,128)S(1)}, f32[10,10,3,128]{3,2,1,0:T(4,128)S(1)}, u32[]{:S(2)}, u32[]{:S(2)}) collective-permute-start(f32[10,10,3,128]{3,2,1,0:T(4,128)S(1)} %get-tuple-element.2), channel_id=1, source_target_pairs={{0,31},{1,2},{2,1},{3,4},{4,3},{5,6},{6,5},{7,8},{8,7},{9,10},{10,... | collective-permute-start | bytes 460808 | tf_op jit(solution)/shard_map/ppermute | solution.py:197
  35.9 0.0 copy-done.3
  35.9 0.7 %broadcast_in_dim.2.cnt_ref = s32[8,8,128]{2,1,0:T(8,128)} broadcast(s32[8,8]{1,0:T(8,128)S(1)} %copy-done.3), dimensions={0,1} | broadcast | bytes 33024 | tf_op jit(solution)/shard_map/broadcast_in_dim | solution.py:205
  36.6 3.6 %shard_map.86.early_ref = f32[10,8,8,128]{3,2,1,0:T(8,128)} custom-call(f32[21]{0:T(128)} %rate_ref.3, f32[21]{0:T(128)} %act_ref.3, f32[21]{0:T(128)} %heat_ref.3, f32[10,8,8,128]{3,2,1,0:T(8,128)} %u_ref.1, s32[8,8,128]{2,1,0:T(8,128)} %broadcast_in_dim.2.cnt_ref), custom_call_target="tpu_custom_call" | custom-call | tf_op jit(solution)/shard_map/pallas_call | solution.py:176
  40.2 0.0 collective-permute-done.3
  40.2 0.0 collective-permute-done.2
  40.2 0.1 broadcast_select_fusion.1
  40.3 0.1 slice.86
  40.4 0.1 slice.87
  40.5 0.0 copy-start.1
  40.5 1.1 %pad_maximum_fusion.1.src_ref = f32[10,10,10,128]{3,2,1,0:T(8,128)} fusion(f32[10,10,1,128]{3,2,1,0:T(1,128)S(1)} %slice.87, f32[10,1,8,128]{3,2,1,0:T(8,128)S(1)} %get-tuple-element.20, f32[10,8,8,128]{3,2,1,0:T(8,128)S(1)} %copy-done.2, f32[10,1,8,128]{3,2,1,0:T(8,128)S(1)} %get-tuple-element.16, f32[10,10,1,128]{3,2,1,0:T(1,128)S(1)} %slice.86), kind=kLoop, calls=%fused_computation.13 | loop fusion | flops 512000 | bytes 1024000 | tf_op jit(solution)/shard_map/concatenate | solution.py:229
  41.7 0.0 copy-done.1
  41.7 1.1 %fusion.3.ext_ref = f32[10,12,12,128]{3,2,1,0:T(8,128)} fusion(f32[10,2,8,128]{3,2,1,0:T(8,128)S(1)} %slice.80, f32[10,8,8,128]{3,2,1,0:T(8,128)S(1)} %copy-done.1, f32[10,2,8,128]{3,2,1,0:T(8,128)S(1)} %slice.79, f32[10,1,2,128]{3,2,1,0:T(2,128)S(1)} %broadcast.6, f32[10,1,8,128]{3,2,1,0:T(8,128)S(1)} %get-tuple-element.19, ...), kind=kLoop, calls=%fused_computation.8 | loop fusion | flops 3870720 | bytes 1525760 | tf_op jit(solution)/shard_map/concatenate | solution.py:221
  42.8 5.6 %shard_map.87 = (f32[10,8,8,128]{3,2,1,0:T(8,128)}, f32[10,8,8,128]{3,2,1,0:T(8,128)}) custom-call(f32[10]{0:T(128)} %diff_ref.1, f32[21]{0:T(128)} %rate_ref.3, f32[21]{0:T(128)} %act_ref.3, f32[21]{0:T(128)} %heat_ref.3, f32[10,12,12,128]{3,2,1,0:T(8,128)} %fusion.3.ext_ref, f32[10,10,10,128]{3,2,1,0:T(8,128)} %pad_maximum_fusion.1.src_ref, ...), custom_call_target="tpu_custom_call" | custom-call | tf_op jit(solution)/shard_map/pallas_call | solution.py:164
  (8 shorter events, 0.1 us)
Async XLA Ops:
  2.4 20.7 %collective-permute-start = (f32[10,3,8,128]{3,2,1,0:T(8,128)S(1)}, f32[10,3,8,128]{3,2,1,0:T(8,128)S(1)}, u32[]{:S(2)}, u32[]{:S(2)}) collective-permute-start(f32[10,3,8,128]{3,2,1,0:T(8,128)S(1)} %get-tuple-element.13), channel_id=1, source_target_pairs={{0,736},{32,64},{64,32},{96,128},{128,96},{160,192},{192,160},{224... | collective-permute-start | bytes 368648 | tf_op jit(solution)/shard_map/ppermute | solution.py:197
  16.7 6.4 %collective-permute-start.1 = (f32[10,3,8,128]{3,2,1,0:T(8,128)S(1)}, f32[10,3,8,128]{3,2,1,0:T(8,128)S(1)}, u32[]{:S(2)}, u32[]{:S(2)}) collective-permute-start(f32[10,3,8,128]{3,2,1,0:T(8,128)S(1)} %get-tuple-element.14), channel_id=1, source_target_pairs={{0,32},{32,0},{64,96},{96,64},{128,160},{160,128},{192,224},{224,1... | collective-permute-start | bytes 368648 | tf_op jit(solution)/shard_map/ppermute | solution.py:196
  23.1 1.0 %copy-start = (f32[10,8,8,128]{3,2,1,0:T(8,128)S(1)}, f32[10,8,8,128]{3,2,1,0:T(8,128)}, u32[]{:S(2)}) copy-start(f32[10,8,8,128]{3,2,1,0:T(8,128)} %u_ref.1) | copy-start | bytes 983044
  23.1 1.1 %copy-start.2 = (f32[10,8,8,128]{3,2,1,0:T(8,128)S(1)}, f32[10,8,8,128]{3,2,1,0:T(8,128)}, u32[]{:S(2)}) copy-start(f32[10,8,8,128]{3,2,1,0:T(8,128)} %param.8) | copy-start | bytes 983044
  24.4 11.5 %copy-start.3 = (s32[8,8]{1,0:T(8,128)S(1)}, s32[8,8]{1,0:T(8,128)}, u32[]{:S(2)}) copy-start(s32[8,8]{1,0:T(8,128)} %param.9) | copy-start | bytes 772
  24.4 15.8 %collective-permute-start.3 = (f32[10,10,3,128]{3,2,1,0:T(4,128)S(1)}, f32[10,10,3,128]{3,2,1,0:T(4,128)S(1)}, u32[]{:S(2)}, u32[]{:S(2)}) collective-permute-start(f32[10,10,3,128]{3,2,1,0:T(4,128)S(1)} %broadcast_select_fusion.2), channel_id=1, source_target_pairs={{0,1},{1,0},{2,3},{3,2},{4,5},{5,4},{6,7},{7,6},{8,9},{9,8},{10,11... | collective-permute-start | bytes 460808 | tf_op jit(solution)/shard_map/ppermute | solution.py:196
  27.9 12.3 %collective-permute-start.2 = (f32[10,10,3,128]{3,2,1,0:T(4,128)S(1)}, f32[10,10,3,128]{3,2,1,0:T(4,128)S(1)}, u32[]{:S(2)}, u32[]{:S(2)}) collective-permute-start(f32[10,10,3,128]{3,2,1,0:T(4,128)S(1)} %get-tuple-element.2), channel_id=1, source_target_pairs={{0,31},{1,2},{2,1},{3,4},{4,3},{5,6},{6,5},{7,8},{8,7},{9,10},{10,... | collective-permute-start | bytes 460808 | tf_op jit(solution)/shard_map/ppermute | solution.py:197
  40.5 1.1 %copy-start.1 = (f32[10,8,8,128]{3,2,1,0:T(8,128)S(1)}, f32[10,8,8,128]{3,2,1,0:T(8,128)}, u32[]{:S(2)}) copy-start(f32[10,8,8,128]{3,2,1,0:T(8,128)} %u_ref.1) | copy-start | bytes 983044

commit v6 on v5

--- a/solution.py
+++ b/solution.py
@@ -209,6 +209,7 @@
     from_xm, from_xp = exchange(to_xm, to_xp, "gx", nx)
 
     early = chemistry(state, cell_counts, log_rate, activation, heat_release)
+    early, from_xm, from_xp = lax.optimization_barrier((early, from_xm, from_xp))
 
     def zeros(a, b):
         return jnp.zeros((rows, a, b, cz), jnp.float32)

time: 48.8 us -> 50.7 us (1.039)
  starting transfers between devices: 27.6 us -> 28.3 us
  local copies, waits for them, and re-layouts: 3.67 us -> 4.32 us
  waiting for transfers between devices: 4.47 us -> 5.12 us
    ppermute x2, starting transfers between devices: 22.2 us -> 22.9 us  [exchange(): second = lax.ppermute(jnp.where(even, to_lo, to_hi), axis, outer)]
    unnamed x8 -> x6, local copies, waits for them, and re-layouts: 1.02 us -> 1.68 us
    ppermute x2, waiting for transfers between devices: 4.47 us -> 5.11 us  [exchange(): second = lax.ppermute(jnp.where(even, to_lo, to_hi), axis, outer)]
  transfers between devices with their start and end apart: 4 -> 4, of which waited for: 1 -> 2; matrix products, arithmetic and copies ran while one was open for 1% -> 1% of each run, Pallas kernels for 8% -> 7%
where the time goes in v6:
time: 50.7 us; the launch traced here: 50.3 us
  starting transfers between devices  28.3 us (56%)
  Pallas kernels  9.2 us (18%)
  waiting for transfers between devices  5.12 us (10%)
  local copies, waits for them, and re-layouts  4.32 us (9%)
  other arithmetic  2.59 us (5%)
  between operations  0.81 us (2%)
    ppermute x2, starting transfers between devices, exchange(): second = lax.ppermute(jnp.where(even, to_lo, to_hi), axis, outer)  22.9 us
    pallas_call x1, Pallas kernels, finish(): pl.pallas_call(finish_kernel, out_shape=(box, box), in_specs=[smem, smem,...  5.56 us
    ppermute x2, starting transfers between devices, exchange(): first = lax.ppermute(jnp.where(even, to_hi, to_lo), axis, inner)  5.41 us
    ppermute x2, waiting for transfers between devices, exchange(): second = lax.ppermute(jnp.where(even, to_lo, to_hi), axis, outer)  5.11 us
    pallas_call x1, Pallas kernels, chemistry(): pl.pallas_call(chem_kernel, out_shape=jax.ShapeDtypeStruct(fields.shape,...  3.63 us
    slice x2, local copies, waits for them, and re-layouts, local(): to_xm = jnp.concatenate([state[:, :2], source_in[:, :1]], 1)  1.75 us
    unnamed x6, local copies, waits for them, and re-layouts  1.68 us
    concatenate x1, other arithmetic, local(): jnp.concatenate([jnp.concatenate([zeros(1, 2), wide[:, :1], zeros(1, 2)],...  1.14 us
  transfers between devices with their start and end apart: 4, of which 2 were waited for; matrix products, arithmetic and copies ran while one was open for 1% of the time, Pallas kernels for 7%

profile of v6, /device:TPU:6, one launch (start us, length us, event | category | flops | bytes accessed | tf_op | source)
XLA Modules:
  0.0 50.3 jit_solution(18277215553114550614)
XLA Ops:
  0.6 0.8 %fusion.14 = (f32[10,1,8,128]{3,2,1,0:T(8,128)S(1)}, f32[10,1,8,128]{3,2,1,0:T(8,128)S(1)}) fusion(f32[10,8,8,128]{3,2,1,0:T(8,128)} %param.8), kind=kLoop, calls=%fused_computation.37 | loop fusion | bytes 163840 | tf_op jit(solution)/shard_map/slice | solution.py:207
  1.5 0.9 %fusion.13 = (f32[10,2,8,128]{3,2,1,0:T(8,128)S(1)}, f32[10,2,8,128]{3,2,1,0:T(8,128)S(1)}) fusion(f32[10,8,8,128]{3,2,1,0:T(8,128)} %u_ref.1), kind=kLoop, calls=%fused_computation.36 | loop fusion | bytes 327680 | tf_op jit(solution)/shard_map/slice | solution.py:207
  2.4 1.9 %collective-permute-start.1 = (f32[10,3,8,128]{3,2,1,0:T(8,128)S(1)}, f32[10,3,8,128]{3,2,1,0:T(8,128)S(1)}, u32[]{:S(2)}, u32[]{:S(2)}) collective-permute-start(f32[10,3,8,128]{3,2,1,0:T(8,128)S(1)} %get-tuple-element.19), channel_id=1, source_target_pairs={{0,32},{32,0},{64,96},{96,64},{128,160},{160,128},{192,224},{224,1... | collective-permute-start | bytes 368648 | tf_op jit(solution)/shard_map/ppermute | solution.py:196
  4.4 14.9 %collective-permute-start = (f32[10,3,8,128]{3,2,1,0:T(8,128)S(1)}, f32[10,3,8,128]{3,2,1,0:T(8,128)S(1)}, u32[]{:S(2)}, u32[]{:S(2)}) collective-permute-start(f32[10,3,8,128]{3,2,1,0:T(8,128)S(1)} %get-tuple-element.20), channel_id=1, source_target_pairs={{0,736},{32,64},{64,32},{96,128},{128,96},{160,192},{192,160},{224... | collective-permute-start | bytes 368648 | tf_op jit(solution)/shard_map/ppermute | solution.py:197
  19.3 0.0 copy-start.2
  19.3 0.7 %copy-done.2 = s32[8,8]{1,0:T(8,128)S(1)} copy-done((s32[8,8]{1,0:T(8,128)S(1)}, s32[8,8]{1,0:T(8,128)}, u32[]{:S(2)}) %copy-start.2) | copy-done | bytes 280
  20.0 0.7 %broadcast_in_dim.2.cnt_ref = s32[8,8,128]{2,1,0:T(8,128)} broadcast(s32[8,8]{1,0:T(8,128)S(1)} %copy-done.2), dimensions={0,1} | broadcast | bytes 33024 | tf_op jit(solution)/shard_map/broadcast_in_dim | solution.py:205
  20.7 3.6 %shard_map.86.early_ref = f32[10,8,8,128]{3,2,1,0:T(8,128)} custom-call(f32[21]{0:T(128)} %rate_ref.3, f32[21]{0:T(128)} %act_ref.3, f32[21]{0:T(128)} %heat_ref.3, f32[10,8,8,128]{3,2,1,0:T(8,128)} %u_ref.1, s32[8,8,128]{2,1,0:T(8,128)} %broadcast_in_dim.2.cnt_ref), custom_call_target="tpu_custom_call" | custom-call | tf_op jit(solution)/shard_map/pallas_call | solution.py:176
  24.3 0.0 collective-permute-done.1
  24.3 1.4 %collective-permute-done = f32[10,3,8,128]{3,2,1,0:T(8,128)S(1)} collective-permute-done((f32[10,3,8,128]{3,2,1,0:T(8,128)S(1)}, f32[10,3,8,128]{3,2,1,0:T(8,128)S(1)}, u32[]{:S(2)}, u32[]{:S(2)}) %collective-permute-start) | collective-permute-done | bytes 122912 | tf_op jit(solution)/shard_map/ppermute | solution.py:197
  25.7 0.0 copy-start
  25.7 0.0 copy-start.1
  25.8 0.9 %copy-done = f32[10,8,8,128]{3,2,1,0:T(8,128)S(1)} copy-done((f32[10,8,8,128]{3,2,1,0:T(8,128)S(1)}, f32[10,8,8,128]{3,2,1,0:T(8,128)}, u32[]{:S(2)}) %copy-start) | copy-done | bytes 327704
  26.7 0.1 copy-done.1
  26.8 0.2 broadcast_select_fusion.3
  27.0 0.1 broadcast_select_fusion.2
  27.0 3.5 %collective-permute-start.3 = (f32[10,10,3,128]{3,2,1,0:T(4,128)S(1)}, f32[10,10,3,128]{3,2,1,0:T(4,128)S(1)}, u32[]{:S(2)}, u32[]{:S(2)}) collective-permute-start(f32[10,10,3,128]{3,2,1,0:T(4,128)S(1)} %broadcast_select_fusion.2), channel_id=1, source_target_pairs={{0,1},{1,0},{2,3},{3,2},{4,5},{5,4},{6,7},{7,6},{8,9},{9,8},{10,11... | collective-permute-start | bytes 460808 | tf_op jit(solution)/shard_map/ppermute | solution.py:196
  30.5 7.9 %collective-permute-start.2 = (f32[10,10,3,128]{3,2,1,0:T(4,128)S(1)}, f32[10,10,3,128]{3,2,1,0:T(4,128)S(1)}, u32[]{:S(2)}, u32[]{:S(2)}) collective-permute-start(f32[10,10,3,128]{3,2,1,0:T(4,128)S(1)} %get-tuple-element.8), channel_id=1, source_target_pairs={{0,31},{1,2},{2,1},{3,4},{4,3},{5,6},{6,5},{7,8},{8,7},{9,10},{10,... | collective-permute-start | bytes 460808 | tf_op jit(solution)/shard_map/ppermute | solution.py:197
  38.5 0.0 collective-permute-done.3
  38.5 3.7 %collective-permute-done.2 = f32[10,10,3,128]{3,2,1,0:T(4,128)S(1)} collective-permute-done((f32[10,10,3,128]{3,2,1,0:T(4,128)S(1)}, f32[10,10,3,128]{3,2,1,0:T(4,128)S(1)}, u32[]{:S(2)}, u32[]{:S(2)}) %collective-permute-start.2) | collective-permute-done | bytes 153632 | tf_op jit(solution)/shard_map/ppermute | solution.py:197
  42.2 0.1 broadcast_select_fusion.1
  42.3 0.1 slice.80
  42.4 0.1 slice.81
  42.5 1.1 %pad_maximum_fusion.1.src_ref = f32[10,10,10,128]{3,2,1,0:T(8,128)} fusion(f32[10,10,1,128]{3,2,1,0:T(1,128)S(1)} %slice.81, f32[10,1,8,128]{3,2,1,0:T(8,128)S(1)} %get-tuple-element.26, f32[10,8,8,128]{3,2,1,0:T(8,128)S(1)} %copy-done.1, f32[10,1,8,128]{3,2,1,0:T(8,128)S(1)} %get-tuple-element.22, f32[10,10,1,128]{3,2,1,0:T(1,128)S(1)} %slice.80), kind=kLoop, calls=%fused_computation.13 | loop fusion | flops 512000 | bytes 1024000 | tf_op jit(solution)/shard_map/concatenate | solution.py:230
  43.6 1.1 %fusion.3.ext_ref = f32[10,12,12,128]{3,2,1,0:T(8,128)} fusion(f32[10,2,8,128]{3,2,1,0:T(8,128)S(1)} %slice.65, f32[10,8,8,128]{3,2,1,0:T(8,128)S(1)} %copy-done, f32[10,2,8,128]{3,2,1,0:T(8,128)S(1)} %slice.64, f32[10,1,2,128]{3,2,1,0:T(2,128)S(1)} %broadcast.6, f32[10,1,8,128]{3,2,1,0:T(8,128)S(1)} %get-tuple-element.25, f32[10,10,2,128]{3,2,1,0:T(2,128)S(1)} %slice.79, ...), kind=kLoop, calls=%fused_computation.8 | loop fusion | flops 3870720 | bytes 1525760 | tf_op jit(solution)/shard_map/concatenate | solution.py:222
  44.7 5.6 %shard_map.87 = (f32[10,8,8,128]{3,2,1,0:T(8,128)}, f32[10,8,8,128]{3,2,1,0:T(8,128)}) custom-call(f32[10]{0:T(128)} %diff_ref.1, f32[21]{0:T(128)} %rate_ref.3, f32[21]{0:T(128)} %act_ref.3, f32[21]{0:T(128)} %heat_ref.3, f32[10,12,12,128]{3,2,1,0:T(8,128)} %fusion.3.ext_ref, f32[10,10,10,128]{3,2,1,0:T(8,128)} %pad_maximum_fusion.1.src_ref, ...), custom_call_target="tpu_custom_call" | custom-call | tf_op jit(solution)/shard_map/pallas_call | solution.py:164
  (8 shorter events, 0.1 us)
Async XLA Ops:
  2.4 21.9 %collective-permute-start.1 = (f32[10,3,8,128]{3,2,1,0:T(8,128)S(1)}, f32[10,3,8,128]{3,2,1,0:T(8,128)S(1)}, u32[]{:S(2)}, u32[]{:S(2)}) collective-permute-start(f32[10,3,8,128]{3,2,1,0:T(8,128)S(1)} %get-tuple-element.19), channel_id=1, source_target_pairs={{0,32},{32,0},{64,96},{96,64},{128,160},{160,128},{192,224},{224,1... | collective-permute-start | bytes 368648 | tf_op jit(solution)/shard_map/ppermute | solution.py:196
  4.4 21.3 %collective-permute-start = (f32[10,3,8,128]{3,2,1,0:T(8,128)S(1)}, f32[10,3,8,128]{3,2,1,0:T(8,128)S(1)}, u32[]{:S(2)}, u32[]{:S(2)}) collective-permute-start(f32[10,3,8,128]{3,2,1,0:T(8,128)S(1)} %get-tuple-element.20), channel_id=1, source_target_pairs={{0,736},{32,64},{64,32},{96,128},{128,96},{160,192},{192,160},{224... | collective-permute-start | bytes 368648 | tf_op jit(solution)/shard_map/ppermute | solution.py:197
  19.3 0.7 %copy-start.2 = (s32[8,8]{1,0:T(8,128)S(1)}, s32[8,8]{1,0:T(8,128)}, u32[]{:S(2)}) copy-start(s32[8,8]{1,0:T(8,128)} %param.9) | copy-start | bytes 772
  25.7 1.0 %copy-start = (f32[10,8,8,128]{3,2,1,0:T(8,128)S(1)}, f32[10,8,8,128]{3,2,1,0:T(8,128)}, u32[]{:S(2)}) copy-start(f32[10,8,8,128]{3,2,1,0:T(8,128)} %u_ref.1) | copy-start | bytes 983044
  25.7 1.1 %copy-start.1 = (f32[10,8,8,128]{3,2,1,0:T(8,128)S(1)}, f32[10,8,8,128]{3,2,1,0:T(8,128)}, u32[]{:S(2)}) copy-start(f32[10,8,8,128]{3,2,1,0:T(8,128)} %param.8) | copy-start | bytes 983044
  27.0 11.4 %collective-permute-start.3 = (f32[10,10,3,128]{3,2,1,0:T(4,128)S(1)}, f32[10,10,3,128]{3,2,1,0:T(4,128)S(1)}, u32[]{:S(2)}, u32[]{:S(2)}) collective-permute-start(f32[10,10,3,128]{3,2,1,0:T(4,128)S(1)} %broadcast_select_fusion.2), channel_id=1, source_target_pairs={{0,1},{1,0},{2,3},{3,2},{4,5},{5,4},{6,7},{7,6},{8,9},{9,8},{10,11... | collective-permute-start | bytes 460808 | tf_op jit(solution)/shard_map/ppermute | solution.py:196
  30.5 11.7 %collective-permute-start.2 = (f32[10,10,3,128]{3,2,1,0:T(4,128)S(1)}, f32[10,10,3,128]{3,2,1,0:T(4,128)S(1)}, u32[]{:S(2)}, u32[]{:S(2)}) collective-permute-start(f32[10,10,3,128]{3,2,1,0:T(4,128)S(1)} %get-tuple-element.8), channel_id=1, source_target_pairs={{0,31},{1,2},{2,1},{3,4},{4,3},{5,6},{6,5},{7,8},{8,7},{9,10},{10,... | collective-permute-start | bytes 460808 | tf_op jit(solution)/shard_map/ppermute | solution.py:197

commit v7 on v5

--- a/solution.py
+++ b/solution.py
@@ -100,43 +100,72 @@
     lax.fori_loop(0, u_ref.shape[1], per_x, 0)
 
 
+def laplace_tile(centre, xm, xp, ym, yp):
+    lanes = centre.shape[-1]
+    beside = xm + xp
+    beside = beside + ym + yp
+    beside = beside + pltpu.roll(centre, 1, 1) + pltpu.roll(centre, lanes - 1, 1)
+    return beside - 6.0 * centre
+
+
+def first_rows(diff_ref, box_ref, src_ref, first_ref, e_of, s_of, rows_i, cy):
+    rows = first_ref.shape[0]
+    for i in rows_i:
+        e, s = e_of(i), s_of(i)
+        for r in range(rows):
+            for lo in (0, 2):
+                centre = box_ref[r, e, pl.ds(lo + 1, cy)]
+                lap = laplace_tile(
+                    centre,
+                    box_ref[r, e - 1, pl.ds(lo + 1, cy)],
+                    box_ref[r, e + 1, pl.ds(lo + 1, cy)],
+                    box_ref[r, e, pl.ds(lo, cy)],
+                    box_ref[r, e, pl.ds(lo + 2, cy)],
+                )
+                first_ref[r, i, pl.ds(lo, cy)] = centre + time_step * (
+                    diff_ref[r] * lap + src_ref[r, s, pl.ds(lo, cy)]
+                )
+
+
+def partial_kernel(
+    diff_ref, rate_ref, act_ref, heat_ref, wide_ref, wsrc_ref, cnt_ref, first_ref, late_ref
+):
+    rows, cx = wide_ref.shape[0], wide_ref.shape[1]
+    cy = late_ref.shape[2]
+    first_rows(
+        diff_ref, wide_ref, wsrc_ref, first_ref,
+        lambda i: i - 1, lambda i: i - 1, range(2, cx), cy,
+    )
+
+    def per_x(x, carry):
+        start = [first_ref[r, x + 1, pl.ds(1, cy)] for r in range(rows)]
+        out = react(start, cnt_ref[x], rate_ref, act_ref, heat_ref)
+        for r in range(rows):
+            late_ref[r, x] = out[r]
+        return carry
+
+    lax.fori_loop(1, cx - 1, per_x, 0)
+
+
 def finish_kernel(
     diff_ref, rate_ref, act_ref, heat_ref, ext_ref, src_ref, early_ref, cnt_ref,
-    next_ref, late_ref, first_ref,
+    part_ref, late_part_ref, next_ref, late_ref, first_ref,
 ):
     rows, cx, cy, _ = early_ref.shape
-    lanes = ext_ref.shape[3]
-
-    def laplace(centre, xm, xp, ym, yp):
-        beside = xm + xp
-        beside = beside + ym + yp
-        beside = beside + pltpu.roll(centre, 1, 1) + pltpu.roll(centre, lanes - 1, 1)
-        return beside - 6.0 * centre
-
-    def first_row(i, carry):
-        e = i + 1
+    edge = (0, 1, cx, cx + 1)
+    first_rows(
+        diff_ref, ext_ref, src_ref, first_ref,
+        lambda i: i + 1, lambda i: i, edge, cy,
+    )
+    for i in range(2, cx):
         for r in range(rows):
-            for lo in (0, 2):
-                centre = ext_ref[r, e, pl.ds(lo + 1, cy)]
-                lap = laplace(
-                    centre,
-                    ext_ref[r, e - 1, pl.ds(lo + 1, cy)],
-                    ext_ref[r, e + 1, pl.ds(lo + 1, cy)],
-                    ext_ref[r, e, pl.ds(lo, cy)],
-                    ext_ref[r, e, pl.ds(lo + 2, cy)],
-                )
-                first_ref[r, i, pl.ds(lo, cy)] = centre + time_step * (
-                    diff_ref[r] * lap + src_ref[r, i, pl.ds(lo, cy)]
-                )
-        return carry
-
-    lax.fori_loop(0, cx + 2, first_row, 0)
-
-    def box_row(x, carry):
+            first_ref[r, i] = part_ref[r, i]
+
+    for x in range(cx):
         start = []
         for r in range(rows):
             centre = first_ref[r, x + 1, pl.ds(1, cy)]
-            lap = laplace(
+            lap = laplace_tile(
                 centre,
                 first_ref[r, x, pl.ds(1, cy)],
                 first_ref[r, x + 2, pl.ds(1, cy)],
@@ -148,15 +177,32 @@
                 centre + time_step * (diff_ref[r] * lap + early_ref[r, x])
             )
             start.append(centre)
-        out = react(start, cnt_ref[x], rate_ref, act_ref, heat_ref)
-        for r in range(rows):
-            late_ref[r, x] = out[r]
-        return carry
-
-    lax.fori_loop(0, cx, box_row, 0)
-
-
-def finish(ext, src, early, cell_counts, diffusivity, log_rate, activation, heat_release):
+        if x in (0, cx - 1):
+            out = react(start, cnt_ref[x], rate_ref, act_ref, heat_ref)
+            for r in range(rows):
+                late_ref[r, x] = out[r]
+        else:
+            for r in range(rows):
+                late_ref[r, x] = late_part_ref[r, x]
+
+
+def partial(wide, wide_src, cell_counts, diffusivity, log_rate, activation, heat_release):
+    rows, cx, _, cz = wide.shape
+    cy = cell_counts.shape[1]
+    smem = pl.BlockSpec(memory_space=pltpu.SMEM)
+    vmem = pl.BlockSpec(memory_space=pltpu.VMEM)
+    return pl.pallas_call(
+        partial_kernel,
+        out_shape=(
+            jax.ShapeDtypeStruct((rows, cx + 2, 2 * cy, cz), jnp.float32),
+            jax.ShapeDtypeStruct((rows, cx, cy, cz), jnp.float32),
+        ),
+        in_specs=[smem, smem, smem, smem, vmem, vmem, vmem],
+        out_specs=(vmem, vmem),
+    )(diffusivity, log_rate, activation, heat_release, wide, wide_src, cell_counts)
+
+
+def finish(ext, src, early, cell_counts, part, late_part, diffusivity, log_rate, activation, heat_release):
     rows, cx, cy, cz = early.shape
     smem = pl.BlockSpec(memory_space=pltpu.SMEM)
     vmem = pl.BlockSpec(memory_space=pltpu.VMEM)
@@ -164,10 +210,10 @@
     return pl.pallas_call(
         finish_kernel,
         out_shape=(box, box),
-        in_specs=[smem, smem, smem, smem, vmem, vmem, vmem, vmem],
+        in_specs=[smem, smem, smem, smem] + [vmem] * 6,
         out_specs=(vmem, vmem),
         scratch_shapes=[pltpu.VMEM((rows, cx + 2, 2 * cy, cz), jnp.float32)],
-    )(diffusivity, log_rate, activation, heat_release, ext, src, early, cell_counts)
+    )(diffusivity, log_rate, activation, heat_release, ext, src, early, cell_counts, part, late_part)
 
 
 def chemistry(fields, cell_counts, log_rate, activation, heat_release):
@@ -204,31 +250,54 @@
     rows, cx, cy, cz = state.shape
     cell_counts = jnp.broadcast_to(counts[:, :, None], (cx, cy, cz))
 
-    to_xm = jnp.concatenate([state[:, :2], source_in[:, :1]], 1)
-    to_xp = jnp.concatenate([state[:, cx - 2:], source_in[:, cx - 1:]], 1)
-    from_xm, from_xp = exchange(to_xm, to_xp, "gx", nx)
-
-    early = chemistry(state, cell_counts, log_rate, activation, heat_release)
-
     def zeros(a, b):
         return jnp.zeros((rows, a, b, cz), jnp.float32)
 
-    wide = jnp.concatenate([from_xm[:, :2], state, from_xp[:, :2]], 1)
-    wide_src = jnp.concatenate([from_xm[:, 2:], source_in, from_xp[:, 2:]], 1)
-    to_ym = jnp.concatenate([wide[:, 1:-1, :2], wide_src[:, :, :1]], 2)
-    to_yp = jnp.concatenate([wide[:, 1:-1, cy - 2:], wide_src[:, :, cy - 1:]], 2)
+    to_ym = jnp.concatenate([state[:, :, :2], source_in[:, :, :1]], 2)
+    to_yp = jnp.concatenate([state[:, :, cy - 2:], source_in[:, :, cy - 1:]], 2)
     from_ym, from_yp = exchange(to_ym, to_yp, "gy", ny)
+    wide = jnp.concatenate([from_ym[:, :, :2], state, from_yp[:, :, :2]], 2)
+    wide_src = jnp.concatenate([from_ym[:, :, 2:], source_in, from_yp[:, :, 2:]], 2)
+
+    def corners(x):
+        return jnp.concatenate([wide[:, x:x + 1, 1:2], wide[:, x:x + 1, cy + 2:cy + 3], zeros(1, cy - 2)], 2)
+
+    to_xm = jnp.concatenate([state[:, :2], source_in[:, :1], corners(0)], 1)
+    to_xp = jnp.concatenate([state[:, cx - 2:], source_in[:, cx - 1:], corners(cx - 1)], 1)
+    from_xm, from_xp = exchange(to_xm, to_xp, "gx", nx)
+
+    early = chemistry(state, cell_counts, log_rate, activation, heat_release)
+    part, late_part = partial(
+        wide, wide_src, cell_counts, diffusivity, log_rate, activation, heat_release
+    )
+    part, late_part, from_xm, from_xp = lax.optimization_barrier(
+        (part, late_part, from_xm, from_xp)
+    )
+
+    def edge_row(got, k):
+        return jnp.concatenate([zeros(1, 1), got[:, 3:, :1], got[:, k:k + 1], got[:, 3:, 1:2], zeros(1, 1)], 2)
+
     ext = jnp.concatenate(
         [
-            jnp.concatenate([zeros(1, 2), wide[:, :1], zeros(1, 2)], 2),
-            jnp.concatenate([from_ym[:, :, :2], wide[:, 1:-1], from_yp[:, :, :2]], 2),
-            jnp.concatenate([zeros(1, 2), wide[:, -1:], zeros(1, 2)], 2),
+            jnp.concatenate([zeros(1, 2), from_xm[:, :1], zeros(1, 2)], 2),
+            edge_row(from_xm, 1),
+            wide,
+            edge_row(from_xp, 0),
+            jnp.concatenate([zeros(1, 2), from_xp[:, 1:2], zeros(1, 2)], 2),
         ],
         1,
     )
-    src = jnp.concatenate([from_ym[:, :, 2:], wide_src, from_yp[:, :, 2:]], 2)
+    src = jnp.concatenate(
+        [
+            jnp.concatenate([zeros(1, 1), from_xm[:, 2:3], zeros(1, 1)], 2),
+            wide_src,
+            jnp.concatenate([zeros(1, 1), from_xp[:, 2:3], zeros(1, 1)], 2),
+        ],
+        1,
+    )
     next_state, late_source = finish(
-        ext, src, early, cell_counts, diffusivity, log_rate, activation, heat_release
+        ext, src, early, cell_counts, part, late_part,
+        diffusivity, log_rate, activation, heat_release,
     )
     return (next_state, late_source)
 

time: 48.8 us -> 50.5 us (1.035)
  the two profiles are of different devices: /device:TPU:6 before, /device:TPU:8 now
where the time goes in v7:
time: 50.5 us; the launch traced here: 50.2 us
  starting transfers between devices  29.2 us (58%)
  Pallas kernels  11.2 us (22%)
  local copies, waits for them, and re-layouts  4.28 us (8%)
  other arithmetic  3.68 us (7%)
  between operations  0.94 us (2%)
  waiting for transfers between devices  0.8 us (2%)
    ppermute x2, starting transfers between devices, exchange(): second = lax.ppermute(jnp.where(even, to_lo, to_hi), axis, outer)  17.5 us
    ppermute x2, starting transfers between devices, exchange(): first = lax.ppermute(jnp.where(even, to_hi, to_lo), axis, inner)  11.7 us
    pallas_call x1, Pallas kernels, partial(): pl.pallas_call(partial_kernel, out_shape=(jax.ShapeDtypeStruct((rows, cx...  4.02 us
    pallas_call x1, Pallas kernels, chemistry(): pl.pallas_call(chem_kernel, out_shape=jax.ShapeDtypeStruct(fields.shape,...  3.66 us
    pallas_call x1, Pallas kernels, finish(): pl.pallas_call(finish_kernel, out_shape=(box, box), in_specs=[smem, smem,...  3.56 us
    slice x2, local copies, waits for them, and re-layouts, local(): to_ym = jnp.concatenate([state[:, :, :2], source_in[:, :, :1]], 2)  2.28 us
    concatenate x1, other arithmetic, local(): jnp.concatenate([jnp.concatenate([zeros(1, 1), from_xm[:, 2:3], zeros(1,...  1.2 us
  transfers between devices with their start and end apart: 4, of which 1 were waited for; matrix products, arithmetic and copies ran while one was open for 6% of the time, Pallas kernels for 15%

profile of v7, /device:TPU:8, one launch (start us, length us, event | category | flops | bytes accessed | tf_op | source)
XLA Modules:
  0.0 50.2 jit_solution(9769010261171015926)
XLA Ops:
  0.6 1.1 %fusion.9 = (f32[10,8,1,128]{3,2,1,0:T(1,128)S(1)}, f32[10,8,1,128]{3,2,1,0:T(1,128)S(1)}) fusion(f32[10,8,8,128]{3,2,1,0:T(8,128)} %param.8), kind=kLoop, calls=%fused_computation.27 | loop fusion | bytes 163840 | tf_op jit(solution)/shard_map/slice | solution.py:256
  1.8 1.1 %fusion.8 = (f32[10,8,2,128]{3,2,1,0:T(2,128)S(1)}, f32[10,8,2,128]{3,2,1,0:T(2,128)S(1)}) fusion(f32[10,8,8,128]{3,2,1,0:T(8,128)} %u_ref.1), kind=kLoop, calls=%fused_computation.26 | loop fusion | bytes 327680 | tf_op jit(solution)/shard_map/slice | solution.py:256
  2.9 0.0 copy-start
  2.9 0.2 fusion.1
  3.1 3.5 %collective-permute-start = (f32[10,8,3,128]{3,2,1,0:T(4,128)S(1)}, f32[10,8,3,128]{3,2,1,0:T(4,128)S(1)}, u32[]{:S(2)}, u32[]{:S(2)}) collective-permute-start(f32[10,8,3,128]{3,2,1,0:T(4,128)S(1)} %get-tuple-element.28), channel_id=1, source_target_pairs={{0,31},{1,2},{2,1},{3,4},{4,3},{5,6},{6,5},{7,8},{8,7},{9,10},{10,... | collective-permute-start | bytes 368648 | tf_op jit(solution)/shard_map/ppermute | solution.py:243
  6.6 9.8 %collective-permute-start.1 = (f32[10,8,3,128]{3,2,1,0:T(4,128)S(1)}, f32[10,8,3,128]{3,2,1,0:T(4,128)S(1)}, u32[]{:S(2)}, u32[]{:S(2)}) collective-permute-start(f32[10,8,3,128]{3,2,1,0:T(4,128)S(1)} %get-tuple-element.29), channel_id=1, source_target_pairs={{0,1},{1,0},{2,3},{3,2},{4,5},{5,4},{6,7},{7,6},{8,9},{9,8},{10,11... | collective-permute-start | bytes 368648 | tf_op jit(solution)/shard_map/ppermute | solution.py:242
  16.4 0.0 copy-done
  16.5 0.0 copy-start.4
  16.5 0.1 pad.27.clone
  16.6 0.6 %copy-done.4 = s32[8,8]{1,0:T(8,128)S(1)} copy-done((s32[8,8]{1,0:T(8,128)S(1)}, s32[8,8]{1,0:T(8,128)}, u32[]{:S(2)}) %copy-start.4) | copy-done | bytes 280
  17.1 0.7 %broadcast_in_dim.2.cnt_ref = s32[8,8,128]{2,1,0:T(8,128)} broadcast(s32[8,8]{1,0:T(8,128)S(1)} %copy-done.4), dimensions={0,1} | broadcast | bytes 33024 | tf_op jit(solution)/shard_map/broadcast_in_dim | solution.py:251
  17.8 0.0 copy-start.2
  17.8 3.7 %shard_map.87.early_ref = f32[10,8,8,128]{3,2,1,0:T(8,128)} custom-call(f32[21]{0:T(128)} %rate_ref.5, f32[21]{0:T(128)} %act_ref.5, f32[21]{0:T(128)} %heat_ref.5, f32[10,8,8,128]{3,2,1,0:T(8,128)} %u_ref.1, s32[8,8,128]{2,1,0:T(8,128)} %broadcast_in_dim.2.cnt_ref), custom_call_target="tpu_custom_call" | custom-call | tf_op jit(solution)/shard_map/pallas_call | solution.py:222
  21.5 0.0 copy-done.2
  21.5 0.0 collective-permute-done
  21.5 0.0 collective-permute-done.1
  21.5 0.1 broadcast_select_fusion.3
  21.7 0.0 copy-start.1
  21.7 0.1 fusion.2
  21.8 1.9 %collective-permute-start.3 = (f32[10,4,8,128]{3,2,1,0:T(8,128)S(1)}, f32[10,4,8,128]{3,2,1,0:T(8,128)S(1)}, u32[]{:S(2)}, u32[]{:S(2)}) collective-permute-start(f32[10,4,8,128]{3,2,1,0:T(8,128)S(1)} %get-tuple-element.26), channel_id=1, source_target_pairs={{0,32},{32,0},{64,96},{96,64},{128,160},{160,128},{192,224},{224,1... | collective-permute-start | bytes 491528 | tf_op jit(solution)/shard_map/ppermute | solution.py:242
  23.8 14.0 %collective-permute-start.2 = (f32[10,4,8,128]{3,2,1,0:T(8,128)S(1)}, f32[10,4,8,128]{3,2,1,0:T(8,128)S(1)}, u32[]{:S(2)}, u32[]{:S(2)}) collective-permute-start(f32[10,4,8,128]{3,2,1,0:T(8,128)S(1)} %get-tuple-element.27), channel_id=1, source_target_pairs={{0,736},{32,64},{64,32},{96,128},{128,96},{160,192},{192,160},{224... | collective-permute-start | bytes 491528 | tf_op jit(solution)/shard_map/ppermute | solution.py:243
  37.8 0.0 copy-done.1
  37.8 1.0 %pad_maximum_fusion.wide_ref = f32[10,8,12,128]{3,2,1,0:T(8,128)} fusion(f32[10,8,2,128]{3,2,1,0:T(2,128)S(1)} %slice.109, f32[10,8,8,128]{3,2,1,0:T(8,128)S(1)} %copy-done.1, f32[10,8,2,128]{3,2,1,0:T(2,128)S(1)} %slice.108), kind=kLoop, calls=%fused_computation.1 | loop fusion | flops 245760 | bytes 983040 | tf_op jit(solution)/shard_map/concatenate | solution.py:259
  38.9 1.0 %pad_maximum_fusion.1.wsrc_ref = f32[10,8,10,128]{3,2,1,0:T(8,128)} fusion(f32[10,8,1,128]{3,2,1,0:T(1,128)S(1)} %slice.111, f32[10,8,8,128]{3,2,1,0:T(8,128)S(1)} %copy-done.2, f32[10,8,1,128]{3,2,1,0:T(1,128)S(1)} %slice.110), kind=kLoop, calls=%fused_computation.2 | loop fusion | flops 204800 | bytes 819200 | tf_op jit(solution)/shard_map/concatenate | solution.py:260
  39.9 4.0 %shard_map.86 = (f32[10,10,16,128]{3,2,1,0:T(8,128)}, f32[10,8,8,128]{3,2,1,0:T(8,128)}) custom-call(f32[10]{0:T(128)} %diff_ref.3, f32[21]{0:T(128)} %rate_ref.5, f32[21]{0:T(128)} %act_ref.5, f32[21]{0:T(128)} %heat_ref.5, f32[10,8,12,128]{3,2,1,0:T(8,128)} %pad_maximum_fusion.wide_ref, f32[10,8,10,128]{3,2,1,0:T(8,128)} %pad_maximum_fusion.1.wsrc_ref, ...), custom_call_target="tpu_custom_call" | custom-call | tf_op jit(solution)/shard_map/pallas_call | solution.py:194
  43.9 0.0 collective-permute-done.3
  43.9 0.8 %collective-permute-done.2 = f32[10,4,8,128]{3,2,1,0:T(8,128)S(1)} collective-permute-done((f32[10,4,8,128]{3,2,1,0:T(8,128)S(1)}, f32[10,4,8,128]{3,2,1,0:T(8,128)S(1)}, u32[]{:S(2)}, u32[]{:S(2)}) %collective-permute-start.2) | collective-permute-done | bytes 163872 | tf_op jit(solution)/shard_map/ppermute | solution.py:243
  44.8 0.2 concatenate.57
  45.0 0.1 constant_dynamic-update-slice_fusion.1
  45.1 0.2 concatenate.58
  45.4 0.0 copy-start.3
  45.4 1.2 %maximum_maximum_fusion.src_ref = f32[10,10,10,128]{3,2,1,0:T(8,128)} fusion(f32[10,1,1,128]{3,2,1,0:T(1,128)S(1)} %broadcast.14, f32[10,1,8,128]{3,2,1,0:T(8,128)S(1)} %get-tuple-element.33, f32[10,8,1,128]{3,2,1,0:T(1,128)S(1)} %slice.111, f32[10,8,8,128]{3,2,1,0:T(8,128)S(1)} %copy-done.2, f32[10,8,1,128]{3,2,1,0:T(1,128)S(1)} %slice.110, ...), kind=kLoop, calls=%fused_computation | loop fusion | flops 1024000 | bytes 1008640 | tf_op jit(solution)/shard_map/concatenate | solution.py:290
  46.6 0.0 copy-done.3
  46.6 3.6 %shard_map.88 = (f32[10,8,8,128]{3,2,1,0:T(8,128)}, f32[10,8,8,128]{3,2,1,0:T(8,128)}) custom-call(f32[10]{0:T(128)} %diff_ref.3, f32[21]{0:T(128)} %rate_ref.5, f32[21]{0:T(128)} %act_ref.5, f32[21]{0:T(128)} %heat_ref.5, f32[10,12,12,128]{3,2,1,0:T(8,128)} %copy-done.3, f32[10,10,10,128]{3,2,1,0:T(8,128)} %maximum_maximum_fusion.src_ref, ...), custom_call_target="tpu_custom_call" | custom-call | tf_op jit(solution)/shard_map/pallas_call | solution.py:210
  (19 shorter events, 0.3 us)
Async XLA Ops:
  2.9 13.5 %copy-start = (f32[10,8,8,128]{3,2,1,0:T(8,128)S(1)}, f32[10,8,8,128]{3,2,1,0:T(8,128)}, u32[]{:S(2)}) copy-start(f32[10,8,8,128]{3,2,1,0:T(8,128)} %u_ref.1) | copy-start | bytes 983044
  3.1 18.4 %collective-permute-start = (f32[10,8,3,128]{3,2,1,0:T(4,128)S(1)}, f32[10,8,3,128]{3,2,1,0:T(4,128)S(1)}, u32[]{:S(2)}, u32[]{:S(2)}) collective-permute-start(f32[10,8,3,128]{3,2,1,0:T(4,128)S(1)} %get-tuple-element.28), channel_id=1, source_target_pairs={{0,31},{1,2},{2,1},{3,4},{4,3},{5,6},{6,5},{7,8},{8,7},{9,10},{10,... | collective-permute-start | bytes 368648 | tf_op jit(solution)/shard_map/ppermute | solution.py:243
  6.6 14.9 %collective-permute-start.1 = (f32[10,8,3,128]{3,2,1,0:T(4,128)S(1)}, f32[10,8,3,128]{3,2,1,0:T(4,128)S(1)}, u32[]{:S(2)}, u32[]{:S(2)}) collective-permute-start(f32[10,8,3,128]{3,2,1,0:T(4,128)S(1)} %get-tuple-element.29), channel_id=1, source_target_pairs={{0,1},{1,0},{2,3},{3,2},{4,5},{5,4},{6,7},{7,6},{8,9},{9,8},{10,11... | collective-permute-start | bytes 368648 | tf_op jit(solution)/shard_map/ppermute | solution.py:242
  16.5 0.7 %copy-start.4 = (s32[8,8]{1,0:T(8,128)S(1)}, s32[8,8]{1,0:T(8,128)}, u32[]{:S(2)}) copy-start(s32[8,8]{1,0:T(8,128)} %param.9) | copy-start | bytes 772
  17.8 3.7 %copy-start.2 = (f32[10,8,8,128]{3,2,1,0:T(8,128)S(1)}, f32[10,8,8,128]{3,2,1,0:T(8,128)}, u32[]{:S(2)}) copy-start(f32[10,8,8,128]{3,2,1,0:T(8,128)} %param.8) | copy-start | bytes 983044
  21.7 16.1 %copy-start.1 = (f32[10,8,8,128]{3,2,1,0:T(8,128)S(1)}, f32[10,8,8,128]{3,2,1,0:T(8,128)}, u32[]{:S(2)}) copy-start(f32[10,8,8,128]{3,2,1,0:T(8,128)} %u_ref.1) | copy-start | bytes 983044
  21.8 22.1 %collective-permute-start.3 = (f32[10,4,8,128]{3,2,1,0:T(8,128)S(1)}, f32[10,4,8,128]{3,2,1,0:T(8,128)S(1)}, u32[]{:S(2)}, u32[]{:S(2)}) collective-permute-start(f32[10,4,8,128]{3,2,1,0:T(8,128)S(1)} %get-tuple-element.26), channel_id=1, source_target_pairs={{0,32},{32,0},{64,96},{96,64},{128,160},{160,128},{192,224},{224,1... | collective-permute-start | bytes 491528 | tf_op jit(solution)/shard_map/ppermute | solution.py:242
  23.8 20.9 %collective-permute-start.2 = (f32[10,4,8,128]{3,2,1,0:T(8,128)S(1)}, f32[10,4,8,128]{3,2,1,0:T(8,128)S(1)}, u32[]{:S(2)}, u32[]{:S(2)}) collective-permute-start(f32[10,4,8,128]{3,2,1,0:T(8,128)S(1)} %get-tuple-element.27), channel_id=1, source_target_pairs={{0,736},{32,64},{64,32},{96,128},{128,96},{160,192},{192,160},{224... | collective-permute-start | bytes 491528 | tf_op jit(solution)/shard_map/ppermute | solution.py:243
  45.4 1.2 %copy-start.3 = (f32[10,12,12,128]{3,2,1,0:T(8,128)}, f32[10,12,12,128]{3,2,1,0:T(8,128)S(1)}, u32[]{:S(2)}) copy-start(f32[10,12,12,128]{3,2,1,0:T(8,128)S(1)} %fusion.5.ext_ref) | copy-start | bytes 2211844

commit v8 on v5

--- a/solution.py
+++ b/solution.py
@@ -54,7 +54,7 @@
     stride = time_step / cnt.astype(jnp.float32)
     cur = list(start)
     for turn in range(CMAX):
-        active = turn < cnt
+        step = jnp.where(turn < cnt, stride, 0.0)
         rates = []
         for r, entry in enumerate(reaction_table):
             term = coeffs[r] * cur[entry[0]]
@@ -78,11 +78,11 @@
             if total is None:
                 new.append(cur[s])
             else:
-                new.append(jnp.where(active, cur[s] + stride * total, cur[s]))
+                new.append(cur[s] + step * total)
         heat_total = heat[0] * rates[0]
         for r in range(1, reactions):
             heat_total = heat_total + heat[r] * rates[r]
-        new.append(jnp.where(active, cur[SPECIES] + stride * heat_total, cur[SPECIES]))
+        new.append(cur[SPECIES] + step * heat_total)
         cur = new
     return [(cur[s] - start[s]) / time_step for s in range(len(start))]
 
@@ -101,11 +101,22 @@
 
 
 def finish_kernel(
-    diff_ref, rate_ref, act_ref, heat_ref, ext_ref, src_ref, early_ref, cnt_ref,
-    next_ref, late_ref, first_ref,
+    diff_ref, rate_ref, act_ref, heat_ref, wide_ref, wsrc_ref, ym_ref, yp_ref,
+    early_ref, cnt_ref, next_ref, late_ref, ext_ref, src_ref, first_ref,
 ):
     rows, cx, cy, _ = early_ref.shape
     lanes = ext_ref.shape[3]
+    ext_ref[...] = jnp.zeros(ext_ref.shape, jnp.float32)
+    src_ref[...] = jnp.zeros(src_ref.shape, jnp.float32)
+    for r in range(rows):
+        for e in range(cx + 4):
+            ext_ref[r, e, pl.ds(2, cy)] = wide_ref[r, e]
+        for i in range(cx + 2):
+            ext_ref[r, i + 1, pl.ds(0, 2)] = ym_ref[r, i, pl.ds(0, 2)]
+            ext_ref[r, i + 1, pl.ds(cy + 2, 2)] = yp_ref[r, i, pl.ds(0, 2)]
+            src_ref[r, i, pl.ds(1, cy)] = wsrc_ref[r, i]
+            src_ref[r, i, pl.ds(0, 1)] = ym_ref[r, i, pl.ds(2, 1)]
+            src_ref[r, i, pl.ds(cy + 1, 1)] = yp_ref[r, i, pl.ds(2, 1)]
 
     def laplace(centre, xm, xp, ym, yp):
         beside = xm + xp
@@ -156,7 +167,7 @@
     lax.fori_loop(0, cx, box_row, 0)
 
 
-def finish(ext, src, early, cell_counts, diffusivity, log_rate, activation, heat_release):
+def finish(wide, wide_src, from_ym, from_yp, early, cell_counts, diffusivity, log_rate, activation, heat_release):
     rows, cx, cy, cz = early.shape
     smem = pl.BlockSpec(memory_space=pltpu.SMEM)
     vmem = pl.BlockSpec(memory_space=pltpu.VMEM)
@@ -164,10 +175,17 @@
     return pl.pallas_call(
         finish_kernel,
         out_shape=(box, box),
-        in_specs=[smem, smem, smem, smem, vmem, vmem, vmem, vmem],
+        in_specs=[smem, smem, smem, smem] + [vmem] * 6,
         out_specs=(vmem, vmem),
-        scratch_shapes=[pltpu.VMEM((rows, cx + 2, 2 * cy, cz), jnp.float32)],
-    )(diffusivity, log_rate, activation, heat_release, ext, src, early, cell_counts)
+        scratch_shapes=[
+            pltpu.VMEM((rows, cx + 4, 2 * cy, cz), jnp.float32),
+            pltpu.VMEM((rows, cx + 2, 2 * cy, cz), jnp.float32),
+            pltpu.VMEM((rows, cx + 2, 2 * cy, cz), jnp.float32),
+        ],
+    )(
+        diffusivity, log_rate, activation, heat_release,
+        wide, wide_src, from_ym, from_yp, early, cell_counts,
+    )
 
 
 def chemistry(fields, cell_counts, log_rate, activation, heat_release):
@@ -218,17 +236,9 @@
     to_ym = jnp.concatenate([wide[:, 1:-1, :2], wide_src[:, :, :1]], 2)
     to_yp = jnp.concatenate([wide[:, 1:-1, cy - 2:], wide_src[:, :, cy - 1:]], 2)
     from_ym, from_yp = exchange(to_ym, to_yp, "gy", ny)
-    ext = jnp.concatenate(
-        [
-            jnp.concatenate([zeros(1, 2), wide[:, :1], zeros(1, 2)], 2),
-            jnp.concatenate([from_ym[:, :, :2], wide[:, 1:-1], from_yp[:, :, :2]], 2),
-            jnp.concatenate([zeros(1, 2), wide[:, -1:], zeros(1, 2)], 2),
-        ],
-        1,
-    )
-    src = jnp.concatenate([from_ym[:, :, 2:], wide_src, from_yp[:, :, 2:]], 2)
     next_state, late_source = finish(
-        ext, src, early, cell_counts, diffusivity, log_rate, activation, heat_release
+        wide, wide_src, from_ym, from_yp, early, cell_counts,
+        diffusivity, log_rate, activation, heat_release,
     )
     return (next_state, late_source)
 

time: 48.8 us -> 48.7 us (level)
  other arithmetic: 2.59 us -> 1.12 us
  local copies, waits for them, and re-layouts: 3.67 us -> 5.04 us
    concatenate x2, other arithmetic: 2.25 us -> 0.06 us  [the longest x1 0.03 us: local(): wide = jnp.concatenate([from_xm[:, :2], state, from_xp[:, :2]], 1)]
    unnamed x8 -> x10, local copies, waits for them, and re-layouts: 1.02 us -> 2.46 us
    select_n x2, other arithmetic: 0.09 us -> 0.84 us  [exchange(): return (jnp.where(even, second, first), jnp.where(even, first, second))]
  transfers between devices with their start and end apart: 4 -> 4, of which waited for: 1 -> 2; matrix products, arithmetic and copies ran while one was open for 1% -> 1% of each run, Pallas kernels for 8% -> 7%
where the time goes in v8:
time: 48.7 us; the launch traced here: 48.3 us
  starting transfers between devices  27.6 us (57%)
  Pallas kernels  9.09 us (19%)
  local copies, waits for them, and re-layouts  5.04 us (10%)
  waiting for transfers between devices  4.64 us (10%)
  other arithmetic  1.12 us (2%)
  between operations  0.83 us (2%)
    ppermute x2, starting transfers between devices, exchange(): second = lax.ppermute(jnp.where(even, to_lo, to_hi), axis, outer)  22.2 us
    pallas_call x1, Pallas kernels, finish(): pl.pallas_call(finish_kernel, out_shape=(box, box), in_specs=[smem, smem,...  5.61 us
    ppermute x2, starting transfers between devices, exchange(): first = lax.ppermute(jnp.where(even, to_hi, to_lo), axis, inner)  5.39 us
    ppermute x2, waiting for transfers between devices, exchange(): second = lax.ppermute(jnp.where(even, to_lo, to_hi), axis, outer)  4.63 us
    pallas_call x1, Pallas kernels, chemistry(): pl.pallas_call(chem_kernel, out_shape=jax.ShapeDtypeStruct(fields.shape,...  3.48 us
    unnamed x10, local copies, waits for them, and re-layouts  2.46 us
    slice x2, local copies, waits for them, and re-layouts, local(): to_xm = jnp.concatenate([state[:, :2], source_in[:, :1]], 1)  1.75 us
  transfers between devices with their start and end apart: 4, of which 2 were waited for; matrix products, arithmetic and copies ran while one was open for 1% of the time, Pallas kernels for 7%

profile of v8, /device:TPU:6, one launch (start us, length us, event | category | flops | bytes accessed | tf_op | source)
XLA Modules:
  0.0 48.3 jit_solution(12448437784692209306)
XLA Ops:
  0.6 0.8 %fusion.7 = (f32[10,1,8,128]{3,2,1,0:T(8,128)S(1)}, f32[10,1,8,128]{3,2,1,0:T(8,128)S(1)}) fusion(f32[10,8,8,128]{3,2,1,0:T(8,128)} %param.8), kind=kLoop, calls=%fused_computation.17 | loop fusion | bytes 163840 | tf_op jit(solution)/shard_map/slice | solution.py:225
  1.5 0.9 %fusion.6 = (f32[10,2,8,128]{3,2,1,0:T(8,128)S(1)}, f32[10,2,8,128]{3,2,1,0:T(8,128)S(1)}) fusion(f32[10,8,8,128]{3,2,1,0:T(8,128)} %u_ref.1), kind=kLoop, calls=%fused_computation.16 | loop fusion | bytes 327680 | tf_op jit(solution)/shard_map/slice | solution.py:225
  2.4 14.3 %collective-permute-start = (f32[10,3,8,128]{3,2,1,0:T(8,128)S(1)}, f32[10,3,8,128]{3,2,1,0:T(8,128)S(1)}, u32[]{:S(2)}, u32[]{:S(2)}) collective-permute-start(f32[10,3,8,128]{3,2,1,0:T(8,128)S(1)} %get-tuple-element.16), channel_id=1, source_target_pairs={{0,736},{32,64},{64,32},{96,128},{128,96},{160,192},{192,160},{224... | collective-permute-start | bytes 368648 | tf_op jit(solution)/shard_map/ppermute | solution.py:215
  16.7 1.9 %collective-permute-start.1 = (f32[10,3,8,128]{3,2,1,0:T(8,128)S(1)}, f32[10,3,8,128]{3,2,1,0:T(8,128)S(1)}, u32[]{:S(2)}, u32[]{:S(2)}) collective-permute-start(f32[10,3,8,128]{3,2,1,0:T(8,128)S(1)} %get-tuple-element.17), channel_id=1, source_target_pairs={{0,32},{32,0},{64,96},{96,64},{128,160},{160,128},{192,224},{224,1... | collective-permute-start | bytes 368648 | tf_op jit(solution)/shard_map/ppermute | solution.py:214
  18.6 4.5 %collective-permute-done = f32[10,3,8,128]{3,2,1,0:T(8,128)S(1)} collective-permute-done((f32[10,3,8,128]{3,2,1,0:T(8,128)S(1)}, f32[10,3,8,128]{3,2,1,0:T(8,128)S(1)}, u32[]{:S(2)}, u32[]{:S(2)}) %collective-permute-start) | collective-permute-done | bytes 122912 | tf_op jit(solution)/shard_map/ppermute | solution.py:215
  23.1 0.0 collective-permute-done.1
  23.1 0.0 copy-start.2
  23.2 0.9 %copy-done.2 = f32[10,8,8,128]{3,2,1,0:T(8,128)S(1)} copy-done((f32[10,8,8,128]{3,2,1,0:T(8,128)S(1)}, f32[10,8,8,128]{3,2,1,0:T(8,128)}, u32[]{:S(2)}) %copy-start.2) | copy-done | bytes 327704
  24.1 0.0 copy-start
  24.2 0.0 copy-start.3
  24.2 0.1 fusion.4
  24.2 1.1 %copy-done.3 = f32[10,8,8,128]{3,2,1,0:T(8,128)S(1)} copy-done((f32[10,8,8,128]{3,2,1,0:T(8,128)S(1)}, f32[10,8,8,128]{3,2,1,0:T(8,128)}, u32[]{:S(2)}) %copy-start.3) | copy-done | bytes 327704
  25.3 0.0 copy-done
  25.3 0.0 copy-start.1
  25.4 0.1 fusion.5
  25.4 0.0 copy-start.4
  25.4 0.2 fusion
  25.6 0.5 copy-done.1
  26.1 3.5 %collective-permute-start.3 = (f32[10,10,3,128]{3,2,1,0:T(4,128)S(1)}, f32[10,10,3,128]{3,2,1,0:T(4,128)S(1)}, u32[]{:S(2)}, u32[]{:S(2)}) collective-permute-start(f32[10,10,3,128]{3,2,1,0:T(4,128)S(1)} %get-tuple-element.12), channel_id=1, source_target_pairs={{0,1},{1,0},{2,3},{3,2},{4,5},{5,4},{6,7},{7,6},{8,9},{9,8},{10,11... | collective-permute-start | bytes 460808 | tf_op jit(solution)/shard_map/ppermute | solution.py:214
  29.6 7.9 %collective-permute-start.2 = (f32[10,10,3,128]{3,2,1,0:T(4,128)S(1)}, f32[10,10,3,128]{3,2,1,0:T(4,128)S(1)}, u32[]{:S(2)}, u32[]{:S(2)}) collective-permute-start(f32[10,10,3,128]{3,2,1,0:T(4,128)S(1)} %get-tuple-element.13), channel_id=1, source_target_pairs={{0,31},{1,2},{2,1},{3,4},{4,3},{5,6},{6,5},{7,8},{8,7},{9,10},{10,... | collective-permute-start | bytes 460808 | tf_op jit(solution)/shard_map/ppermute | solution.py:215
  37.5 0.0 copy-done.4
  37.5 0.7 %broadcast_in_dim.2.cnt_ref = s32[8,8,128]{2,1,0:T(8,128)} broadcast(s32[8,8]{1,0:T(8,128)S(1)} %copy-done.4), dimensions={0,1} | broadcast | bytes 33024 | tf_op jit(solution)/shard_map/broadcast_in_dim | solution.py:223
  38.2 3.5 %shard_map.86.early_ref = f32[10,8,8,128]{3,2,1,0:T(8,128)} custom-call(f32[21]{0:T(128)} %rate_ref.3, f32[21]{0:T(128)} %act_ref.3, f32[21]{0:T(128)} %heat_ref.3, f32[10,8,8,128]{3,2,1,0:T(8,128)} %u_ref.1, s32[8,8,128]{2,1,0:T(8,128)} %broadcast_in_dim.2.cnt_ref), custom_call_target="tpu_custom_call" | custom-call | tf_op jit(solution)/shard_map/pallas_call | solution.py:194
  41.7 0.0 collective-permute-done.3
  41.7 0.2 collective-permute-done.2
  41.9 0.8 %broadcast_select_fusion = (f32[10,10,3,128]{3,2,1,0:T(4,128)}, f32[10,10,3,128]{3,2,1,0:T(4,128)}) fusion(f32[10,10,3,128]{3,2,1,0:T(4,128)S(1)} %collective-permute-done.3, f32[10,10,3,128]{3,2,1,0:T(4,128)S(1)} %collective-permute-done.2, pred[]{:T(512)S(6)} %eq.10), kind=kLoop, calls=%fused_computation.8 | loop fusion | flops 76800 | bytes 614401 | tf_op jit(solution)/shard_map/jit(_where)/select_n | solution.py:216
  42.7 5.6 %shard_map.87 = (f32[10,8,8,128]{3,2,1,0:T(8,128)}, f32[10,8,8,128]{3,2,1,0:T(8,128)}) custom-call(f32[10]{0:T(128)} %diff_ref.1, f32[21]{0:T(128)} %rate_ref.3, f32[21]{0:T(128)} %act_ref.3, f32[21]{0:T(128)} %heat_ref.3, f32[10,12,8,128]{3,2,1,0:T(8,128)} %copy-done, f32[10,10,8,128]{3,2,1,0:T(8,128)} %copy-done.1, ...), custom_call_target="tpu_custom_call" | custom-call | tf_op jit(solution)/shard_map/pallas_call | solution.py:175
  (8 shorter events, 0.1 us)
Async XLA Ops:
  2.4 20.7 %collective-permute-start = (f32[10,3,8,128]{3,2,1,0:T(8,128)S(1)}, f32[10,3,8,128]{3,2,1,0:T(8,128)S(1)}, u32[]{:S(2)}, u32[]{:S(2)}) collective-permute-start(f32[10,3,8,128]{3,2,1,0:T(8,128)S(1)} %get-tuple-element.16), channel_id=1, source_target_pairs={{0,736},{32,64},{64,32},{96,128},{128,96},{160,192},{192,160},{224... | collective-permute-start | bytes 368648 | tf_op jit(solution)/shard_map/ppermute | solution.py:215
  16.7 6.4 %collective-permute-start.1 = (f32[10,3,8,128]{3,2,1,0:T(8,128)S(1)}, f32[10,3,8,128]{3,2,1,0:T(8,128)S(1)}, u32[]{:S(2)}, u32[]{:S(2)}) collective-permute-start(f32[10,3,8,128]{3,2,1,0:T(8,128)S(1)} %get-tuple-element.17), channel_id=1, source_target_pairs={{0,32},{32,0},{64,96},{96,64},{128,160},{160,128},{192,224},{224,1... | collective-permute-start | bytes 368648 | tf_op jit(solution)/shard_map/ppermute | solution.py:214
  23.1 1.0 %copy-start.2 = (f32[10,8,8,128]{3,2,1,0:T(8,128)S(1)}, f32[10,8,8,128]{3,2,1,0:T(8,128)}, u32[]{:S(2)}) copy-start(f32[10,8,8,128]{3,2,1,0:T(8,128)} %u_ref.1) | copy-start | bytes 983044
  24.1 1.2 %copy-start = (f32[10,12,8,128]{3,2,1,0:T(8,128)}, f32[10,12,8,128]{3,2,1,0:T(8,128)S(1)}, u32[]{:S(2)}) copy-start(f32[10,12,8,128]{3,2,1,0:T(8,128)S(1)} %pad_maximum_fusion.wide_ref) | copy-start | bytes 1474564
  24.2 1.2 %copy-start.3 = (f32[10,8,8,128]{3,2,1,0:T(8,128)S(1)}, f32[10,8,8,128]{3,2,1,0:T(8,128)}, u32[]{:S(2)}) copy-start(f32[10,8,8,128]{3,2,1,0:T(8,128)} %param.8) | copy-start | bytes 983044
  25.3 0.8 %copy-start.1 = (f32[10,10,8,128]{3,2,1,0:T(8,128)}, f32[10,10,8,128]{3,2,1,0:T(8,128)S(1)}, u32[]{:S(2)}) copy-start(f32[10,10,8,128]{3,2,1,0:T(8,128)S(1)} %pad_maximum_fusion.1.wsrc_ref) | copy-start | bytes 1228804
  25.4 12.1 %copy-start.4 = (s32[8,8]{1,0:T(8,128)S(1)}, s32[8,8]{1,0:T(8,128)}, u32[]{:S(2)}) copy-start(s32[8,8]{1,0:T(8,128)} %param.9) | copy-start | bytes 772
  26.1 15.6 %collective-permute-start.3 = (f32[10,10,3,128]{3,2,1,0:T(4,128)S(1)}, f32[10,10,3,128]{3,2,1,0:T(4,128)S(1)}, u32[]{:S(2)}, u32[]{:S(2)}) collective-permute-start(f32[10,10,3,128]{3,2,1,0:T(4,128)S(1)} %get-tuple-element.12), channel_id=1, source_target_pairs={{0,1},{1,0},{2,3},{3,2},{4,5},{5,4},{6,7},{7,6},{8,9},{9,8},{10,11... | collective-permute-start | bytes 460808 | tf_op jit(solution)/shard_map/ppermute | solution.py:214
  29.6 12.3 %collective-permute-start.2 = (f32[10,10,3,128]{3,2,1,0:T(4,128)S(1)}, f32[10,10,3,128]{3,2,1,0:T(4,128)S(1)}, u32[]{:S(2)}, u32[]{:S(2)}) collective-permute-start(f32[10,10,3,128]{3,2,1,0:T(4,128)S(1)} %get-tuple-element.13), channel_id=1, source_target_pairs={{0,31},{1,2},{2,1},{3,4},{4,3},{5,6},{6,5},{7,8},{8,7},{9,10},{10,... | collective-permute-start | bytes 460808 | tf_op jit(solution)/shard_map/ppermute | solution.py:215

commit v9 on v8

--- a/solution.py
+++ b/solution.py
@@ -87,12 +87,21 @@
     return [(cur[s] - start[s]) / time_step for s in range(len(start))]
 
 
+def counts_tile(cnt_ref, x, shape):
+    sub = lax.broadcasted_iota(jnp.int32, shape, 0)
+    tile = jnp.zeros(shape, jnp.int32)
+    for y in range(shape[0]):
+        tile = jnp.where(sub == y, cnt_ref[x, y], tile)
+    return tile
+
+
 def chem_kernel(rate_ref, act_ref, heat_ref, u_ref, cnt_ref, o_ref):
     rows = u_ref.shape[0]
 
     def per_x(x, carry):
         start = [u_ref[s, x] for s in range(rows)]
-        out = react(start, cnt_ref[x], rate_ref, act_ref, heat_ref)
+        cnt = counts_tile(cnt_ref, x, start[0].shape)
+        out = react(start, cnt, rate_ref, act_ref, heat_ref)
         for s in range(rows):
             o_ref[s, x] = out[s]
         return carry
@@ -101,22 +110,27 @@
 
 
 def finish_kernel(
-    diff_ref, rate_ref, act_ref, heat_ref, wide_ref, wsrc_ref, ym_ref, yp_ref,
+    diff_ref, rate_ref, act_ref, heat_ref, par_ref, wide_ref, wsrc_ref, one_ref, two_ref,
     early_ref, cnt_ref, next_ref, late_ref, ext_ref, src_ref, first_ref,
 ):
     rows, cx, cy, _ = early_ref.shape
     lanes = ext_ref.shape[3]
+    even = par_ref[0] == 0
     ext_ref[...] = jnp.zeros(ext_ref.shape, jnp.float32)
     src_ref[...] = jnp.zeros(src_ref.shape, jnp.float32)
     for r in range(rows):
         for e in range(cx + 4):
             ext_ref[r, e, pl.ds(2, cy)] = wide_ref[r, e]
         for i in range(cx + 2):
-            ext_ref[r, i + 1, pl.ds(0, 2)] = ym_ref[r, i, pl.ds(0, 2)]
-            ext_ref[r, i + 1, pl.ds(cy + 2, 2)] = yp_ref[r, i, pl.ds(0, 2)]
+            one = one_ref[r, i]
+            two = two_ref[r, i]
+            ym = jnp.where(even, two, one)
+            yp = jnp.where(even, one, two)
+            ext_ref[r, i + 1, pl.ds(0, 2)] = ym[0:2]
+            ext_ref[r, i + 1, pl.ds(cy + 2, 2)] = yp[0:2]
             src_ref[r, i, pl.ds(1, cy)] = wsrc_ref[r, i]
-            src_ref[r, i, pl.ds(0, 1)] = ym_ref[r, i, pl.ds(2, 1)]
-            src_ref[r, i, pl.ds(cy + 1, 1)] = yp_ref[r, i, pl.ds(2, 1)]
+            src_ref[r, i, pl.ds(0, 1)] = ym[2:3]
+            src_ref[r, i, pl.ds(cy + 1, 1)] = yp[2:3]
 
     def laplace(centre, xm, xp, ym, yp):
         beside = xm + xp
@@ -159,7 +173,7 @@
                 centre + time_step * (diff_ref[r] * lap + early_ref[r, x])
             )
             start.append(centre)
-        out = react(start, cnt_ref[x], rate_ref, act_ref, heat_ref)
+        out = react(start, counts_tile(cnt_ref, x, centre.shape), rate_ref, act_ref, heat_ref)
         for r in range(rows):
             late_ref[r, x] = out[r]
         return carry
@@ -167,7 +181,7 @@
     lax.fori_loop(0, cx, box_row, 0)
 
 
-def finish(wide, wide_src, from_ym, from_yp, early, cell_counts, diffusivity, log_rate, activation, heat_release):
+def finish(parity, wide, wide_src, one, two, early, counts, diffusivity, log_rate, activation, heat_release):
     rows, cx, cy, cz = early.shape
     smem = pl.BlockSpec(memory_space=pltpu.SMEM)
     vmem = pl.BlockSpec(memory_space=pltpu.VMEM)
@@ -175,7 +189,7 @@
     return pl.pallas_call(
         finish_kernel,
         out_shape=(box, box),
-        in_specs=[smem, smem, smem, smem] + [vmem] * 6,
+        in_specs=[smem] * 5 + [vmem] * 5 + [smem],
         out_specs=(vmem, vmem),
         scratch_shapes=[
             pltpu.VMEM((rows, cx + 4, 2 * cy, cz), jnp.float32),
@@ -183,8 +197,8 @@
             pltpu.VMEM((rows, cx + 2, 2 * cy, cz), jnp.float32),
         ],
     )(
-        diffusivity, log_rate, activation, heat_release,
-        wide, wide_src, from_ym, from_yp, early, cell_counts,
+        diffusivity, log_rate, activation, heat_release, parity,
+        wide, wide_src, one, two, early, counts,
     )
 
 
@@ -194,7 +208,7 @@
     return pl.pallas_call(
         chem_kernel,
         out_shape=jax.ShapeDtypeStruct(fields.shape, jnp.float32),
-        in_specs=[smem, smem, smem, vmem, vmem],
+        in_specs=[smem, smem, smem, vmem, smem],
         out_specs=vmem,
     )(log_rate, activation, heat_release, fields, cell_counts)
 
@@ -203,7 +217,7 @@
     return [(i, (i + step) % size) for i in range(size)]
 
 
-def exchange(to_lo, to_hi, axis, size):
+def exchange(to_lo, to_hi, axis, size, raw=False):
     if size % 2:
         from_lo = lax.ppermute(to_hi, axis, shift_pairs(size, 1))
         from_hi = lax.ppermute(to_lo, axis, shift_pairs(size, -1))
@@ -213,6 +227,8 @@
     outer = [(i, (i - 1) % size if i % 2 == 0 else (i + 1) % size) for i in range(size)]
     first = lax.ppermute(jnp.where(even, to_hi, to_lo), axis, inner)
     second = lax.ppermute(jnp.where(even, to_lo, to_hi), axis, outer)
+    if raw:
+        return first, second
     return jnp.where(even, second, first), jnp.where(even, first, second)
 
 
@@ -220,13 +236,12 @@
     nx = lax.axis_size("gx")
     ny = lax.axis_size("gy")
     rows, cx, cy, cz = state.shape
-    cell_counts = jnp.broadcast_to(counts[:, :, None], (cx, cy, cz))
 
     to_xm = jnp.concatenate([state[:, :2], source_in[:, :1]], 1)
     to_xp = jnp.concatenate([state[:, cx - 2:], source_in[:, cx - 1:]], 1)
     from_xm, from_xp = exchange(to_xm, to_xp, "gx", nx)
 
-    early = chemistry(state, cell_counts, log_rate, activation, heat_release)
+    early = chemistry(state, counts, log_rate, activation, heat_release)
 
     def zeros(a, b):
         return jnp.zeros((rows, a, b, cz), jnp.float32)
@@ -235,9 +250,14 @@
     wide_src = jnp.concatenate([from_xm[:, 2:], source_in, from_xp[:, 2:]], 1)
     to_ym = jnp.concatenate([wide[:, 1:-1, :2], wide_src[:, :, :1]], 2)
     to_yp = jnp.concatenate([wide[:, 1:-1, cy - 2:], wide_src[:, :, cy - 1:]], 2)
-    from_ym, from_yp = exchange(to_ym, to_yp, "gy", ny)
+    if ny % 2:
+        one, two = exchange(to_ym, to_yp, "gy", ny)
+        parity = jnp.ones((1,), jnp.int32)
+    else:
+        one, two = exchange(to_ym, to_yp, "gy", ny, raw=True)
+        parity = (lax.axis_index("gy") % 2).astype(jnp.int32).reshape(1)
     next_state, late_source = finish(
-        wide, wide_src, from_ym, from_yp, early, cell_counts,
+        parity, wide, wide_src, one, two, early, counts,
         diffusivity, log_rate, activation, heat_release,
     )
     return (next_state, late_source)

time: 48.7 us -> 49 us (level)
  waiting for transfers between devices: 4.64 us -> 7.01 us
  starting transfers between devices: 27.6 us -> 26.3 us
  other arithmetic: 1.12 us -> 0.3 us
    ppermute x2, waiting for transfers between devices: 0.01 us -> 2.54 us  [exchange(): first = lax.ppermute(jnp.where(even, to_hi, to_lo), axis, inner)]
    ppermute x2, starting transfers between devices: 5.39 us -> 3.84 us  [exchange(): first = lax.ppermute(jnp.where(even, to_hi, to_lo), axis, inner)]
    select_n x2 -> x1, other arithmetic: 0.84 us -> 0.02 us  [exchange(): return (jnp.where(even, second, first), jnp.where(even, first, second))]
    broadcast_in_dim x1 -> x0, local copies, waits for them, and re-layouts: 0.68 us -> none  [local(): cell_counts = jnp.broadcast_to(counts[:, :, None], (cx, cy, cz))]
    unnamed x10 -> x12, local copies, waits for them, and re-layouts: 2.46 us -> 3.13 us
  transfers between devices with their start and end apart: 4 -> 4, of which waited for: 2 -> 2; matrix products, arithmetic and copies ran while one was open for 1% -> 0% of each run, Pallas kernels for 7% -> 7%
where the time goes in v9:
time: 49 us; the launch traced here: 48.6 us
  starting transfers between devices  26.3 us (54%)
  Pallas kernels  9.15 us (19%)
  waiting for transfers between devices  7.01 us (14%)
  local copies, waits for them, and re-layouts  5.03 us (10%)
  between operations  0.81 us (2%)
    ppermute x2, starting transfers between devices, exchange(): second = lax.ppermute(jnp.where(even, to_lo, to_hi), axis, outer)  22.4 us
    pallas_call x1, Pallas kernels, finish(): pl.pallas_call(finish_kernel, out_shape=(box, box), in_specs=[smem] * 5 +...  5.63 us
    ppermute x2, waiting for transfers between devices, exchange(): second = lax.ppermute(jnp.where(even, to_lo, to_hi), axis, outer)  4.47 us
    ppermute x2, starting transfers between devices, exchange(): first = lax.ppermute(jnp.where(even, to_hi, to_lo), axis, inner)  3.84 us
    pallas_call x1, Pallas kernels, chemistry(): pl.pallas_call(chem_kernel, out_shape=jax.ShapeDtypeStruct(fields.shape,...  3.52 us
    unnamed x12, local copies, waits for them, and re-layouts  3.13 us
    ppermute x2, waiting for transfers between devices, exchange(): first = lax.ppermute(jnp.where(even, to_hi, to_lo), axis, inner)  2.54 us
    slice x2, local copies, waits for them, and re-layouts, local(): to_xm = jnp.concatenate([state[:, :2], source_in[:, :1]], 1)  1.75 us
  transfers between devices with their start and end apart: 4, of which 2 were waited for; matrix products, arithmetic and copies ran while one was open for 0% of the time, Pallas kernels for 7%

profile of v9, /device:TPU:6, one launch (start us, length us, event | category | flops | bytes accessed | tf_op | source)
XLA Modules:
  0.0 48.6 jit_solution(16481192374068328147)
XLA Ops:
  0.6 0.8 %fusion.7 = (f32[10,1,8,128]{3,2,1,0:T(8,128)S(1)}, f32[10,1,8,128]{3,2,1,0:T(8,128)S(1)}) fusion(f32[10,8,8,128]{3,2,1,0:T(8,128)} %param.8), kind=kLoop, calls=%fused_computation.15 | loop fusion | bytes 163840 | tf_op jit(solution)/shard_map/slice | solution.py:240
  1.5 0.9 %fusion.6 = (f32[10,2,8,128]{3,2,1,0:T(8,128)S(1)}, f32[10,2,8,128]{3,2,1,0:T(8,128)S(1)}) fusion(f32[10,8,8,128]{3,2,1,0:T(8,128)} %u_ref.1), kind=kLoop, calls=%fused_computation.14 | loop fusion | bytes 327680 | tf_op jit(solution)/shard_map/slice | solution.py:240
  2.4 14.3 %collective-permute-start = (f32[10,3,8,128]{3,2,1,0:T(8,128)S(1)}, f32[10,3,8,128]{3,2,1,0:T(8,128)S(1)}, u32[]{:S(2)}, u32[]{:S(2)}) collective-permute-start(f32[10,3,8,128]{3,2,1,0:T(8,128)S(1)} %get-tuple-element.14), channel_id=1, source_target_pairs={{0,736},{32,64},{64,32},{96,128},{128,96},{160,192},{192,160},{224... | collective-permute-start | bytes 368648 | tf_op jit(solution)/shard_map/ppermute | solution.py:229
  16.7 1.9 %collective-permute-start.1 = (f32[10,3,8,128]{3,2,1,0:T(8,128)S(1)}, f32[10,3,8,128]{3,2,1,0:T(8,128)S(1)}, u32[]{:S(2)}, u32[]{:S(2)}) collective-permute-start(f32[10,3,8,128]{3,2,1,0:T(8,128)S(1)} %get-tuple-element.15), channel_id=1, source_target_pairs={{0,32},{32,0},{64,96},{96,64},{128,160},{160,128},{192,224},{224,1... | collective-permute-start | bytes 368648 | tf_op jit(solution)/shard_map/ppermute | solution.py:228
  18.6 4.5 %collective-permute-done = f32[10,3,8,128]{3,2,1,0:T(8,128)S(1)} collective-permute-done((f32[10,3,8,128]{3,2,1,0:T(8,128)S(1)}, f32[10,3,8,128]{3,2,1,0:T(8,128)S(1)}, u32[]{:S(2)}, u32[]{:S(2)}) %collective-permute-start) | collective-permute-done | bytes 122912 | tf_op jit(solution)/shard_map/ppermute | solution.py:229
  23.1 0.0 collective-permute-done.1
  23.1 0.0 copy-start.2
  23.2 0.9 %copy-done.2 = f32[10,8,8,128]{3,2,1,0:T(8,128)S(1)} copy-done((f32[10,8,8,128]{3,2,1,0:T(8,128)S(1)}, f32[10,8,8,128]{3,2,1,0:T(8,128)}, u32[]{:S(2)}) %copy-start.2) | copy-done | bytes 327704
  24.1 0.0 copy-start
  24.2 0.0 copy-start.3
  24.2 0.1 fusion.4
  24.2 1.1 %copy-done.3 = f32[10,8,8,128]{3,2,1,0:T(8,128)S(1)} copy-done((f32[10,8,8,128]{3,2,1,0:T(8,128)S(1)}, f32[10,8,8,128]{3,2,1,0:T(8,128)}, u32[]{:S(2)}) %copy-start.3) | copy-done | bytes 327704
  25.3 0.0 copy-done
  25.3 0.0 copy-start.1
  25.4 0.1 fusion.5
  25.4 0.2 fusion
  25.6 0.5 copy-done.1
  26.1 8.2 %collective-permute-start.3 = (f32[10,10,3,128]{3,2,1,0:T(4,128)S(1)}, f32[10,10,3,128]{3,2,1,0:T(4,128)S(1)}, u32[]{:S(2)}, u32[]{:S(2)}) collective-permute-start(f32[10,10,3,128]{3,2,1,0:T(4,128)S(1)} %get-tuple-element.10), channel_id=1, source_target_pairs={{0,31},{1,2},{2,1},{3,4},{4,3},{5,6},{6,5},{7,8},{8,7},{9,10},{10,... | collective-permute-start | bytes 460808 | tf_op jit(solution)/shard_map/ppermute | solution.py:229
  34.3 1.9 %collective-permute-start.2 = (f32[10,10,3,128]{3,2,1,0:T(4,128)S(1)}, f32[10,10,3,128]{3,2,1,0:T(4,128)S(1)}, u32[]{:S(2)}, u32[]{:S(2)}) collective-permute-start(f32[10,10,3,128]{3,2,1,0:T(4,128)S(1)} %get-tuple-element.11), channel_id=1, source_target_pairs={{0,1},{1,0},{2,3},{3,2},{4,5},{5,4},{6,7},{7,6},{8,9},{9,8},{10,11... | collective-permute-start | bytes 460808 | tf_op jit(solution)/shard_map/ppermute | solution.py:228
  36.2 3.5 %shard_map.86.early_ref = f32[10,8,8,128]{3,2,1,0:T(8,128)} custom-call(f32[21]{0:T(128)} %rate_ref.3, f32[21]{0:T(128)} %act_ref.3, f32[21]{0:T(128)} %heat_ref.3, f32[10,8,8,128]{3,2,1,0:T(8,128)} %u_ref.1, s32[8,8]{1,0:T(8,128)} %cnt_ref.3), custom_call_target="tpu_custom_call" | custom-call | tf_op jit(solution)/shard_map/pallas_call | solution.py:208
  39.7 0.0 collective-permute-done.3.two_ref
  39.7 0.0 copy-start.4
  39.7 2.5 %collective-permute-done.2.one_ref = f32[10,10,3,128]{3,2,1,0:T(4,128)S(1)} collective-permute-done((f32[10,10,3,128]{3,2,1,0:T(4,128)S(1)}, f32[10,10,3,128]{3,2,1,0:T(4,128)S(1)}, u32[]{:S(2)}, u32[]{:S(2)}) %collective-permute-start.2) | collective-permute-done | bytes 153632 | tf_op jit(solution)/shard_map/ppermute | solution.py:228
  42.3 0.0 copy-start.5
  42.3 0.0 copy-done.4
  42.3 0.7 %copy-done.5 = f32[10,10,3,128]{3,2,1,0:T(4,128)} copy-done((f32[10,10,3,128]{3,2,1,0:T(4,128)}, f32[10,10,3,128]{3,2,1,0:T(4,128)S(1)}, u32[]{:S(2)}) %copy-start.5) | copy-done | bytes 153624
  42.9 5.6 %shard_map.87 = (f32[10,8,8,128]{3,2,1,0:T(8,128)}, f32[10,8,8,128]{3,2,1,0:T(8,128)}) custom-call(f32[10]{0:T(128)} %diff_ref.1, f32[21]{0:T(128)} %rate_ref.3, f32[21]{0:T(128)} %act_ref.3, f32[21]{0:T(128)} %heat_ref.3, s32[1]{0:T(128)} %bitcast.par_ref, f32[10,12,8,128]{3,2,1,0:T(8,128)} %copy-done, f32[10,10,8,128]{3,2,1,0:T(8,128)} %copy-done.1, ...), custom_call_target="tpu_custom_call" | custom-call | tf_op jit(solution)/shard_map/pallas_call | solution.py:189
  (8 shorter events, 0.1 us)
Async XLA Ops:
  2.4 20.7 %collective-permute-start = (f32[10,3,8,128]{3,2,1,0:T(8,128)S(1)}, f32[10,3,8,128]{3,2,1,0:T(8,128)S(1)}, u32[]{:S(2)}, u32[]{:S(2)}) collective-permute-start(f32[10,3,8,128]{3,2,1,0:T(8,128)S(1)} %get-tuple-element.14), channel_id=1, source_target_pairs={{0,736},{32,64},{64,32},{96,128},{128,96},{160,192},{192,160},{224... | collective-permute-start | bytes 368648 | tf_op jit(solution)/shard_map/ppermute | solution.py:229
  16.7 6.4 %collective-permute-start.1 = (f32[10,3,8,128]{3,2,1,0:T(8,128)S(1)}, f32[10,3,8,128]{3,2,1,0:T(8,128)S(1)}, u32[]{:S(2)}, u32[]{:S(2)}) collective-permute-start(f32[10,3,8,128]{3,2,1,0:T(8,128)S(1)} %get-tuple-element.15), channel_id=1, source_target_pairs={{0,32},{32,0},{64,96},{96,64},{128,160},{160,128},{192,224},{224,1... | collective-permute-start | bytes 368648 | tf_op jit(solution)/shard_map/ppermute | solution.py:228
  23.1 1.0 %copy-start.2 = (f32[10,8,8,128]{3,2,1,0:T(8,128)S(1)}, f32[10,8,8,128]{3,2,1,0:T(8,128)}, u32[]{:S(2)}) copy-start(f32[10,8,8,128]{3,2,1,0:T(8,128)} %u_ref.1) | copy-start | bytes 983044
  24.1 1.2 %copy-start = (f32[10,12,8,128]{3,2,1,0:T(8,128)}, f32[10,12,8,128]{3,2,1,0:T(8,128)S(1)}, u32[]{:S(2)}) copy-start(f32[10,12,8,128]{3,2,1,0:T(8,128)S(1)} %pad_maximum_fusion.wide_ref) | copy-start | bytes 1474564
  24.2 1.2 %copy-start.3 = (f32[10,8,8,128]{3,2,1,0:T(8,128)S(1)}, f32[10,8,8,128]{3,2,1,0:T(8,128)}, u32[]{:S(2)}) copy-start(f32[10,8,8,128]{3,2,1,0:T(8,128)} %param.8) | copy-start | bytes 983044
  25.3 0.8 %copy-start.1 = (f32[10,10,8,128]{3,2,1,0:T(8,128)}, f32[10,10,8,128]{3,2,1,0:T(8,128)S(1)}, u32[]{:S(2)}) copy-start(f32[10,10,8,128]{3,2,1,0:T(8,128)S(1)} %pad_maximum_fusion.1.wsrc_ref) | copy-start | bytes 1228804
  26.1 13.6 %collective-permute-start.3 = (f32[10,10,3,128]{3,2,1,0:T(4,128)S(1)}, f32[10,10,3,128]{3,2,1,0:T(4,128)S(1)}, u32[]{:S(2)}, u32[]{:S(2)}) collective-permute-start(f32[10,10,3,128]{3,2,1,0:T(4,128)S(1)} %get-tuple-element.10), channel_id=1, source_target_pairs={{0,31},{1,2},{2,1},{3,4},{4,3},{5,6},{6,5},{7,8},{8,7},{9,10},{10,... | collective-permute-start | bytes 460808 | tf_op jit(solution)/shard_map/ppermute | solution.py:229
  34.3 8.0 %collective-permute-start.2 = (f32[10,10,3,128]{3,2,1,0:T(4,128)S(1)}, f32[10,10,3,128]{3,2,1,0:T(4,128)S(1)}, u32[]{:S(2)}, u32[]{:S(2)}) collective-permute-start(f32[10,10,3,128]{3,2,1,0:T(4,128)S(1)} %get-tuple-element.11), channel_id=1, source_target_pairs={{0,1},{1,0},{2,3},{3,2},{4,5},{5,4},{6,7},{7,6},{8,9},{9,8},{10,11... | collective-permute-start | bytes 460808 | tf_op jit(solution)/shard_map/ppermute | solution.py:228
  39.7 2.5 %copy-start.4 = (f32[10,10,3,128]{3,2,1,0:T(4,128)}, f32[10,10,3,128]{3,2,1,0:T(4,128)S(1)}, u32[]{:S(2)}) copy-start(f32[10,10,3,128]{3,2,1,0:T(4,128)S(1)} %collective-permute-done.3.two_ref) | copy-start | bytes 460804
  42.3 0.7 %copy-start.5 = (f32[10,10,3,128]{3,2,1,0:T(4,128)}, f32[10,10,3,128]{3,2,1,0:T(4,128)S(1)}, u32[]{:S(2)}) copy-start(f32[10,10,3,128]{3,2,1,0:T(4,128)S(1)} %collective-permute-done.2.one_ref) | copy-start | bytes 460804

commit v10 on v5

--- a/solution.py
+++ b/solution.py
@@ -87,12 +87,24 @@
     return [(cur[s] - start[s]) / time_step for s in range(len(start))]
 
 
-def chem_kernel(rate_ref, act_ref, heat_ref, u_ref, cnt_ref, o_ref):
+def counts_tile(cnt_ref, x, shape):
+    sub = lax.broadcasted_iota(jnp.int32, shape, 0)
+    tile = jnp.zeros(shape, jnp.int32)
+    for y in range(shape[0]):
+        tile = jnp.where(sub == y, cnt_ref[x, y], tile)
+    return tile
+
+
+def chem_kernel(rate_ref, act_ref, heat_ref, hbm_ref, cnt_ref, o_ref, u_ref, sem):
     rows = u_ref.shape[0]
+    copy = pltpu.make_async_copy(hbm_ref, u_ref, sem)
+    copy.start()
+    copy.wait()
 
     def per_x(x, carry):
         start = [u_ref[s, x] for s in range(rows)]
-        out = react(start, cnt_ref[x], rate_ref, act_ref, heat_ref)
+        cnt = counts_tile(cnt_ref, x, start[0].shape)
+        out = react(start, cnt, rate_ref, act_ref, heat_ref)
         for s in range(rows):
             o_ref[s, x] = out[s]
         return carry
@@ -148,7 +160,7 @@
                 centre + time_step * (diff_ref[r] * lap + early_ref[r, x])
             )
             start.append(centre)
-        out = react(start, cnt_ref[x], rate_ref, act_ref, heat_ref)
+        out = react(start, counts_tile(cnt_ref, x, centre.shape), rate_ref, act_ref, heat_ref)
         for r in range(rows):
             late_ref[r, x] = out[r]
         return carry
@@ -164,7 +176,7 @@
     return pl.pallas_call(
         finish_kernel,
         out_shape=(box, box),
-        in_specs=[smem, smem, smem, smem, vmem, vmem, vmem, vmem],
+        in_specs=[smem, smem, smem, smem, vmem, vmem, vmem, smem],
         out_specs=(vmem, vmem),
         scratch_shapes=[pltpu.VMEM((rows, cx + 2, 2 * cy, cz), jnp.float32)],
     )(diffusivity, log_rate, activation, heat_release, ext, src, early, cell_counts)
@@ -176,8 +188,12 @@
     return pl.pallas_call(
         chem_kernel,
         out_shape=jax.ShapeDtypeStruct(fields.shape, jnp.float32),
-        in_specs=[smem, smem, smem, vmem, vmem],
+        in_specs=[smem, smem, smem, pl.BlockSpec(memory_space=pl.ANY), smem],
         out_specs=vmem,
+        scratch_shapes=[
+            pltpu.VMEM(fields.shape, jnp.float32),
+            pltpu.SemaphoreType.DMA(()),
+        ],
     )(log_rate, activation, heat_release, fields, cell_counts)
 
 
@@ -202,7 +218,7 @@
     nx = lax.axis_size("gx")
     ny = lax.axis_size("gy")
     rows, cx, cy, cz = state.shape
-    cell_counts = jnp.broadcast_to(counts[:, :, None], (cx, cy, cz))
+    cell_counts = counts
 
     to_xm = jnp.concatenate([state[:, :2], source_in[:, :1]], 1)
     to_xp = jnp.concatenate([state[:, cx - 2:], source_in[:, cx - 1:]], 1)

time: 48.8 us -> 48.9 us (level)
  Pallas kernels: 9.21 us -> 9.99 us
  local copies, waits for them, and re-layouts: 3.67 us -> 2.98 us
    pallas_call x1, Pallas kernels: 3.65 us -> 4.39 us  [chemistry(): pl.pallas_call(chem_kernel, out_shape=jax.ShapeDtypeStruct(fields.shape,...]
    broadcast_in_dim x1 -> x0, local copies, waits for them, and re-layouts: 0.68 us -> none  [local(): cell_counts = jnp.broadcast_to(counts[:, :, None], (cx, cy, cz))]
    unnamed x8 -> x6, local copies, waits for them, and re-layouts: 1.02 us -> 1.01 us
  transfers between devices with their start and end apart: 4 -> 4, of which waited for: 1 -> 1; matrix products, arithmetic and copies ran while one was open for 1% -> 0% of each run, Pallas kernels for 8% -> 9%
where the time goes in v10:
time: 48.9 us; the launch traced here: 48.5 us
  starting transfers between devices  27.6 us (56%)
  Pallas kernels  9.99 us (20%)
  waiting for transfers between devices  4.47 us (9%)
  local copies, waits for them, and re-layouts  2.98 us (6%)
  other arithmetic  2.58 us (5%)
  between operations  0.83 us (2%)
    ppermute x2, starting transfers between devices, exchange(): second = lax.ppermute(jnp.where(even, to_lo, to_hi), axis, outer)  22.2 us
    pallas_call x1, Pallas kernels, finish(): pl.pallas_call(finish_kernel, out_shape=(box, box), in_specs=[smem, smem,...  5.6 us
    ppermute x2, starting transfers between devices, exchange(): first = lax.ppermute(jnp.where(even, to_hi, to_lo), axis, inner)  5.41 us
    ppermute x2, waiting for transfers between devices, exchange(): second = lax.ppermute(jnp.where(even, to_lo, to_hi), axis, outer)  4.47 us
    pallas_call x1, Pallas kernels, chemistry(): pl.pallas_call(chem_kernel, out_shape=jax.ShapeDtypeStruct(fields.shape,...  4.39 us
    slice x2, local copies, waits for them, and re-layouts, local(): to_xm = jnp.concatenate([state[:, :2], source_in[:, :1]], 1)  1.75 us
    concatenate x1, other arithmetic, local(): jnp.concatenate([jnp.concatenate([zeros(1, 2), wide[:, :1], zeros(1, 2)],...  1.13 us
    concatenate x1, other arithmetic, local(): src = jnp.concatenate([from_ym[:, :, 2:], wide_src, from_yp[:, :, 2:]], 2)  1.12 us
  transfers between devices with their start and end apart: 4, of which 1 were waited for; matrix products, arithmetic and copies ran while one was open for 0% of the time, Pallas kernels for 9%

profile of v10, /device:TPU:6, one launch (start us, length us, event | category | flops | bytes accessed | tf_op | source)
XLA Modules:
  0.0 48.5 jit_solution(16224795867525874124)
XLA Ops:
  0.6 0.8 %fusion.14 = (f32[10,1,8,128]{3,2,1,0:T(8,128)S(1)}, f32[10,1,8,128]{3,2,1,0:T(8,128)S(1)}) fusion(f32[10,8,8,128]{3,2,1,0:T(8,128)} %param.8), kind=kLoop, calls=%fused_computation.37 | loop fusion | bytes 163840 | tf_op jit(solution)/shard_map/slice | solution.py:223
  1.5 0.9 %fusion.13 = (f32[10,2,8,128]{3,2,1,0:T(8,128)S(1)}, f32[10,2,8,128]{3,2,1,0:T(8,128)S(1)}) fusion(f32[10,8,8,128]{3,2,1,0:T(8,128)} %hbm_ref.1), kind=kLoop, calls=%fused_computation.36 | loop fusion | bytes 327680 | tf_op jit(solution)/shard_map/slice | solution.py:223
  2.4 14.3 %collective-permute-start = (f32[10,3,8,128]{3,2,1,0:T(8,128)S(1)}, f32[10,3,8,128]{3,2,1,0:T(8,128)S(1)}, u32[]{:S(2)}, u32[]{:S(2)}) collective-permute-start(f32[10,3,8,128]{3,2,1,0:T(8,128)S(1)} %get-tuple-element.13), channel_id=1, source_target_pairs={{0,736},{32,64},{64,32},{96,128},{128,96},{160,192},{192,160},{224... | collective-permute-start | bytes 368648 | tf_op jit(solution)/shard_map/ppermute | solution.py:213
  16.7 1.9 %collective-permute-start.1 = (f32[10,3,8,128]{3,2,1,0:T(8,128)S(1)}, f32[10,3,8,128]{3,2,1,0:T(8,128)S(1)}, u32[]{:S(2)}, u32[]{:S(2)}) collective-permute-start(f32[10,3,8,128]{3,2,1,0:T(8,128)S(1)} %get-tuple-element.14), channel_id=1, source_target_pairs={{0,32},{32,0},{64,96},{96,64},{128,160},{160,128},{192,224},{224,1... | collective-permute-start | bytes 368648 | tf_op jit(solution)/shard_map/ppermute | solution.py:212
  18.6 4.5 %collective-permute-done = f32[10,3,8,128]{3,2,1,0:T(8,128)S(1)} collective-permute-done((f32[10,3,8,128]{3,2,1,0:T(8,128)S(1)}, f32[10,3,8,128]{3,2,1,0:T(8,128)S(1)}, u32[]{:S(2)}, u32[]{:S(2)}) %collective-permute-start) | collective-permute-done | bytes 122912 | tf_op jit(solution)/shard_map/ppermute | solution.py:213
  23.1 0.0 collective-permute-done.1
  23.1 0.0 copy-start
  23.1 0.0 copy-start.2
  23.2 0.9 %copy-done = f32[10,8,8,128]{3,2,1,0:T(8,128)S(1)} copy-done((f32[10,8,8,128]{3,2,1,0:T(8,128)S(1)}, f32[10,8,8,128]{3,2,1,0:T(8,128)}, u32[]{:S(2)}) %copy-start) | copy-done | bytes 327704
  24.1 0.1 copy-done.2
  24.2 0.2 broadcast_select_fusion.3
  24.4 0.1 broadcast_select_fusion.2
  24.4 3.5 %collective-permute-start.3 = (f32[10,10,3,128]{3,2,1,0:T(4,128)S(1)}, f32[10,10,3,128]{3,2,1,0:T(4,128)S(1)}, u32[]{:S(2)}, u32[]{:S(2)}) collective-permute-start(f32[10,10,3,128]{3,2,1,0:T(4,128)S(1)} %broadcast_select_fusion.2), channel_id=1, source_target_pairs={{0,1},{1,0},{2,3},{3,2},{4,5},{5,4},{6,7},{7,6},{8,9},{9,8},{10,11... | collective-permute-start | bytes 460808 | tf_op jit(solution)/shard_map/ppermute | solution.py:212
  27.9 7.9 %collective-permute-start.2 = (f32[10,10,3,128]{3,2,1,0:T(4,128)S(1)}, f32[10,10,3,128]{3,2,1,0:T(4,128)S(1)}, u32[]{:S(2)}, u32[]{:S(2)}) collective-permute-start(f32[10,10,3,128]{3,2,1,0:T(4,128)S(1)} %get-tuple-element.2), channel_id=1, source_target_pairs={{0,31},{1,2},{2,1},{3,4},{4,3},{5,6},{6,5},{7,8},{8,7},{9,10},{10,... | collective-permute-start | bytes 460808 | tf_op jit(solution)/shard_map/ppermute | solution.py:213
  35.9 4.4 %shard_map.86.early_ref = f32[10,8,8,128]{3,2,1,0:T(8,128)} custom-call(f32[21]{0:T(128)} %rate_ref.3, f32[21]{0:T(128)} %act_ref.3, f32[21]{0:T(128)} %heat_ref.3, f32[10,8,8,128]{3,2,1,0:T(8,128)} %hbm_ref.1, s32[8,8]{1,0:T(8,128)} %cnt_ref.3), custom_call_target="tpu_custom_call" | custom-call | tf_op jit(solution)/shard_map/pallas_call | solution.py:188
  40.3 0.0 collective-permute-done.3
  40.3 0.0 collective-permute-done.2
  40.3 0.1 broadcast_select_fusion.1
  40.4 0.1 slice.86
  40.5 0.1 slice.87
  40.6 0.0 copy-start.1
  40.6 1.1 %pad_maximum_fusion.1.src_ref = f32[10,10,10,128]{3,2,1,0:T(8,128)} fusion(f32[10,10,1,128]{3,2,1,0:T(1,128)S(1)} %slice.87, f32[10,1,8,128]{3,2,1,0:T(8,128)S(1)} %get-tuple-element.20, f32[10,8,8,128]{3,2,1,0:T(8,128)S(1)} %copy-done.2, f32[10,1,8,128]{3,2,1,0:T(8,128)S(1)} %get-tuple-element.16, f32[10,10,1,128]{3,2,1,0:T(1,128)S(1)} %slice.86), kind=kLoop, calls=%fused_computation.13 | loop fusion | flops 512000 | bytes 1024000 | tf_op jit(solution)/shard_map/concatenate | solution.py:245
  41.7 0.0 copy-done.1
  41.7 1.1 %fusion.3.ext_ref = f32[10,12,12,128]{3,2,1,0:T(8,128)} fusion(f32[10,2,8,128]{3,2,1,0:T(8,128)S(1)} %slice.80, f32[10,8,8,128]{3,2,1,0:T(8,128)S(1)} %copy-done.1, f32[10,2,8,128]{3,2,1,0:T(8,128)S(1)} %slice.79, f32[10,1,2,128]{3,2,1,0:T(2,128)S(1)} %broadcast.5, f32[10,1,8,128]{3,2,1,0:T(8,128)S(1)} %get-tuple-element.19, ...), kind=kLoop, calls=%fused_computation.8 | loop fusion | flops 3870720 | bytes 1525760 | tf_op jit(solution)/shard_map/concatenate | solution.py:237
  42.9 5.6 %shard_map.87 = (f32[10,8,8,128]{3,2,1,0:T(8,128)}, f32[10,8,8,128]{3,2,1,0:T(8,128)}) custom-call(f32[10]{0:T(128)} %diff_ref.1, f32[21]{0:T(128)} %rate_ref.3, f32[21]{0:T(128)} %act_ref.3, f32[21]{0:T(128)} %heat_ref.3, f32[10,12,12,128]{3,2,1,0:T(8,128)} %fusion.3.ext_ref, f32[10,10,10,128]{3,2,1,0:T(8,128)} %pad_maximum_fusion.1.src_ref, ...), custom_call_target="tpu_custom_call" | custom-call | tf_op jit(solution)/shard_map/pallas_call | solution.py:176
  (8 shorter events, 0.1 us)
Async XLA Ops:
  2.4 20.7 %collective-permute-start = (f32[10,3,8,128]{3,2,1,0:T(8,128)S(1)}, f32[10,3,8,128]{3,2,1,0:T(8,128)S(1)}, u32[]{:S(2)}, u32[]{:S(2)}) collective-permute-start(f32[10,3,8,128]{3,2,1,0:T(8,128)S(1)} %get-tuple-element.13), channel_id=1, source_target_pairs={{0,736},{32,64},{64,32},{96,128},{128,96},{160,192},{192,160},{224... | collective-permute-start | bytes 368648 | tf_op jit(solution)/shard_map/ppermute | solution.py:213
  16.7 6.4 %collective-permute-start.1 = (f32[10,3,8,128]{3,2,1,0:T(8,128)S(1)}, f32[10,3,8,128]{3,2,1,0:T(8,128)S(1)}, u32[]{:S(2)}, u32[]{:S(2)}) collective-permute-start(f32[10,3,8,128]{3,2,1,0:T(8,128)S(1)} %get-tuple-element.14), channel_id=1, source_target_pairs={{0,32},{32,0},{64,96},{96,64},{128,160},{160,128},{192,224},{224,1... | collective-permute-start | bytes 368648 | tf_op jit(solution)/shard_map/ppermute | solution.py:212
  23.1 1.0 %copy-start = (f32[10,8,8,128]{3,2,1,0:T(8,128)S(1)}, f32[10,8,8,128]{3,2,1,0:T(8,128)}, u32[]{:S(2)}) copy-start(f32[10,8,8,128]{3,2,1,0:T(8,128)} %hbm_ref.1) | copy-start | bytes 983044
  23.1 1.1 %copy-start.2 = (f32[10,8,8,128]{3,2,1,0:T(8,128)S(1)}, f32[10,8,8,128]{3,2,1,0:T(8,128)}, u32[]{:S(2)}) copy-start(f32[10,8,8,128]{3,2,1,0:T(8,128)} %param.8) | copy-start | bytes 983044
  24.4 15.8 %collective-permute-start.3 = (f32[10,10,3,128]{3,2,1,0:T(4,128)S(1)}, f32[10,10,3,128]{3,2,1,0:T(4,128)S(1)}, u32[]{:S(2)}, u32[]{:S(2)}) collective-permute-start(f32[10,10,3,128]{3,2,1,0:T(4,128)S(1)} %broadcast_select_fusion.2), channel_id=1, source_target_pairs={{0,1},{1,0},{2,3},{3,2},{4,5},{5,4},{6,7},{7,6},{8,9},{9,8},{10,11... | collective-permute-start | bytes 460808 | tf_op jit(solution)/shard_map/ppermute | solution.py:212
  27.9 12.4 %collective-permute-start.2 = (f32[10,10,3,128]{3,2,1,0:T(4,128)S(1)}, f32[10,10,3,128]{3,2,1,0:T(4,128)S(1)}, u32[]{:S(2)}, u32[]{:S(2)}) collective-permute-start(f32[10,10,3,128]{3,2,1,0:T(4,128)S(1)} %get-tuple-element.2), channel_id=1, source_target_pairs={{0,31},{1,2},{2,1},{3,4},{4,3},{5,6},{6,5},{7,8},{8,7},{9,10},{10,... | collective-permute-start | bytes 460808 | tf_op jit(solution)/shard_map/ppermute | solution.py:213
  40.6 1.1 %copy-start.1 = (f32[10,8,8,128]{3,2,1,0:T(8,128)S(1)}, f32[10,8,8,128]{3,2,1,0:T(8,128)}, u32[]{:S(2)}) copy-start(f32[10,8,8,128]{3,2,1,0:T(8,128)} %hbm_ref.1) | copy-start | bytes 983044

commit v11 on v5

--- a/solution.py
+++ b/solution.py
@@ -198,15 +198,38 @@
     return jnp.where(even, second, first), jnp.where(even, first, second)
 
 
+def exchange_edges(state, source_in, axis, size):
+    cx = state.shape[1]
+    if size % 2:
+        to_lo = jnp.concatenate([state[:, :2], source_in[:, :1]], 1)
+        to_hi = jnp.concatenate([state[:, cx - 2:], source_in[:, cx - 1:]], 1)
+        return exchange(to_lo, to_hi, axis, size)
+    even = lax.axis_index(axis) % 2 == 0
+
+    def rows_from(high):
+        top = jnp.where(high, cx - 2, 0)
+        return jnp.concatenate(
+            [
+                lax.dynamic_slice_in_dim(state, top, 2, 1),
+                lax.dynamic_slice_in_dim(source_in, jnp.where(high, cx - 1, 0), 1, 1),
+            ],
+            1,
+        )
+
+    inner = [(i, i + 1 if i % 2 == 0 else i - 1) for i in range(size)]
+    outer = [(i, (i - 1) % size if i % 2 == 0 else (i + 1) % size) for i in range(size)]
+    first = lax.ppermute(rows_from(even), axis, inner)
+    second = lax.ppermute(rows_from(jnp.logical_not(even)), axis, outer)
+    return jnp.where(even, second, first), jnp.where(even, first, second)
+
+
 def local(state, source_in, counts, diffusivity, log_rate, activation, heat_release):
     nx = lax.axis_size("gx")
     ny = lax.axis_size("gy")
     rows, cx, cy, cz = state.shape
     cell_counts = jnp.broadcast_to(counts[:, :, None], (cx, cy, cz))
 
-    to_xm = jnp.concatenate([state[:, :2], source_in[:, :1]], 1)
-    to_xp = jnp.concatenate([state[:, cx - 2:], source_in[:, cx - 1:]], 1)
-    from_xm, from_xp = exchange(to_xm, to_xp, "gx", nx)
+    from_xm, from_xp = exchange_edges(state, source_in, "gx", nx)
 
     early = chemistry(state, cell_counts, log_rate, activation, heat_release)
 

time: 48.8 us -> 51.4 us (1.053)
  waiting for transfers between devices: 4.47 us -> 6.39 us
  starting transfers between devices: 27.6 us -> 28.3 us
    ppermute x0 -> x2, starting transfers between devices: none -> 16.8 us  [the longest x1 14.9 us: exchange_edges(): second = lax.ppermute(rows_from(jnp.logical_not(even)), axis, outer)]
    ppermute x2 -> x1, starting transfers between devices: 22.2 us -> 7.94 us  [exchange(): second = lax.ppermute(jnp.where(even, to_lo, to_hi), axis, outer)]
    ppermute x0 -> x2, waiting for transfers between devices: none -> 6.38 us  [the longest x1 6.38 us: exchange_edges(): second = lax.ppermute(rows_from(jnp.logical_not(even)), axis, outer)]
    ppermute x2 -> x1, waiting for transfers between devices: 4.47 us -> 0.01 us  [exchange(): second = lax.ppermute(jnp.where(even, to_lo, to_hi), axis, outer)]
    ppermute x2 -> x1, starting transfers between devices: 5.41 us -> 3.48 us  [exchange(): first = lax.ppermute(jnp.where(even, to_hi, to_lo), axis, inner)]
    dynamic_slice x0 -> x2, local copies, waits for them, and re-layouts: none -> 1.75 us  [the longest x1 0.94 us: rows_from(): lax.dynamic_slice_in_dim(state, top, 2, 1)]
    slice x2 -> x0, local copies, waits for them, and re-layouts: 1.75 us -> none  [local(): to_xm = jnp.concatenate([state[:, :2], source_in[:, :1]], 1)]
  transfers between devices with their start and end apart: 4 -> 4, of which waited for: 1 -> 1; matrix products, arithmetic and copies ran while one was open for 1% -> 1% of each run, Pallas kernels for 8% -> 7%
where the time goes in v11:
time: 51.4 us; the launch traced here: 51 us
  starting transfers between devices  28.3 us (55%)
  Pallas kernels  9.2 us (18%)
  waiting for transfers between devices  6.39 us (12%)
  local copies, waits for them, and re-layouts  3.67 us (7%)
  other arithmetic  2.58 us (5%)
  between operations  0.85 us (2%)
    ppermute x1, starting transfers between devices, exchange_edges(): second = lax.ppermute(rows_from(jnp.logical_not(even)), axis, outer)  14.9 us
    ppermute x1, starting transfers between devices, exchange(): second = lax.ppermute(jnp.where(even, to_lo, to_hi), axis, outer)  7.94 us
    ppermute x1, waiting for transfers between devices, exchange_edges(): second = lax.ppermute(rows_from(jnp.logical_not(even)), axis, outer)  6.38 us
    pallas_call x1, Pallas kernels, finish(): pl.pallas_call(finish_kernel, out_shape=(box, box), in_specs=[smem, smem,...  5.56 us
    pallas_call x1, Pallas kernels, chemistry(): pl.pallas_call(chem_kernel, out_shape=jax.ShapeDtypeStruct(fields.shape,...  3.63 us
    ppermute x1, starting transfers between devices, exchange(): first = lax.ppermute(jnp.where(even, to_hi, to_lo), axis, inner)  3.48 us
    ppermute x1, starting transfers between devices, exchange_edges(): first = lax.ppermute(rows_from(even), axis, inner)  1.92 us
    concatenate x1, other arithmetic, local(): jnp.concatenate([jnp.concatenate([zeros(1, 2), wide[:, :1], zeros(1, 2)],...  1.13 us
  transfers between devices with their start and end apart: 4, of which 1 were waited for; matrix products, arithmetic and copies ran while one was open for 1% of the time, Pallas kernels for 7%

profile of v11, /device:TPU:6, one launch (start us, length us, event | category | flops | bytes accessed | tf_op | source)
XLA Modules:
  0.0 51.0 jit_solution(8047982835509090642)
XLA Ops:
  0.7 0.8 %constant_dynamic-slice_fusion.2 = (f32[10,1,8,128]{3,2,1,0:T(8,128)S(1)}, f32[10,1,8,128]{3,2,1,0:T(8,128)S(1)}) fusion(f32[10,8,8,128]{3,2,1,0:T(8,128)} %param.8, s32[]{:T(128)S(6)} %select_n.63, s32[]{:T(128)S(6)} %select_n.65), kind=kLoop, calls=%fused_computation.36 | loop fusion | bytes 163848 | tf_op jit(solution)/shard_map/dynamic_slice | solution.py:214
  1.5 0.9 %constant_dynamic-slice_fusion.3 = (f32[10,2,8,128]{3,2,1,0:T(8,128)S(1)}, f32[10,2,8,128]{3,2,1,0:T(8,128)S(1)}) fusion(f32[10,8,8,128]{3,2,1,0:T(8,128)} %u_ref.1, s32[]{:T(128)S(6)} %select_n.62, s32[]{:T(128)S(6)} %select_n.64), kind=kLoop, calls=%fused_computation.37 | loop fusion | bytes 327688 | tf_op jit(solution)/shard_map/dynamic_slice | solution.py:213
  2.4 1.9 %collective-permute-start.1 = (f32[10,3,8,128]{3,2,1,0:T(8,128)S(1)}, f32[10,3,8,128]{3,2,1,0:T(8,128)S(1)}, u32[]{:S(2)}, u32[]{:S(2)}) collective-permute-start(f32[10,3,8,128]{3,2,1,0:T(8,128)S(1)} %pad_maximum_fusion.7), channel_id=1, source_target_pairs={{0,32},{32,0},{64,96},{96,64},{128,160},{160,128},{192,224},{224,1... | collective-permute-start | bytes 368648 | tf_op jit(solution)/shard_map/ppermute | solution.py:221
  4.4 14.9 %collective-permute-start = (f32[10,3,8,128]{3,2,1,0:T(8,128)S(1)}, f32[10,3,8,128]{3,2,1,0:T(8,128)S(1)}, u32[]{:S(2)}, u32[]{:S(2)}) collective-permute-start(f32[10,3,8,128]{3,2,1,0:T(8,128)S(1)} %pad_maximum_fusion.6), channel_id=1, source_target_pairs={{0,736},{32,64},{64,32},{96,128},{128,96},{160,192},{192,160},{224... | collective-permute-start | bytes 368648 | tf_op jit(solution)/shard_map/ppermute | solution.py:222
  19.3 0.0 collective-permute-done.1
  19.3 6.4 %collective-permute-done = f32[10,3,8,128]{3,2,1,0:T(8,128)S(1)} collective-permute-done((f32[10,3,8,128]{3,2,1,0:T(8,128)S(1)}, f32[10,3,8,128]{3,2,1,0:T(8,128)S(1)}, u32[]{:S(2)}, u32[]{:S(2)}) %collective-permute-start) | collective-permute-done | bytes 122912 | tf_op jit(solution)/shard_map/ppermute | solution.py:222
  25.7 0.0 copy-start
  25.7 0.0 copy-start.2
  25.8 0.9 %copy-done = f32[10,8,8,128]{3,2,1,0:T(8,128)S(1)} copy-done((f32[10,8,8,128]{3,2,1,0:T(8,128)S(1)}, f32[10,8,8,128]{3,2,1,0:T(8,128)}, u32[]{:S(2)}) %copy-start) | copy-done | bytes 327704
  26.7 0.1 copy-done.2
  26.8 0.2 broadcast_select_fusion.3
  27.0 0.0 copy-start.3
  27.0 0.1 broadcast_select_fusion.2
  27.1 3.5 %collective-permute-start.3 = (f32[10,10,3,128]{3,2,1,0:T(4,128)S(1)}, f32[10,10,3,128]{3,2,1,0:T(4,128)S(1)}, u32[]{:S(2)}, u32[]{:S(2)}) collective-permute-start(f32[10,10,3,128]{3,2,1,0:T(4,128)S(1)} %broadcast_select_fusion.2), channel_id=1, source_target_pairs={{0,1},{1,0},{2,3},{3,2},{4,5},{5,4},{6,7},{7,6},{8,9},{9,8},{10,11... | collective-permute-start | bytes 460808 | tf_op jit(solution)/shard_map/ppermute | solution.py:196
  30.5 7.9 %collective-permute-start.2 = (f32[10,10,3,128]{3,2,1,0:T(4,128)S(1)}, f32[10,10,3,128]{3,2,1,0:T(4,128)S(1)}, u32[]{:S(2)}, u32[]{:S(2)}) collective-permute-start(f32[10,10,3,128]{3,2,1,0:T(4,128)S(1)} %get-tuple-element.2), channel_id=1, source_target_pairs={{0,31},{1,2},{2,1},{3,4},{4,3},{5,6},{6,5},{7,8},{8,7},{9,10},{10,... | collective-permute-start | bytes 460808 | tf_op jit(solution)/shard_map/ppermute | solution.py:197
  38.5 0.0 copy-done.3
  38.5 0.7 %broadcast_in_dim.2.cnt_ref = s32[8,8,128]{2,1,0:T(8,128)} broadcast(s32[8,8]{1,0:T(8,128)S(1)} %copy-done.3), dimensions={0,1} | broadcast | bytes 33024 | tf_op jit(solution)/shard_map/broadcast_in_dim | solution.py:230
  39.2 3.6 %shard_map.86.early_ref = f32[10,8,8,128]{3,2,1,0:T(8,128)} custom-call(f32[21]{0:T(128)} %rate_ref.3, f32[21]{0:T(128)} %act_ref.3, f32[21]{0:T(128)} %heat_ref.3, f32[10,8,8,128]{3,2,1,0:T(8,128)} %u_ref.1, s32[8,8,128]{2,1,0:T(8,128)} %broadcast_in_dim.2.cnt_ref), custom_call_target="tpu_custom_call" | custom-call | tf_op jit(solution)/shard_map/pallas_call | solution.py:176
  42.8 0.0 collective-permute-done.3
  42.8 0.0 collective-permute-done.2
  42.8 0.1 broadcast_select_fusion.1
  42.9 0.1 slice.70
  43.0 0.1 slice.71
  43.1 0.0 copy-start.1
  43.1 1.1 %pad_maximum_fusion.1.src_ref = f32[10,10,10,128]{3,2,1,0:T(8,128)} fusion(f32[10,10,1,128]{3,2,1,0:T(1,128)S(1)} %slice.71, f32[10,1,8,128]{3,2,1,0:T(8,128)S(1)} %get-tuple-element.18, f32[10,8,8,128]{3,2,1,0:T(8,128)S(1)} %copy-done.2, f32[10,1,8,128]{3,2,1,0:T(8,128)S(1)} %get-tuple-element.14, f32[10,10,1,128]{3,2,1,0:T(1,128)S(1)} %slice.70), kind=kLoop, calls=%fused_computation.13 | loop fusion | flops 512000 | bytes 1024000 | tf_op jit(solution)/shard_map/concatenate | solution.py:252
  44.3 0.0 copy-done.1
  44.3 1.1 %fusion.3.ext_ref = f32[10,12,12,128]{3,2,1,0:T(8,128)} fusion(f32[10,2,8,128]{3,2,1,0:T(8,128)S(1)} %slice.64, f32[10,8,8,128]{3,2,1,0:T(8,128)S(1)} %copy-done.1, f32[10,2,8,128]{3,2,1,0:T(8,128)S(1)} %slice.63, f32[10,1,2,128]{3,2,1,0:T(2,128)S(1)} %broadcast.6, f32[10,1,8,128]{3,2,1,0:T(8,128)S(1)} %get-tuple-element.17, ...), kind=kLoop, calls=%fused_computation.8 | loop fusion | flops 3870720 | bytes 1525760 | tf_op jit(solution)/shard_map/concatenate | solution.py:244
  45.4 5.6 %shard_map.87 = (f32[10,8,8,128]{3,2,1,0:T(8,128)}, f32[10,8,8,128]{3,2,1,0:T(8,128)}) custom-call(f32[10]{0:T(128)} %diff_ref.1, f32[21]{0:T(128)} %rate_ref.3, f32[21]{0:T(128)} %act_ref.3, f32[21]{0:T(128)} %heat_ref.3, f32[10,12,12,128]{3,2,1,0:T(8,128)} %fusion.3.ext_ref, f32[10,10,10,128]{3,2,1,0:T(8,128)} %pad_maximum_fusion.1.src_ref, ...), custom_call_target="tpu_custom_call" | custom-call | tf_op jit(solution)/shard_map/pallas_call | solution.py:164
  (9 shorter events, 0.1 us)
Async XLA Ops:
  2.4 16.9 %collective-permute-start.1 = (f32[10,3,8,128]{3,2,1,0:T(8,128)S(1)}, f32[10,3,8,128]{3,2,1,0:T(8,128)S(1)}, u32[]{:S(2)}, u32[]{:S(2)}) collective-permute-start(f32[10,3,8,128]{3,2,1,0:T(8,128)S(1)} %pad_maximum_fusion.7), channel_id=1, source_target_pairs={{0,32},{32,0},{64,96},{96,64},{128,160},{160,128},{192,224},{224,1... | collective-permute-start | bytes 368648 | tf_op jit(solution)/shard_map/ppermute | solution.py:221
  4.4 21.3 %collective-permute-start = (f32[10,3,8,128]{3,2,1,0:T(8,128)S(1)}, f32[10,3,8,128]{3,2,1,0:T(8,128)S(1)}, u32[]{:S(2)}, u32[]{:S(2)}) collective-permute-start(f32[10,3,8,128]{3,2,1,0:T(8,128)S(1)} %pad_maximum_fusion.6), channel_id=1, source_target_pairs={{0,736},{32,64},{64,32},{96,128},{128,96},{160,192},{192,160},{224... | collective-permute-start | bytes 368648 | tf_op jit(solution)/shard_map/ppermute | solution.py:222
  25.7 1.0 %copy-start = (f32[10,8,8,128]{3,2,1,0:T(8,128)S(1)}, f32[10,8,8,128]{3,2,1,0:T(8,128)}, u32[]{:S(2)}) copy-start(f32[10,8,8,128]{3,2,1,0:T(8,128)} %u_ref.1) | copy-start | bytes 983044
  25.7 1.1 %copy-start.2 = (f32[10,8,8,128]{3,2,1,0:T(8,128)S(1)}, f32[10,8,8,128]{3,2,1,0:T(8,128)}, u32[]{:S(2)}) copy-start(f32[10,8,8,128]{3,2,1,0:T(8,128)} %param.8) | copy-start | bytes 983044
  27.0 11.5 %copy-start.3 = (s32[8,8]{1,0:T(8,128)S(1)}, s32[8,8]{1,0:T(8,128)}, u32[]{:S(2)}) copy-start(s32[8,8]{1,0:T(8,128)} %param.9) | copy-start | bytes 772
  27.1 15.8 %collective-permute-start.3 = (f32[10,10,3,128]{3,2,1,0:T(4,128)S(1)}, f32[10,10,3,128]{3,2,1,0:T(4,128)S(1)}, u32[]{:S(2)}, u32[]{:S(2)}) collective-permute-start(f32[10,10,3,128]{3,2,1,0:T(4,128)S(1)} %broadcast_select_fusion.2), channel_id=1, source_target_pairs={{0,1},{1,0},{2,3},{3,2},{4,5},{5,4},{6,7},{7,6},{8,9},{9,8},{10,11... | collective-permute-start | bytes 460808 | tf_op jit(solution)/shard_map/ppermute | solution.py:196
  30.5 12.3 %collective-permute-start.2 = (f32[10,10,3,128]{3,2,1,0:T(4,128)S(1)}, f32[10,10,3,128]{3,2,1,0:T(4,128)S(1)}, u32[]{:S(2)}, u32[]{:S(2)}) collective-permute-start(f32[10,10,3,128]{3,2,1,0:T(4,128)S(1)} %get-tuple-element.2), channel_id=1, source_target_pairs={{0,31},{1,2},{2,1},{3,4},{4,3},{5,6},{6,5},{7,8},{8,7},{9,10},{10,... | collective-permute-start | bytes 460808 | tf_op jit(solution)/shard_map/ppermute | solution.py:197
  43.1 1.1 %copy-start.1 = (f32[10,8,8,128]{3,2,1,0:T(8,128)S(1)}, f32[10,8,8,128]{3,2,1,0:T(8,128)}, u32[]{:S(2)}) copy-start(f32[10,8,8,128]{3,2,1,0:T(8,128)} %u_ref.1) | copy-start | bytes 983044

commit v12 on v10

--- a/solution.py
+++ b/solution.py
@@ -95,11 +95,8 @@
     return tile
 
 
-def chem_kernel(rate_ref, act_ref, heat_ref, hbm_ref, cnt_ref, o_ref, u_ref, sem):
+def chem_kernel(rate_ref, act_ref, heat_ref, u_ref, cnt_ref, o_ref):
     rows = u_ref.shape[0]
-    copy = pltpu.make_async_copy(hbm_ref, u_ref, sem)
-    copy.start()
-    copy.wait()
 
     def per_x(x, carry):
         start = [u_ref[s, x] for s in range(rows)]
@@ -188,12 +185,8 @@
     return pl.pallas_call(
         chem_kernel,
         out_shape=jax.ShapeDtypeStruct(fields.shape, jnp.float32),
-        in_specs=[smem, smem, smem, pl.BlockSpec(memory_space=pl.ANY), smem],
+        in_specs=[smem, smem, smem, vmem, smem],
         out_specs=vmem,
-        scratch_shapes=[
-            pltpu.VMEM(fields.shape, jnp.float32),
-            pltpu.SemaphoreType.DMA(()),
-        ],
     )(log_rate, activation, heat_release, fields, cell_counts)
 
 

time: 48.9 us -> 48.8 us (level)
  Pallas kernels: 9.99 us -> 9.25 us
  waiting for transfers between devices: 4.47 us -> 5.16 us
    pallas_call x1, Pallas kernels: 4.39 us -> 3.65 us  [chemistry(): pl.pallas_call(chem_kernel, out_shape=jax.ShapeDtypeStruct(fields.shape,...]
    ppermute x2, waiting for transfers between devices: 4.47 us -> 5.15 us  [exchange(): second = lax.ppermute(jnp.where(even, to_lo, to_hi), axis, outer)]
  transfers between devices with their start and end apart: 4 -> 4, of which waited for: 1 -> 2; matrix products, arithmetic and copies ran while one was open for 0% -> 0% of each run, Pallas kernels for 9% -> 8%
where the time goes in v12:
time: 48.8 us; the launch traced here: 48.4 us
  starting transfers between devices  27.6 us (57%)
  Pallas kernels  9.25 us (19%)
  waiting for transfers between devices  5.16 us (11%)
  local copies, waits for them, and re-layouts  2.98 us (6%)
  other arithmetic  2.58 us (5%)
  between operations  0.8 us (2%)
    ppermute x2, starting transfers between devices, exchange(): second = lax.ppermute(jnp.where(even, to_lo, to_hi), axis, outer)  22.2 us
    pallas_call x1, Pallas kernels, finish(): pl.pallas_call(finish_kernel, out_shape=(box, box), in_specs=[smem, smem,...  5.6 us
    ppermute x2, starting transfers between devices, exchange(): first = lax.ppermute(jnp.where(even, to_hi, to_lo), axis, inner)  5.41 us
    ppermute x2, waiting for transfers between devices, exchange(): second = lax.ppermute(jnp.where(even, to_lo, to_hi), axis, outer)  5.15 us
    pallas_call x1, Pallas kernels, chemistry(): pl.pallas_call(chem_kernel, out_shape=jax.ShapeDtypeStruct(fields.shape,...  3.65 us
    slice x2, local copies, waits for them, and re-layouts, local(): to_xm = jnp.concatenate([state[:, :2], source_in[:, :1]], 1)  1.75 us
    concatenate x1, other arithmetic, local(): jnp.concatenate([jnp.concatenate([zeros(1, 2), wide[:, :1], zeros(1, 2)],...  1.13 us
    concatenate x1, other arithmetic, local(): src = jnp.concatenate([from_ym[:, :, 2:], wide_src, from_yp[:, :, 2:]], 2)  1.12 us
  transfers between devices with their start and end apart: 4, of which 2 were waited for; matrix products, arithmetic and copies ran while one was open for 0% of the time, Pallas kernels for 8%

profile of v12, /device:TPU:6, one launch (start us, length us, event | category | flops | bytes accessed | tf_op | source)
XLA Modules:
  0.0 48.4 jit_solution(14440909546173754288)
XLA Ops:
  0.6 0.8 %fusion.14 = (f32[10,1,8,128]{3,2,1,0:T(8,128)S(1)}, f32[10,1,8,128]{3,2,1,0:T(8,128)S(1)}) fusion(f32[10,8,8,128]{3,2,1,0:T(8,128)} %param.8), kind=kLoop, calls=%fused_computation.37 | loop fusion | bytes 163840 | tf_op jit(solution)/shard_map/slice | solution.py:216
  1.5 0.9 %fusion.13 = (f32[10,2,8,128]{3,2,1,0:T(8,128)S(1)}, f32[10,2,8,128]{3,2,1,0:T(8,128)S(1)}) fusion(f32[10,8,8,128]{3,2,1,0:T(8,128)} %u_ref.1), kind=kLoop, calls=%fused_computation.36 | loop fusion | bytes 327680 | tf_op jit(solution)/shard_map/slice | solution.py:216
  2.4 14.3 %collective-permute-start = (f32[10,3,8,128]{3,2,1,0:T(8,128)S(1)}, f32[10,3,8,128]{3,2,1,0:T(8,128)S(1)}, u32[]{:S(2)}, u32[]{:S(2)}) collective-permute-start(f32[10,3,8,128]{3,2,1,0:T(8,128)S(1)} %get-tuple-element.13), channel_id=1, source_target_pairs={{0,736},{32,64},{64,32},{96,128},{128,96},{160,192},{192,160},{224... | collective-permute-start | bytes 368648 | tf_op jit(solution)/shard_map/ppermute | solution.py:206
  16.7 1.9 %collective-permute-start.1 = (f32[10,3,8,128]{3,2,1,0:T(8,128)S(1)}, f32[10,3,8,128]{3,2,1,0:T(8,128)S(1)}, u32[]{:S(2)}, u32[]{:S(2)}) collective-permute-start(f32[10,3,8,128]{3,2,1,0:T(8,128)S(1)} %get-tuple-element.14), channel_id=1, source_target_pairs={{0,32},{32,0},{64,96},{96,64},{128,160},{160,128},{192,224},{224,1... | collective-permute-start | bytes 368648 | tf_op jit(solution)/shard_map/ppermute | solution.py:205
  18.6 4.5 %collective-permute-done = f32[10,3,8,128]{3,2,1,0:T(8,128)S(1)} collective-permute-done((f32[10,3,8,128]{3,2,1,0:T(8,128)S(1)}, f32[10,3,8,128]{3,2,1,0:T(8,128)S(1)}, u32[]{:S(2)}, u32[]{:S(2)}) %collective-permute-start) | collective-permute-done | bytes 122912 | tf_op jit(solution)/shard_map/ppermute | solution.py:206
  23.1 0.0 collective-permute-done.1
  23.1 0.0 copy-start
  23.1 0.0 copy-start.2
  23.2 0.9 %copy-done = f32[10,8,8,128]{3,2,1,0:T(8,128)S(1)} copy-done((f32[10,8,8,128]{3,2,1,0:T(8,128)S(1)}, f32[10,8,8,128]{3,2,1,0:T(8,128)}, u32[]{:S(2)}) %copy-start) | copy-done | bytes 327704
  24.1 0.1 copy-done.2
  24.2 0.2 broadcast_select_fusion.3
  24.4 0.1 broadcast_select_fusion.2
  24.4 3.5 %collective-permute-start.3 = (f32[10,10,3,128]{3,2,1,0:T(4,128)S(1)}, f32[10,10,3,128]{3,2,1,0:T(4,128)S(1)}, u32[]{:S(2)}, u32[]{:S(2)}) collective-permute-start(f32[10,10,3,128]{3,2,1,0:T(4,128)S(1)} %broadcast_select_fusion.2), channel_id=1, source_target_pairs={{0,1},{1,0},{2,3},{3,2},{4,5},{5,4},{6,7},{7,6},{8,9},{9,8},{10,11... | collective-permute-start | bytes 460808 | tf_op jit(solution)/shard_map/ppermute | solution.py:205
  27.9 7.9 %collective-permute-start.2 = (f32[10,10,3,128]{3,2,1,0:T(4,128)S(1)}, f32[10,10,3,128]{3,2,1,0:T(4,128)S(1)}, u32[]{:S(2)}, u32[]{:S(2)}) collective-permute-start(f32[10,10,3,128]{3,2,1,0:T(4,128)S(1)} %get-tuple-element.2), channel_id=1, source_target_pairs={{0,31},{1,2},{2,1},{3,4},{4,3},{5,6},{6,5},{7,8},{8,7},{9,10},{10,... | collective-permute-start | bytes 460808 | tf_op jit(solution)/shard_map/ppermute | solution.py:206
  35.9 3.7 %shard_map.86.early_ref = f32[10,8,8,128]{3,2,1,0:T(8,128)} custom-call(f32[21]{0:T(128)} %rate_ref.3, f32[21]{0:T(128)} %act_ref.3, f32[21]{0:T(128)} %heat_ref.3, f32[10,8,8,128]{3,2,1,0:T(8,128)} %u_ref.1, s32[8,8]{1,0:T(8,128)} %cnt_ref.3), custom_call_target="tpu_custom_call" | custom-call | tf_op jit(solution)/shard_map/pallas_call | solution.py:185
  39.5 0.0 collective-permute-done.3
  39.5 0.7 %collective-permute-done.2 = f32[10,10,3,128]{3,2,1,0:T(4,128)S(1)} collective-permute-done((f32[10,10,3,128]{3,2,1,0:T(4,128)S(1)}, f32[10,10,3,128]{3,2,1,0:T(4,128)S(1)}, u32[]{:S(2)}, u32[]{:S(2)}) %collective-permute-start.2) | collective-permute-done | bytes 153632 | tf_op jit(solution)/shard_map/ppermute | solution.py:206
  40.2 0.1 broadcast_select_fusion.1
  40.3 0.1 slice.86
  40.4 0.1 slice.87
  40.5 0.0 copy-start.1
  40.5 1.1 %pad_maximum_fusion.1.src_ref = f32[10,10,10,128]{3,2,1,0:T(8,128)} fusion(f32[10,10,1,128]{3,2,1,0:T(1,128)S(1)} %slice.87, f32[10,1,8,128]{3,2,1,0:T(8,128)S(1)} %get-tuple-element.20, f32[10,8,8,128]{3,2,1,0:T(8,128)S(1)} %copy-done.2, f32[10,1,8,128]{3,2,1,0:T(8,128)S(1)} %get-tuple-element.16, f32[10,10,1,128]{3,2,1,0:T(1,128)S(1)} %slice.86), kind=kLoop, calls=%fused_computation.13 | loop fusion | flops 512000 | bytes 1024000 | tf_op jit(solution)/shard_map/concatenate | solution.py:238
  41.6 0.0 copy-done.1
  41.6 1.1 %fusion.3.ext_ref = f32[10,12,12,128]{3,2,1,0:T(8,128)} fusion(f32[10,2,8,128]{3,2,1,0:T(8,128)S(1)} %slice.80, f32[10,8,8,128]{3,2,1,0:T(8,128)S(1)} %copy-done.1, f32[10,2,8,128]{3,2,1,0:T(8,128)S(1)} %slice.79, f32[10,1,2,128]{3,2,1,0:T(2,128)S(1)} %broadcast.5, f32[10,1,8,128]{3,2,1,0:T(8,128)S(1)} %get-tuple-element.19, ...), kind=kLoop, calls=%fused_computation.8 | loop fusion | flops 3870720 | bytes 1525760 | tf_op jit(solution)/shard_map/concatenate | solution.py:230
  42.8 5.6 %shard_map.87 = (f32[10,8,8,128]{3,2,1,0:T(8,128)}, f32[10,8,8,128]{3,2,1,0:T(8,128)}) custom-call(f32[10]{0:T(128)} %diff_ref.1, f32[21]{0:T(128)} %rate_ref.3, f32[21]{0:T(128)} %act_ref.3, f32[21]{0:T(128)} %heat_ref.3, f32[10,12,12,128]{3,2,1,0:T(8,128)} %fusion.3.ext_ref, f32[10,10,10,128]{3,2,1,0:T(8,128)} %pad_maximum_fusion.1.src_ref, ...), custom_call_target="tpu_custom_call" | custom-call | tf_op jit(solution)/shard_map/pallas_call | solution.py:173
  (8 shorter events, 0.1 us)
Async XLA Ops:
  2.4 20.7 %collective-permute-start = (f32[10,3,8,128]{3,2,1,0:T(8,128)S(1)}, f32[10,3,8,128]{3,2,1,0:T(8,128)S(1)}, u32[]{:S(2)}, u32[]{:S(2)}) collective-permute-start(f32[10,3,8,128]{3,2,1,0:T(8,128)S(1)} %get-tuple-element.13), channel_id=1, source_target_pairs={{0,736},{32,64},{64,32},{96,128},{128,96},{160,192},{192,160},{224... | collective-permute-start | bytes 368648 | tf_op jit(solution)/shard_map/ppermute | solution.py:206
  16.7 6.4 %collective-permute-start.1 = (f32[10,3,8,128]{3,2,1,0:T(8,128)S(1)}, f32[10,3,8,128]{3,2,1,0:T(8,128)S(1)}, u32[]{:S(2)}, u32[]{:S(2)}) collective-permute-start(f32[10,3,8,128]{3,2,1,0:T(8,128)S(1)} %get-tuple-element.14), channel_id=1, source_target_pairs={{0,32},{32,0},{64,96},{96,64},{128,160},{160,128},{192,224},{224,1... | collective-permute-start | bytes 368648 | tf_op jit(solution)/shard_map/ppermute | solution.py:205
  23.1 1.0 %copy-start = (f32[10,8,8,128]{3,2,1,0:T(8,128)S(1)}, f32[10,8,8,128]{3,2,1,0:T(8,128)}, u32[]{:S(2)}) copy-start(f32[10,8,8,128]{3,2,1,0:T(8,128)} %u_ref.1) | copy-start | bytes 983044
  23.1 1.1 %copy-start.2 = (f32[10,8,8,128]{3,2,1,0:T(8,128)S(1)}, f32[10,8,8,128]{3,2,1,0:T(8,128)}, u32[]{:S(2)}) copy-start(f32[10,8,8,128]{3,2,1,0:T(8,128)} %param.8) | copy-start | bytes 983044
  24.4 15.1 %collective-permute-start.3 = (f32[10,10,3,128]{3,2,1,0:T(4,128)S(1)}, f32[10,10,3,128]{3,2,1,0:T(4,128)S(1)}, u32[]{:S(2)}, u32[]{:S(2)}) collective-permute-start(f32[10,10,3,128]{3,2,1,0:T(4,128)S(1)} %broadcast_select_fusion.2), channel_id=1, source_target_pairs={{0,1},{1,0},{2,3},{3,2},{4,5},{5,4},{6,7},{7,6},{8,9},{9,8},{10,11... | collective-permute-start | bytes 460808 | tf_op jit(solution)/shard_map/ppermute | solution.py:205
  27.9 12.3 %collective-permute-start.2 = (f32[10,10,3,128]{3,2,1,0:T(4,128)S(1)}, f32[10,10,3,128]{3,2,1,0:T(4,128)S(1)}, u32[]{:S(2)}, u32[]{:S(2)}) collective-permute-start(f32[10,10,3,128]{3,2,1,0:T(4,128)S(1)} %get-tuple-element.2), channel_id=1, source_target_pairs={{0,31},{1,2},{2,1},{3,4},{4,3},{5,6},{6,5},{7,8},{8,7},{9,10},{10,... | collective-permute-start | bytes 460808 | tf_op jit(solution)/shard_map/ppermute | solution.py:206
  40.5 1.1 %copy-start.1 = (f32[10,8,8,128]{3,2,1,0:T(8,128)S(1)}, f32[10,8,8,128]{3,2,1,0:T(8,128)}, u32[]{:S(2)}) copy-start(f32[10,8,8,128]{3,2,1,0:T(8,128)} %u_ref.1) | copy-start | bytes 983044

commit v13 on v5

--- a/solution.py
+++ b/solution.py
@@ -54,7 +54,7 @@
     stride = time_step / cnt.astype(jnp.float32)
     cur = list(start)
     for turn in range(CMAX):
-        active = turn < cnt
+        step = jnp.where(turn < cnt, stride, 0.0)
         rates = []
         for r, entry in enumerate(reaction_table):
             term = coeffs[r] * cur[entry[0]]
@@ -78,11 +78,11 @@
             if total is None:
                 new.append(cur[s])
             else:
-                new.append(jnp.where(active, cur[s] + stride * total, cur[s]))
+                new.append(cur[s] + step * total)
         heat_total = heat[0] * rates[0]
         for r in range(1, reactions):
             heat_total = heat_total + heat[r] * rates[r]
-        new.append(jnp.where(active, cur[SPECIES] + stride * heat_total, cur[SPECIES]))
+        new.append(cur[SPECIES] + step * heat_total)
         cur = new
     return [(cur[s] - start[s]) / time_step for s in range(len(start))]
 

time: 48.8 us -> 48.6 us (level)
  transfers between devices with their start and end apart: 4 -> 4, of which waited for: 1 -> 2; matrix products, arithmetic and copies ran while one was open for 1% -> 1% of each run, Pallas kernels for 8% -> 7%
where the time goes in v13:
time: 48.6 us; the launch traced here: 48.2 us
  starting transfers between devices  27.6 us (57%)
  Pallas kernels  8.94 us (18%)
  waiting for transfers between devices  4.61 us (9%)
  local copies, waits for them, and re-layouts  3.67 us (8%)
  other arithmetic  2.58 us (5%)
  between operations  0.82 us (2%)
    ppermute x2, starting transfers between devices, exchange(): second = lax.ppermute(jnp.where(even, to_lo, to_hi), axis, outer)  22.2 us
    pallas_call x1, Pallas kernels, finish(): pl.pallas_call(finish_kernel, out_shape=(box, box), in_specs=[smem, smem,...  5.43 us
    ppermute x2, starting transfers between devices, exchange(): first = lax.ppermute(jnp.where(even, to_hi, to_lo), axis, inner)  5.41 us
    ppermute x2, waiting for transfers between devices, exchange(): second = lax.ppermute(jnp.where(even, to_lo, to_hi), axis, outer)  4.6 us
    pallas_call x1, Pallas kernels, chemistry(): pl.pallas_call(chem_kernel, out_shape=jax.ShapeDtypeStruct(fields.shape,...  3.51 us
    slice x2, local copies, waits for them, and re-layouts, local(): to_xm = jnp.concatenate([state[:, :2], source_in[:, :1]], 1)  1.75 us
    concatenate x1, other arithmetic, local(): jnp.concatenate([jnp.concatenate([zeros(1, 2), wide[:, :1], zeros(1, 2)],...  1.14 us
    concatenate x1, other arithmetic, local(): src = jnp.concatenate([from_ym[:, :, 2:], wide_src, from_yp[:, :, 2:]], 2)  1.11 us
  transfers between devices with their start and end apart: 4, of which 2 were waited for; matrix products, arithmetic and copies ran while one was open for 1% of the time, Pallas kernels for 7%

profile of v13, /device:TPU:6, one launch (start us, length us, event | category | flops | bytes accessed | tf_op | source)
XLA Modules:
  0.0 48.2 jit_solution(14801072880917876476)
XLA Ops:
  0.6 0.8 %fusion.14 = (f32[10,1,8,128]{3,2,1,0:T(8,128)S(1)}, f32[10,1,8,128]{3,2,1,0:T(8,128)S(1)}) fusion(f32[10,8,8,128]{3,2,1,0:T(8,128)} %param.8), kind=kLoop, calls=%fused_computation.37 | loop fusion | bytes 163840 | tf_op jit(solution)/shard_map/slice | solution.py:207
  1.5 0.9 %fusion.13 = (f32[10,2,8,128]{3,2,1,0:T(8,128)S(1)}, f32[10,2,8,128]{3,2,1,0:T(8,128)S(1)}) fusion(f32[10,8,8,128]{3,2,1,0:T(8,128)} %u_ref.1), kind=kLoop, calls=%fused_computation.36 | loop fusion | bytes 327680 | tf_op jit(solution)/shard_map/slice | solution.py:207
  2.4 14.3 %collective-permute-start = (f32[10,3,8,128]{3,2,1,0:T(8,128)S(1)}, f32[10,3,8,128]{3,2,1,0:T(8,128)S(1)}, u32[]{:S(2)}, u32[]{:S(2)}) collective-permute-start(f32[10,3,8,128]{3,2,1,0:T(8,128)S(1)} %get-tuple-element.13), channel_id=1, source_target_pairs={{0,736},{32,64},{64,32},{96,128},{128,96},{160,192},{192,160},{224... | collective-permute-start | bytes 368648 | tf_op jit(solution)/shard_map/ppermute | solution.py:197
  16.7 1.9 %collective-permute-start.1 = (f32[10,3,8,128]{3,2,1,0:T(8,128)S(1)}, f32[10,3,8,128]{3,2,1,0:T(8,128)S(1)}, u32[]{:S(2)}, u32[]{:S(2)}) collective-permute-start(f32[10,3,8,128]{3,2,1,0:T(8,128)S(1)} %get-tuple-element.14), channel_id=1, source_target_pairs={{0,32},{32,0},{64,96},{96,64},{128,160},{160,128},{192,224},{224,1... | collective-permute-start | bytes 368648 | tf_op jit(solution)/shard_map/ppermute | solution.py:196
  18.6 4.5 %collective-permute-done = f32[10,3,8,128]{3,2,1,0:T(8,128)S(1)} collective-permute-done((f32[10,3,8,128]{3,2,1,0:T(8,128)S(1)}, f32[10,3,8,128]{3,2,1,0:T(8,128)S(1)}, u32[]{:S(2)}, u32[]{:S(2)}) %collective-permute-start) | collective-permute-done | bytes 122912 | tf_op jit(solution)/shard_map/ppermute | solution.py:197
  23.1 0.0 collective-permute-done.1
  23.1 0.0 copy-start
  23.1 0.0 copy-start.2
  23.2 0.9 %copy-done = f32[10,8,8,128]{3,2,1,0:T(8,128)S(1)} copy-done((f32[10,8,8,128]{3,2,1,0:T(8,128)S(1)}, f32[10,8,8,128]{3,2,1,0:T(8,128)}, u32[]{:S(2)}) %copy-start) | copy-done | bytes 327704
  24.1 0.1 copy-done.2
  24.2 0.2 broadcast_select_fusion.3
  24.4 0.0 copy-start.3
  24.4 0.1 broadcast_select_fusion.2
  24.4 3.5 %collective-permute-start.3 = (f32[10,10,3,128]{3,2,1,0:T(4,128)S(1)}, f32[10,10,3,128]{3,2,1,0:T(4,128)S(1)}, u32[]{:S(2)}, u32[]{:S(2)}) collective-permute-start(f32[10,10,3,128]{3,2,1,0:T(4,128)S(1)} %broadcast_select_fusion.2), channel_id=1, source_target_pairs={{0,1},{1,0},{2,3},{3,2},{4,5},{5,4},{6,7},{7,6},{8,9},{9,8},{10,11... | collective-permute-start | bytes 460808 | tf_op jit(solution)/shard_map/ppermute | solution.py:196
  27.9 7.9 %collective-permute-start.2 = (f32[10,10,3,128]{3,2,1,0:T(4,128)S(1)}, f32[10,10,3,128]{3,2,1,0:T(4,128)S(1)}, u32[]{:S(2)}, u32[]{:S(2)}) collective-permute-start(f32[10,10,3,128]{3,2,1,0:T(4,128)S(1)} %get-tuple-element.2), channel_id=1, source_target_pairs={{0,31},{1,2},{2,1},{3,4},{4,3},{5,6},{6,5},{7,8},{8,7},{9,10},{10,... | collective-permute-start | bytes 460808 | tf_op jit(solution)/shard_map/ppermute | solution.py:197
  35.9 0.0 copy-done.3
  35.9 0.7 %broadcast_in_dim.2.cnt_ref = s32[8,8,128]{2,1,0:T(8,128)} broadcast(s32[8,8]{1,0:T(8,128)S(1)} %copy-done.3), dimensions={0,1} | broadcast | bytes 33024 | tf_op jit(solution)/shard_map/broadcast_in_dim | solution.py:205
  36.6 3.5 %shard_map.86.early_ref = f32[10,8,8,128]{3,2,1,0:T(8,128)} custom-call(f32[21]{0:T(128)} %rate_ref.3, f32[21]{0:T(128)} %act_ref.3, f32[21]{0:T(128)} %heat_ref.3, f32[10,8,8,128]{3,2,1,0:T(8,128)} %u_ref.1, s32[8,8,128]{2,1,0:T(8,128)} %broadcast_in_dim.2.cnt_ref), custom_call_target="tpu_custom_call" | custom-call | tf_op jit(solution)/shard_map/pallas_call | solution.py:176
  40.1 0.0 collective-permute-done.3
  40.1 0.1 collective-permute-done.2
  40.2 0.1 broadcast_select_fusion.1
  40.3 0.1 slice.86
  40.4 0.1 slice.87
  40.5 0.0 copy-start.1
  40.5 1.1 %pad_maximum_fusion.1.src_ref = f32[10,10,10,128]{3,2,1,0:T(8,128)} fusion(f32[10,10,1,128]{3,2,1,0:T(1,128)S(1)} %slice.87, f32[10,1,8,128]{3,2,1,0:T(8,128)S(1)} %get-tuple-element.20, f32[10,8,8,128]{3,2,1,0:T(8,128)S(1)} %copy-done.2, f32[10,1,8,128]{3,2,1,0:T(8,128)S(1)} %get-tuple-element.16, f32[10,10,1,128]{3,2,1,0:T(1,128)S(1)} %slice.86), kind=kLoop, calls=%fused_computation.13 | loop fusion | flops 512000 | bytes 1024000 | tf_op jit(solution)/shard_map/concatenate | solution.py:229
  41.7 0.0 copy-done.1
  41.7 1.1 %fusion.3.ext_ref = f32[10,12,12,128]{3,2,1,0:T(8,128)} fusion(f32[10,2,8,128]{3,2,1,0:T(8,128)S(1)} %slice.80, f32[10,8,8,128]{3,2,1,0:T(8,128)S(1)} %copy-done.1, f32[10,2,8,128]{3,2,1,0:T(8,128)S(1)} %slice.79, f32[10,1,2,128]{3,2,1,0:T(2,128)S(1)} %broadcast.6, f32[10,1,8,128]{3,2,1,0:T(8,128)S(1)} %get-tuple-element.19, ...), kind=kLoop, calls=%fused_computation.8 | loop fusion | flops 3870720 | bytes 1525760 | tf_op jit(solution)/shard_map/concatenate | solution.py:221
  42.8 5.4 %shard_map.87 = (f32[10,8,8,128]{3,2,1,0:T(8,128)}, f32[10,8,8,128]{3,2,1,0:T(8,128)}) custom-call(f32[10]{0:T(128)} %diff_ref.1, f32[21]{0:T(128)} %rate_ref.3, f32[21]{0:T(128)} %act_ref.3, f32[21]{0:T(128)} %heat_ref.3, f32[10,12,12,128]{3,2,1,0:T(8,128)} %fusion.3.ext_ref, f32[10,10,10,128]{3,2,1,0:T(8,128)} %pad_maximum_fusion.1.src_ref, ...), custom_call_target="tpu_custom_call" | custom-call | tf_op jit(solution)/shard_map/pallas_call | solution.py:164
  (8 shorter events, 0.1 us)
Async XLA Ops:
  2.4 20.7 %collective-permute-start = (f32[10,3,8,128]{3,2,1,0:T(8,128)S(1)}, f32[10,3,8,128]{3,2,1,0:T(8,128)S(1)}, u32[]{:S(2)}, u32[]{:S(2)}) collective-permute-start(f32[10,3,8,128]{3,2,1,0:T(8,128)S(1)} %get-tuple-element.13), channel_id=1, source_target_pairs={{0,736},{32,64},{64,32},{96,128},{128,96},{160,192},{192,160},{224... | collective-permute-start | bytes 368648 | tf_op jit(solution)/shard_map/ppermute | solution.py:197
  16.7 6.4 %collective-permute-start.1 = (f32[10,3,8,128]{3,2,1,0:T(8,128)S(1)}, f32[10,3,8,128]{3,2,1,0:T(8,128)S(1)}, u32[]{:S(2)}, u32[]{:S(2)}) collective-permute-start(f32[10,3,8,128]{3,2,1,0:T(8,128)S(1)} %get-tuple-element.14), channel_id=1, source_target_pairs={{0,32},{32,0},{64,96},{96,64},{128,160},{160,128},{192,224},{224,1... | collective-permute-start | bytes 368648 | tf_op jit(solution)/shard_map/ppermute | solution.py:196
  23.1 1.0 %copy-start = (f32[10,8,8,128]{3,2,1,0:T(8,128)S(1)}, f32[10,8,8,128]{3,2,1,0:T(8,128)}, u32[]{:S(2)}) copy-start(f32[10,8,8,128]{3,2,1,0:T(8,128)} %u_ref.1) | copy-start | bytes 983044
  23.1 1.1 %copy-start.2 = (f32[10,8,8,128]{3,2,1,0:T(8,128)S(1)}, f32[10,8,8,128]{3,2,1,0:T(8,128)}, u32[]{:S(2)}) copy-start(f32[10,8,8,128]{3,2,1,0:T(8,128)} %param.8) | copy-start | bytes 983044
  24.4 11.5 %copy-start.3 = (s32[8,8]{1,0:T(8,128)S(1)}, s32[8,8]{1,0:T(8,128)}, u32[]{:S(2)}) copy-start(s32[8,8]{1,0:T(8,128)} %param.9) | copy-start | bytes 772
  24.4 15.6 %collective-permute-start.3 = (f32[10,10,3,128]{3,2,1,0:T(4,128)S(1)}, f32[10,10,3,128]{3,2,1,0:T(4,128)S(1)}, u32[]{:S(2)}, u32[]{:S(2)}) collective-permute-start(f32[10,10,3,128]{3,2,1,0:T(4,128)S(1)} %broadcast_select_fusion.2), channel_id=1, source_target_pairs={{0,1},{1,0},{2,3},{3,2},{4,5},{5,4},{6,7},{7,6},{8,9},{9,8},{10,11... | collective-permute-start | bytes 460808 | tf_op jit(solution)/shard_map/ppermute | solution.py:196
  27.9 12.3 %collective-permute-start.2 = (f32[10,10,3,128]{3,2,1,0:T(4,128)S(1)}, f32[10,10,3,128]{3,2,1,0:T(4,128)S(1)}, u32[]{:S(2)}, u32[]{:S(2)}) collective-permute-start(f32[10,10,3,128]{3,2,1,0:T(4,128)S(1)} %get-tuple-element.2), channel_id=1, source_target_pairs={{0,31},{1,2},{2,1},{3,4},{4,3},{5,6},{6,5},{7,8},{8,7},{9,10},{10,... | collective-permute-start | bytes 460808 | tf_op jit(solution)/shard_map/ppermute | solution.py:197
  40.5 1.1 %copy-start.1 = (f32[10,8,8,128]{3,2,1,0:T(8,128)S(1)}, f32[10,8,8,128]{3,2,1,0:T(8,128)}, u32[]{:S(2)}) copy-start(f32[10,8,8,128]{3,2,1,0:T(8,128)} %u_ref.1) | copy-start | bytes 983044

commit v14 on v5

--- a/solution.py
+++ b/solution.py
@@ -113,10 +113,10 @@
         beside = beside + pltpu.roll(centre, 1, 1) + pltpu.roll(centre, lanes - 1, 1)
         return beside - 6.0 * centre
 
-    def first_row(i, carry):
+    def first_row(i, carry, windows=(0, 2)):
         e = i + 1
         for r in range(rows):
-            for lo in (0, 2):
+            for lo in windows:
                 centre = ext_ref[r, e, pl.ds(lo + 1, cy)]
                 lap = laplace(
                     centre,
@@ -130,7 +130,9 @@
                 )
         return carry
 
-    lax.fori_loop(0, cx + 2, first_row, 0)
+    first_row(0, 0, (1,))
+    first_row(cx + 1, 0, (1,))
+    lax.fori_loop(1, cx + 1, first_row, 0)
 
     def box_row(x, carry):
         start = []

time: 48.8 us -> 48.6 us (level)
  no operation moved by 1% of the time
where the time goes in v14:
time: 48.6 us; the launch traced here: 48.2 us
  starting transfers between devices  27.6 us (57%)
  Pallas kernels  9.08 us (19%)
  waiting for transfers between devices  4.47 us (9%)
  local copies, waits for them, and re-layouts  3.67 us (8%)
  other arithmetic  2.59 us (5%)
  between operations  0.83 us (2%)
    ppermute x2, starting transfers between devices, exchange(): second = lax.ppermute(jnp.where(even, to_lo, to_hi), axis, outer)  22.2 us
    pallas_call x1, Pallas kernels, finish(): pl.pallas_call(finish_kernel, out_shape=(box, box), in_specs=[smem, smem,...  5.44 us
    ppermute x2, starting transfers between devices, exchange(): first = lax.ppermute(jnp.where(even, to_hi, to_lo), axis, inner)  5.41 us
    ppermute x2, waiting for transfers between devices, exchange(): second = lax.ppermute(jnp.where(even, to_lo, to_hi), axis, outer)  4.47 us
    pallas_call x1, Pallas kernels, chemistry(): pl.pallas_call(chem_kernel, out_shape=jax.ShapeDtypeStruct(fields.shape,...  3.65 us
    slice x2, local copies, waits for them, and re-layouts, local(): to_xm = jnp.concatenate([state[:, :2], source_in[:, :1]], 1)  1.75 us
    concatenate x1, other arithmetic, local(): jnp.concatenate([jnp.concatenate([zeros(1, 2), wide[:, :1], zeros(1, 2)],...  1.14 us
    concatenate x1, other arithmetic, local(): src = jnp.concatenate([from_ym[:, :, 2:], wide_src, from_yp[:, :, 2:]], 2)  1.11 us
  transfers between devices with their start and end apart: 4, of which 1 were waited for; matrix products, arithmetic and copies ran while one was open for 1% of the time, Pallas kernels for 8%

profile of v14, /device:TPU:6, one launch (start us, length us, event | category | flops | bytes accessed | tf_op | source)
XLA Modules:
  0.0 48.2 jit_solution(6660046677562297073)
XLA Ops:
  0.6 0.8 %fusion.14 = (f32[10,1,8,128]{3,2,1,0:T(8,128)S(1)}, f32[10,1,8,128]{3,2,1,0:T(8,128)S(1)}) fusion(f32[10,8,8,128]{3,2,1,0:T(8,128)} %param.8), kind=kLoop, calls=%fused_computation.37 | loop fusion | bytes 163840 | tf_op jit(solution)/shard_map/slice | solution.py:209
  1.5 0.9 %fusion.13 = (f32[10,2,8,128]{3,2,1,0:T(8,128)S(1)}, f32[10,2,8,128]{3,2,1,0:T(8,128)S(1)}) fusion(f32[10,8,8,128]{3,2,1,0:T(8,128)} %u_ref.1), kind=kLoop, calls=%fused_computation.36 | loop fusion | bytes 327680 | tf_op jit(solution)/shard_map/slice | solution.py:209
  2.4 14.3 %collective-permute-start = (f32[10,3,8,128]{3,2,1,0:T(8,128)S(1)}, f32[10,3,8,128]{3,2,1,0:T(8,128)S(1)}, u32[]{:S(2)}, u32[]{:S(2)}) collective-permute-start(f32[10,3,8,128]{3,2,1,0:T(8,128)S(1)} %get-tuple-element.13), channel_id=1, source_target_pairs={{0,736},{32,64},{64,32},{96,128},{128,96},{160,192},{192,160},{224... | collective-permute-start | bytes 368648 | tf_op jit(solution)/shard_map/ppermute | solution.py:199
  16.7 1.9 %collective-permute-start.1 = (f32[10,3,8,128]{3,2,1,0:T(8,128)S(1)}, f32[10,3,8,128]{3,2,1,0:T(8,128)S(1)}, u32[]{:S(2)}, u32[]{:S(2)}) collective-permute-start(f32[10,3,8,128]{3,2,1,0:T(8,128)S(1)} %get-tuple-element.14), channel_id=1, source_target_pairs={{0,32},{32,0},{64,96},{96,64},{128,160},{160,128},{192,224},{224,1... | collective-permute-start | bytes 368648 | tf_op jit(solution)/shard_map/ppermute | solution.py:198
  18.6 4.5 %collective-permute-done = f32[10,3,8,128]{3,2,1,0:T(8,128)S(1)} collective-permute-done((f32[10,3,8,128]{3,2,1,0:T(8,128)S(1)}, f32[10,3,8,128]{3,2,1,0:T(8,128)S(1)}, u32[]{:S(2)}, u32[]{:S(2)}) %collective-permute-start) | collective-permute-done | bytes 122912 | tf_op jit(solution)/shard_map/ppermute | solution.py:199
  23.1 0.0 collective-permute-done.1
  23.1 0.0 copy-start
  23.1 0.0 copy-start.2
  23.2 0.9 %copy-done = f32[10,8,8,128]{3,2,1,0:T(8,128)S(1)} copy-done((f32[10,8,8,128]{3,2,1,0:T(8,128)S(1)}, f32[10,8,8,128]{3,2,1,0:T(8,128)}, u32[]{:S(2)}) %copy-start) | copy-done | bytes 327704
  24.1 0.1 copy-done.2
  24.2 0.2 broadcast_select_fusion.3
  24.4 0.0 copy-start.3
  24.4 0.1 broadcast_select_fusion.2
  24.4 3.5 %collective-permute-start.3 = (f32[10,10,3,128]{3,2,1,0:T(4,128)S(1)}, f32[10,10,3,128]{3,2,1,0:T(4,128)S(1)}, u32[]{:S(2)}, u32[]{:S(2)}) collective-permute-start(f32[10,10,3,128]{3,2,1,0:T(4,128)S(1)} %broadcast_select_fusion.2), channel_id=1, source_target_pairs={{0,1},{1,0},{2,3},{3,2},{4,5},{5,4},{6,7},{7,6},{8,9},{9,8},{10,11... | collective-permute-start | bytes 460808 | tf_op jit(solution)/shard_map/ppermute | solution.py:198
  27.9 7.9 %collective-permute-start.2 = (f32[10,10,3,128]{3,2,1,0:T(4,128)S(1)}, f32[10,10,3,128]{3,2,1,0:T(4,128)S(1)}, u32[]{:S(2)}, u32[]{:S(2)}) collective-permute-start(f32[10,10,3,128]{3,2,1,0:T(4,128)S(1)} %get-tuple-element.2), channel_id=1, source_target_pairs={{0,31},{1,2},{2,1},{3,4},{4,3},{5,6},{6,5},{7,8},{8,7},{9,10},{10,... | collective-permute-start | bytes 460808 | tf_op jit(solution)/shard_map/ppermute | solution.py:199
  35.9 0.0 copy-done.3
  35.9 0.7 %broadcast_in_dim.2.cnt_ref = s32[8,8,128]{2,1,0:T(8,128)} broadcast(s32[8,8]{1,0:T(8,128)S(1)} %copy-done.3), dimensions={0,1} | broadcast | bytes 33024 | tf_op jit(solution)/shard_map/broadcast_in_dim | solution.py:207
  36.6 3.6 %shard_map.86.early_ref = f32[10,8,8,128]{3,2,1,0:T(8,128)} custom-call(f32[21]{0:T(128)} %rate_ref.3, f32[21]{0:T(128)} %act_ref.3, f32[21]{0:T(128)} %heat_ref.3, f32[10,8,8,128]{3,2,1,0:T(8,128)} %u_ref.1, s32[8,8,128]{2,1,0:T(8,128)} %broadcast_in_dim.2.cnt_ref), custom_call_target="tpu_custom_call" | custom-call | tf_op jit(solution)/shard_map/pallas_call | solution.py:178
  40.2 0.0 collective-permute-done.3
  40.2 0.0 collective-permute-done.2
  40.2 0.1 broadcast_select_fusion.1
  40.3 0.1 slice.86
  40.4 0.1 slice.87
  40.5 0.0 copy-start.1
  40.5 1.1 %pad_maximum_fusion.1.src_ref = f32[10,10,10,128]{3,2,1,0:T(8,128)} fusion(f32[10,10,1,128]{3,2,1,0:T(1,128)S(1)} %slice.87, f32[10,1,8,128]{3,2,1,0:T(8,128)S(1)} %get-tuple-element.20, f32[10,8,8,128]{3,2,1,0:T(8,128)S(1)} %copy-done.2, f32[10,1,8,128]{3,2,1,0:T(8,128)S(1)} %get-tuple-element.16, f32[10,10,1,128]{3,2,1,0:T(1,128)S(1)} %slice.86), kind=kLoop, calls=%fused_computation.13 | loop fusion | flops 512000 | bytes 1024000 | tf_op jit(solution)/shard_map/concatenate | solution.py:231
  41.7 0.0 copy-done.1
  41.7 1.1 %fusion.3.ext_ref = f32[10,12,12,128]{3,2,1,0:T(8,128)} fusion(f32[10,2,8,128]{3,2,1,0:T(8,128)S(1)} %slice.80, f32[10,8,8,128]{3,2,1,0:T(8,128)S(1)} %copy-done.1, f32[10,2,8,128]{3,2,1,0:T(8,128)S(1)} %slice.79, f32[10,1,2,128]{3,2,1,0:T(2,128)S(1)} %broadcast.6, f32[10,1,8,128]{3,2,1,0:T(8,128)S(1)} %get-tuple-element.19, ...), kind=kLoop, calls=%fused_computation.8 | loop fusion | flops 3870720 | bytes 1525760 | tf_op jit(solution)/shard_map/concatenate | solution.py:223
  42.8 5.4 %shard_map.87 = (f32[10,8,8,128]{3,2,1,0:T(8,128)}, f32[10,8,8,128]{3,2,1,0:T(8,128)}) custom-call(f32[10]{0:T(128)} %diff_ref.1, f32[21]{0:T(128)} %rate_ref.3, f32[21]{0:T(128)} %act_ref.3, f32[21]{0:T(128)} %heat_ref.3, f32[10,12,12,128]{3,2,1,0:T(8,128)} %fusion.3.ext_ref, f32[10,10,10,128]{3,2,1,0:T(8,128)} %pad_maximum_fusion.1.src_ref, ...), custom_call_target="tpu_custom_call" | custom-call | tf_op jit(solution)/shard_map/pallas_call | solution.py:166
  (8 shorter events, 0.1 us)
Async XLA Ops:
  2.4 20.7 %collective-permute-start = (f32[10,3,8,128]{3,2,1,0:T(8,128)S(1)}, f32[10,3,8,128]{3,2,1,0:T(8,128)S(1)}, u32[]{:S(2)}, u32[]{:S(2)}) collective-permute-start(f32[10,3,8,128]{3,2,1,0:T(8,128)S(1)} %get-tuple-element.13), channel_id=1, source_target_pairs={{0,736},{32,64},{64,32},{96,128},{128,96},{160,192},{192,160},{224... | collective-permute-start | bytes 368648 | tf_op jit(solution)/shard_map/ppermute | solution.py:199
  16.7 6.4 %collective-permute-start.1 = (f32[10,3,8,128]{3,2,1,0:T(8,128)S(1)}, f32[10,3,8,128]{3,2,1,0:T(8,128)S(1)}, u32[]{:S(2)}, u32[]{:S(2)}) collective-permute-start(f32[10,3,8,128]{3,2,1,0:T(8,128)S(1)} %get-tuple-element.14), channel_id=1, source_target_pairs={{0,32},{32,0},{64,96},{96,64},{128,160},{160,128},{192,224},{224,1... | collective-permute-start | bytes 368648 | tf_op jit(solution)/shard_map/ppermute | solution.py:198
  23.1 1.0 %copy-start = (f32[10,8,8,128]{3,2,1,0:T(8,128)S(1)}, f32[10,8,8,128]{3,2,1,0:T(8,128)}, u32[]{:S(2)}) copy-start(f32[10,8,8,128]{3,2,1,0:T(8,128)} %u_ref.1) | copy-start | bytes 983044
  23.1 1.1 %copy-start.2 = (f32[10,8,8,128]{3,2,1,0:T(8,128)S(1)}, f32[10,8,8,128]{3,2,1,0:T(8,128)}, u32[]{:S(2)}) copy-start(f32[10,8,8,128]{3,2,1,0:T(8,128)} %param.8) | copy-start | bytes 983044
  24.4 11.5 %copy-start.3 = (s32[8,8]{1,0:T(8,128)S(1)}, s32[8,8]{1,0:T(8,128)}, u32[]{:S(2)}) copy-start(s32[8,8]{1,0:T(8,128)} %param.9) | copy-start | bytes 772
  24.4 15.8 %collective-permute-start.3 = (f32[10,10,3,128]{3,2,1,0:T(4,128)S(1)}, f32[10,10,3,128]{3,2,1,0:T(4,128)S(1)}, u32[]{:S(2)}, u32[]{:S(2)}) collective-permute-start(f32[10,10,3,128]{3,2,1,0:T(4,128)S(1)} %broadcast_select_fusion.2), channel_id=1, source_target_pairs={{0,1},{1,0},{2,3},{3,2},{4,5},{5,4},{6,7},{7,6},{8,9},{9,8},{10,11... | collective-permute-start | bytes 460808 | tf_op jit(solution)/shard_map/ppermute | solution.py:198
  27.9 12.3 %collective-permute-start.2 = (f32[10,10,3,128]{3,2,1,0:T(4,128)S(1)}, f32[10,10,3,128]{3,2,1,0:T(4,128)S(1)}, u32[]{:S(2)}, u32[]{:S(2)}) collective-permute-start(f32[10,10,3,128]{3,2,1,0:T(4,128)S(1)} %get-tuple-element.2), channel_id=1, source_target_pairs={{0,31},{1,2},{2,1},{3,4},{4,3},{5,6},{6,5},{7,8},{8,7},{9,10},{10,... | collective-permute-start | bytes 460808 | tf_op jit(solution)/shard_map/ppermute | solution.py:199
  40.5 1.1 %copy-start.1 = (f32[10,8,8,128]{3,2,1,0:T(8,128)S(1)}, f32[10,8,8,128]{3,2,1,0:T(8,128)}, u32[]{:S(2)}) copy-start(f32[10,8,8,128]{3,2,1,0:T(8,128)} %u_ref.1) | copy-start | bytes 983044

commit v15 on v14

--- a/solution.py
+++ b/solution.py
@@ -54,7 +54,7 @@
     stride = time_step / cnt.astype(jnp.float32)
     cur = list(start)
     for turn in range(CMAX):
-        active = turn < cnt
+        step = jnp.where(turn < cnt, stride, 0.0)
         rates = []
         for r, entry in enumerate(reaction_table):
             term = coeffs[r] * cur[entry[0]]
@@ -78,11 +78,11 @@
             if total is None:
                 new.append(cur[s])
             else:
-                new.append(jnp.where(active, cur[s] + stride * total, cur[s]))
+                new.append(cur[s] + step * total)
         heat_total = heat[0] * rates[0]
         for r in range(1, reactions):
             heat_total = heat_total + heat[r] * rates[r]
-        new.append(jnp.where(active, cur[SPECIES] + stride * heat_total, cur[SPECIES]))
+        new.append(cur[SPECIES] + step * heat_total)
         cur = new
     return [(cur[s] - start[s]) / time_step for s in range(len(start))]
 

time: 48.6 us -> 48.5 us (level)
  transfers between devices with their start and end apart: 4 -> 4, of which waited for: 1 -> 2; matrix products, arithmetic and copies ran while one was open for 1% -> 1% of each run, Pallas kernels for 8% -> 7%
where the time goes in v15:
time: 48.5 us; the launch traced here: 48.1 us
  starting transfers between devices  27.6 us (57%)
  Pallas kernels  8.82 us (18%)
  waiting for transfers between devices  4.61 us (10%)
  local copies, waits for them, and re-layouts  3.67 us (8%)
  other arithmetic  2.58 us (5%)
  between operations  0.82 us (2%)
    ppermute x2, starting transfers between devices, exchange(): second = lax.ppermute(jnp.where(even, to_lo, to_hi), axis, outer)  22.2 us
    ppermute x2, starting transfers between devices, exchange(): first = lax.ppermute(jnp.where(even, to_hi, to_lo), axis, inner)  5.41 us
    pallas_call x1, Pallas kernels, finish(): pl.pallas_call(finish_kernel, out_shape=(box, box), in_specs=[smem, smem,...  5.31 us
    ppermute x2, waiting for transfers between devices, exchange(): second = lax.ppermute(jnp.where(even, to_lo, to_hi), axis, outer)  4.6 us
    pallas_call x1, Pallas kernels, chemistry(): pl.pallas_call(chem_kernel, out_shape=jax.ShapeDtypeStruct(fields.shape,...  3.51 us
    slice x2, local copies, waits for them, and re-layouts, local(): to_xm = jnp.concatenate([state[:, :2], source_in[:, :1]], 1)  1.75 us
    concatenate x1, other arithmetic, local(): jnp.concatenate([jnp.concatenate([zeros(1, 2), wide[:, :1], zeros(1, 2)],...  1.14 us
    concatenate x1, other arithmetic, local(): src = jnp.concatenate([from_ym[:, :, 2:], wide_src, from_yp[:, :, 2:]], 2)  1.11 us
  transfers between devices with their start and end apart: 4, of which 2 were waited for; matrix products, arithmetic and copies ran while one was open for 1% of the time, Pallas kernels for 7%

profile of v15, /device:TPU:6, one launch (start us, length us, event | category | flops | bytes accessed | tf_op | source)
XLA Modules:
  0.0 48.1 jit_solution(8442671370770570036)
XLA Ops:
  0.6 0.8 %fusion.14 = (f32[10,1,8,128]{3,2,1,0:T(8,128)S(1)}, f32[10,1,8,128]{3,2,1,0:T(8,128)S(1)}) fusion(f32[10,8,8,128]{3,2,1,0:T(8,128)} %param.8), kind=kLoop, calls=%fused_computation.37 | loop fusion | bytes 163840 | tf_op jit(solution)/shard_map/slice | solution.py:209
  1.5 0.9 %fusion.13 = (f32[10,2,8,128]{3,2,1,0:T(8,128)S(1)}, f32[10,2,8,128]{3,2,1,0:T(8,128)S(1)}) fusion(f32[10,8,8,128]{3,2,1,0:T(8,128)} %u_ref.1), kind=kLoop, calls=%fused_computation.36 | loop fusion | bytes 327680 | tf_op jit(solution)/shard_map/slice | solution.py:209
  2.4 14.3 %collective-permute-start = (f32[10,3,8,128]{3,2,1,0:T(8,128)S(1)}, f32[10,3,8,128]{3,2,1,0:T(8,128)S(1)}, u32[]{:S(2)}, u32[]{:S(2)}) collective-permute-start(f32[10,3,8,128]{3,2,1,0:T(8,128)S(1)} %get-tuple-element.13), channel_id=1, source_target_pairs={{0,736},{32,64},{64,32},{96,128},{128,96},{160,192},{192,160},{224... | collective-permute-start | bytes 368648 | tf_op jit(solution)/shard_map/ppermute | solution.py:199
  16.7 1.9 %collective-permute-start.1 = (f32[10,3,8,128]{3,2,1,0:T(8,128)S(1)}, f32[10,3,8,128]{3,2,1,0:T(8,128)S(1)}, u32[]{:S(2)}, u32[]{:S(2)}) collective-permute-start(f32[10,3,8,128]{3,2,1,0:T(8,128)S(1)} %get-tuple-element.14), channel_id=1, source_target_pairs={{0,32},{32,0},{64,96},{96,64},{128,160},{160,128},{192,224},{224,1... | collective-permute-start | bytes 368648 | tf_op jit(solution)/shard_map/ppermute | solution.py:198
  18.6 4.5 %collective-permute-done = f32[10,3,8,128]{3,2,1,0:T(8,128)S(1)} collective-permute-done((f32[10,3,8,128]{3,2,1,0:T(8,128)S(1)}, f32[10,3,8,128]{3,2,1,0:T(8,128)S(1)}, u32[]{:S(2)}, u32[]{:S(2)}) %collective-permute-start) | collective-permute-done | bytes 122912 | tf_op jit(solution)/shard_map/ppermute | solution.py:199
  23.1 0.0 collective-permute-done.1
  23.1 0.0 copy-start
  23.1 0.0 copy-start.2
  23.2 0.9 %copy-done = f32[10,8,8,128]{3,2,1,0:T(8,128)S(1)} copy-done((f32[10,8,8,128]{3,2,1,0:T(8,128)S(1)}, f32[10,8,8,128]{3,2,1,0:T(8,128)}, u32[]{:S(2)}) %copy-start) | copy-done | bytes 327704
  24.1 0.1 copy-done.2
  24.2 0.2 broadcast_select_fusion.3
  24.4 0.0 copy-start.3
  24.4 0.1 broadcast_select_fusion.2
  24.4 3.5 %collective-permute-start.3 = (f32[10,10,3,128]{3,2,1,0:T(4,128)S(1)}, f32[10,10,3,128]{3,2,1,0:T(4,128)S(1)}, u32[]{:S(2)}, u32[]{:S(2)}) collective-permute-start(f32[10,10,3,128]{3,2,1,0:T(4,128)S(1)} %broadcast_select_fusion.2), channel_id=1, source_target_pairs={{0,1},{1,0},{2,3},{3,2},{4,5},{5,4},{6,7},{7,6},{8,9},{9,8},{10,11... | collective-permute-start | bytes 460808 | tf_op jit(solution)/shard_map/ppermute | solution.py:198
  27.9 7.9 %collective-permute-start.2 = (f32[10,10,3,128]{3,2,1,0:T(4,128)S(1)}, f32[10,10,3,128]{3,2,1,0:T(4,128)S(1)}, u32[]{:S(2)}, u32[]{:S(2)}) collective-permute-start(f32[10,10,3,128]{3,2,1,0:T(4,128)S(1)} %get-tuple-element.2), channel_id=1, source_target_pairs={{0,31},{1,2},{2,1},{3,4},{4,3},{5,6},{6,5},{7,8},{8,7},{9,10},{10,... | collective-permute-start | bytes 460808 | tf_op jit(solution)/shard_map/ppermute | solution.py:199
  35.9 0.0 copy-done.3
  35.9 0.7 %broadcast_in_dim.2.cnt_ref = s32[8,8,128]{2,1,0:T(8,128)} broadcast(s32[8,8]{1,0:T(8,128)S(1)} %copy-done.3), dimensions={0,1} | broadcast | bytes 33024 | tf_op jit(solution)/shard_map/broadcast_in_dim | solution.py:207
  36.6 3.5 %shard_map.86.early_ref = f32[10,8,8,128]{3,2,1,0:T(8,128)} custom-call(f32[21]{0:T(128)} %rate_ref.3, f32[21]{0:T(128)} %act_ref.3, f32[21]{0:T(128)} %heat_ref.3, f32[10,8,8,128]{3,2,1,0:T(8,128)} %u_ref.1, s32[8,8,128]{2,1,0:T(8,128)} %broadcast_in_dim.2.cnt_ref), custom_call_target="tpu_custom_call" | custom-call | tf_op jit(solution)/shard_map/pallas_call | solution.py:178
  40.1 0.0 collective-permute-done.3
  40.1 0.1 collective-permute-done.2
  40.2 0.1 broadcast_select_fusion.1
  40.3 0.1 slice.86
  40.4 0.1 slice.87
  40.5 0.0 copy-start.1
  40.5 1.1 %pad_maximum_fusion.1.src_ref = f32[10,10,10,128]{3,2,1,0:T(8,128)} fusion(f32[10,10,1,128]{3,2,1,0:T(1,128)S(1)} %slice.87, f32[10,1,8,128]{3,2,1,0:T(8,128)S(1)} %get-tuple-element.20, f32[10,8,8,128]{3,2,1,0:T(8,128)S(1)} %copy-done.2, f32[10,1,8,128]{3,2,1,0:T(8,128)S(1)} %get-tuple-element.16, f32[10,10,1,128]{3,2,1,0:T(1,128)S(1)} %slice.86), kind=kLoop, calls=%fused_computation.13 | loop fusion | flops 512000 | bytes 1024000 | tf_op jit(solution)/shard_map/concatenate | solution.py:231
  41.7 0.0 copy-done.1
  41.7 1.1 %fusion.3.ext_ref = f32[10,12,12,128]{3,2,1,0:T(8,128)} fusion(f32[10,2,8,128]{3,2,1,0:T(8,128)S(1)} %slice.80, f32[10,8,8,128]{3,2,1,0:T(8,128)S(1)} %copy-done.1, f32[10,2,8,128]{3,2,1,0:T(8,128)S(1)} %slice.79, f32[10,1,2,128]{3,2,1,0:T(2,128)S(1)} %broadcast.6, f32[10,1,8,128]{3,2,1,0:T(8,128)S(1)} %get-tuple-element.19, ...), kind=kLoop, calls=%fused_computation.8 | loop fusion | flops 3870720 | bytes 1525760 | tf_op jit(solution)/shard_map/concatenate | solution.py:223
  42.8 5.3 %shard_map.87 = (f32[10,8,8,128]{3,2,1,0:T(8,128)}, f32[10,8,8,128]{3,2,1,0:T(8,128)}) custom-call(f32[10]{0:T(128)} %diff_ref.1, f32[21]{0:T(128)} %rate_ref.3, f32[21]{0:T(128)} %act_ref.3, f32[21]{0:T(128)} %heat_ref.3, f32[10,12,12,128]{3,2,1,0:T(8,128)} %fusion.3.ext_ref, f32[10,10,10,128]{3,2,1,0:T(8,128)} %pad_maximum_fusion.1.src_ref, ...), custom_call_target="tpu_custom_call" | custom-call | tf_op jit(solution)/shard_map/pallas_call | solution.py:166
  (8 shorter events, 0.1 us)
Async XLA Ops:
  2.4 20.7 %collective-permute-start = (f32[10,3,8,128]{3,2,1,0:T(8,128)S(1)}, f32[10,3,8,128]{3,2,1,0:T(8,128)S(1)}, u32[]{:S(2)}, u32[]{:S(2)}) collective-permute-start(f32[10,3,8,128]{3,2,1,0:T(8,128)S(1)} %get-tuple-element.13), channel_id=1, source_target_pairs={{0,736},{32,64},{64,32},{96,128},{128,96},{160,192},{192,160},{224... | collective-permute-start | bytes 368648 | tf_op jit(solution)/shard_map/ppermute | solution.py:199
  16.7 6.4 %collective-permute-start.1 = (f32[10,3,8,128]{3,2,1,0:T(8,128)S(1)}, f32[10,3,8,128]{3,2,1,0:T(8,128)S(1)}, u32[]{:S(2)}, u32[]{:S(2)}) collective-permute-start(f32[10,3,8,128]{3,2,1,0:T(8,128)S(1)} %get-tuple-element.14), channel_id=1, source_target_pairs={{0,32},{32,0},{64,96},{96,64},{128,160},{160,128},{192,224},{224,1... | collective-permute-start | bytes 368648 | tf_op jit(solution)/shard_map/ppermute | solution.py:198
  23.1 1.0 %copy-start = (f32[10,8,8,128]{3,2,1,0:T(8,128)S(1)}, f32[10,8,8,128]{3,2,1,0:T(8,128)}, u32[]{:S(2)}) copy-start(f32[10,8,8,128]{3,2,1,0:T(8,128)} %u_ref.1) | copy-start | bytes 983044
  23.1 1.1 %copy-start.2 = (f32[10,8,8,128]{3,2,1,0:T(8,128)S(1)}, f32[10,8,8,128]{3,2,1,0:T(8,128)}, u32[]{:S(2)}) copy-start(f32[10,8,8,128]{3,2,1,0:T(8,128)} %param.8) | copy-start | bytes 983044
  24.4 11.5 %copy-start.3 = (s32[8,8]{1,0:T(8,128)S(1)}, s32[8,8]{1,0:T(8,128)}, u32[]{:S(2)}) copy-start(s32[8,8]{1,0:T(8,128)} %param.9) | copy-start | bytes 772
  24.4 15.6 %collective-permute-start.3 = (f32[10,10,3,128]{3,2,1,0:T(4,128)S(1)}, f32[10,10,3,128]{3,2,1,0:T(4,128)S(1)}, u32[]{:S(2)}, u32[]{:S(2)}) collective-permute-start(f32[10,10,3,128]{3,2,1,0:T(4,128)S(1)} %broadcast_select_fusion.2), channel_id=1, source_target_pairs={{0,1},{1,0},{2,3},{3,2},{4,5},{5,4},{6,7},{7,6},{8,9},{9,8},{10,11... | collective-permute-start | bytes 460808 | tf_op jit(solution)/shard_map/ppermute | solution.py:198
  27.9 12.3 %collective-permute-start.2 = (f32[10,10,3,128]{3,2,1,0:T(4,128)S(1)}, f32[10,10,3,128]{3,2,1,0:T(4,128)S(1)}, u32[]{:S(2)}, u32[]{:S(2)}) collective-permute-start(f32[10,10,3,128]{3,2,1,0:T(4,128)S(1)} %get-tuple-element.2), channel_id=1, source_target_pairs={{0,31},{1,2},{2,1},{3,4},{4,3},{5,6},{6,5},{7,8},{8,7},{9,10},{10,... | collective-permute-start | bytes 460808 | tf_op jit(solution)/shard_map/ppermute | solution.py:199
  40.5 1.1 %copy-start.1 = (f32[10,8,8,128]{3,2,1,0:T(8,128)S(1)}, f32[10,8,8,128]{3,2,1,0:T(8,128)}, u32[]{:S(2)}) copy-start(f32[10,8,8,128]{3,2,1,0:T(8,128)} %u_ref.1) | copy-start | bytes 983044
